TPU v7x, 768 devices: a whole 4x8x12 slice. The times are simulated.
768 devices in a mesh: occ: 16 (over y, core), virt: 12 (over z), rep: 4 (over x).
Axes of the slice: x: 4, y: 8, z: 12, core: 2. Of those that a mesh axis runs over, the one named last changes fastest.
Arguments:
- amplitudes: bfloat16 [4096, 15360], P(('occ', 'rep'), 'virt'), may hold values from -6 to 6
- integrals: bfloat16 [15360, 3072], P(('occ', 'rep'), 'virt'), may hold values from -0.125 to 0.125
- cd_irrep: int32 [15360], P(('occ', 'rep')), may hold values from 0 to 7
- ab_irrep: int32 [3072], P('virt'), may hold values from 0 to 7
Outputs:
- residual: float32 [4096, 3072], P(('occ', 'rep'), 'virt')
Inputs may be any that keep to these rules, and one draw needn't show every extreme that they name: `cd_irrep`: irreps of the eight D2h irreducible representations. `ab_irrep`: irreps of the eight D2h irreducible representations.
All inputs are finite; a program needn't handle non-finite values.
Results may differ from a plain program's by a relative error of at most 0.0003.
Values may be sent and summed in bfloat16 or wider, within the bound.
No kernel may reach another device: no remote copies, remote signals or barrier semaphores. Data moves between devices by JAX's collectives and lax.ppermute only.
A program may use at most 32 MiB of HBM per device.

v0:
```python
import jax
import jax.numpy as jnp
from jax import lax
from jax.sharding import PartitionSpec as P


def local(amplitudes, integrals, cd_irrep, ab_irrep):
    allowed = cd_irrep[:, None] == ab_irrep[None, :]
    masked = jnp.where(allowed, integrals, jnp.zeros_like(integrals))
    columns = lax.all_gather(amplitudes, "virt", axis=1, tiled=True)
    regrouped = lax.all_to_all(columns, ("occ", "rep"), split_axis=1, concat_axis=0, tiled=True)
    partial_sum = jnp.dot(regrouped, masked, preferred_element_type=jnp.float32)
    return lax.psum_scatter(partial_sum, ("occ", "rep"), scatter_dimension=0, tiled=True)


def solution(mesh):
    in_specs = (P(("occ", "rep"), "virt"), P(("occ", "rep"), "virt"), P(("occ", "rep")), P("virt"))
    out_specs = P(("occ", "rep"), "virt")
    return jax.shard_map(local, mesh=mesh, in_specs=in_specs, out_specs=out_specs, check_vma=False)
```

profile of v0, /device:TPU:6, one launch (start us, length us, event | category | flops | bytes accessed | tf_op | source)
XLA Modules:
  0.0 313.5 jit_solution(14854267666763822234)
XLA Ops:
  6.5 0.0 all-gather.2.cloned.1.call-start
  6.5 0.7 all-gather.2.cloned.1.call-update
  7.3 0.0 reduce-scatter.4.cloned.1.call-start
  7.3 70.1 %all-gather.2.cloned.1.call-done = bf16[64,15360]{1,0:T(8,128)(2,1)} async-done(((bf16[64,1280]{1,0:T(8,128)(2,1)}), bf16[64,15360]{1,0:T(8,128)(2,1)}) %all-gather.2.cloned.1.call-update) | async-done | bytes 1966096 | tf_op jit(solution)/shard_map/all_gather | solution.py:10
  77.5 6.1 %all_to_all.14 = bf16[64,64,240]{2,1,0:T(8,128)(2,1)S(1)} reshape(bf16[64,15360]{1,0:T(8,128)(2,1)} %all-gather.2.cloned.1.call-done) | data formatting | bytes 3932160 | tf_op jit(solution)/shard_map/all_to_all | solution.py:11
  83.5 1.2 copy.8
  84.7 0.0 copy-start
  84.7 0.0 copy-start.1
  84.7 0.0 copy-start.2
  84.7 61.5 %all_to_all.19 = bf16[64,64,240]{2,0,1:T(8,128)(2,1)S(1)} all-to-all(bf16[64,64,240]{2,0,1:T(8,128)(2,1)S(1)} %copy.8), channel_id=1, replica_groups=mesh['occ'=16,'virt'=12,'rep'=4] {'occ','rep'}, dimensions={1} | all-to-all | bytes 3932160 | tf_op jit(solution)/shard_map/all_to_all | solution.py:11
  146.2 0.0 copy-done
  146.2 0.0 copy-done.1
  146.2 0.0 copy-done.2
  146.2 2.8 convolution_bitcast_fusion
  149.0 5.6 %copy.10 = f32[4096,256]{1,0:T(8,128)} copy(f32[4096,256]{0,1:T(8,128)} %convolution_bitcast_fusion) | data formatting | bytes 8388608
  154.7 0.0 reduce-scatter.4.cloned.1.call-update
  154.7 152.0 %reduce-scatter.4.cloned.1.call-done = f32[64,256]{1,0:T(8,128)} async-done(((f32[4096,256]{1,0:T(8,128)}), f32[64,256]{1,0:T(8,128)}) %reduce-scatter.4.cloned.1.call-update) | async-done | bytes 65552 | tf_op jit(solution)/shard_map/reduce_scatter | solution.py:13
Async XLA Ops:
  6.5 70.9 %all-gather.2.cloned.1.call-start = ((), (), s32[]{:S(2)}) async-start(), calls=%async_computation.2 | async-start | bytes 2129920 | tf_op jit(solution)/shard_map/all_gather | solution.py:10
  7.3 299.5 %reduce-scatter.4.cloned.1.call-start = ((), (), s32[]{:S(2)}) async-start(), calls=%async_computation.3 | async-start | bytes 4259840 | tf_op jit(solution)/shard_map/reduce_scatter | solution.py:13
  84.7 61.5 %copy-start = (bf16[240,256]{1,0:T(8,128)(2,1)S(1)}, bf16[240,256]{1,0:T(8,128)(2,1)}, u32[]{:S(2)}) copy-start(bf16[240,256]{1,0:T(8,128)(2,1)} %param.5) | copy-start | bytes 368644
  84.7 61.5 %copy-start.1 = (s32[256]{0:T(256)S(1)}, s32[256]{0:T(256)}, u32[]{:S(2)}) copy-start(s32[256]{0:T(256)} %param.7) | copy-start | bytes 3076
  84.7 61.5 %copy-start.2 = (s32[240]{0:T(256)S(1)}, s32[240]{0:T(256)}, u32[]{:S(2)}) copy-start(s32[240]{0:T(256)} %param.6) | copy-start | bytes 2884
Sparse Core Ops, SparseCore 0:
  9.7 67.6 all-gather.1
  154.8 151.8 reduce-scatter.3
where the time goes:
time: 315 us; the launch traced here: 314 us
  waiting for transfers between devices  223 us (71%)
  blocking collectives  61.5 us (20%)
  between operations  13.4 us (4%)
  local copies, waits for them, and re-layouts  12.9 us (4%)
    reduce_scatter x1, waiting for transfers between devices, local(): lax.psum_scatter(partial_sum, ('occ', 'rep'), scatter_dimension=0, tiled=...  152 us
    all_gather x1, waiting for transfers between devices, local(): columns = lax.all_gather(amplitudes, 'virt', axis=1, tiled=True)  70.1 us
    all_to_all x1, blocking collectives, local(): lax.all_to_all(columns, ('occ', 'rep'), split_axis=1, concat_axis=0, tile...  61.5 us
    all_to_all x2, local copies, waits for them, and re-layouts, local(): lax.all_to_all(columns, ('occ', 'rep'), split_axis=1, concat_axis=0, tile...  7.25 us
  transfers between devices with their start and end apart: 2, of which 2 were waited for; matrix products, arithmetic and copies ran while one was open for 0% of the time, Pallas kernels for 0%

commit v1 on v0

v1 whole, which is shorter than its diff:
```python
import math

import jax
import jax.numpy as jnp
from jax import lax
from jax.sharding import PartitionSpec as P


def local(amplitudes, integrals, cd_irrep, ab_irrep, n_rep):
    rows, cols = amplitudes.shape
    kb, nb = integrals.shape
    atom = math.gcd(cols, kb)
    per_v = cols // atom
    per_k = kb // atom
    assert per_v % n_rep == 0 and per_k <= n_rep
    r = lax.axis_index("rep")

    masked = jnp.where(cd_irrep[:, None] == ab_irrep[None, :], integrals, jnp.zeros_like(integrals))

    a = amplitudes.reshape(rows, per_v // n_rep, n_rep, atom)
    a = lax.all_to_all(a, "rep", split_axis=2, concat_axis=0, tiled=True)
    a = a.reshape(n_rep * rows, (per_v // n_rep) * atom)
    a = lax.all_gather(a, "virt", axis=1, tiled=True)

    b = masked.reshape(per_k, atom, nb)
    b = jnp.concatenate([b, jnp.zeros((n_rep - per_k, atom, nb), b.dtype)], axis=0)
    dest = jnp.arange(n_rep)
    send_idx = (dest - per_k * r) % n_rep
    b = jnp.take(b, send_idx, axis=0)
    b = lax.all_to_all(b, "rep", split_axis=0, concat_axis=0, tiled=True)
    got = (r - per_k * dest) % n_rep
    keep = jnp.nonzero(got < per_k, size=per_k)[0]
    b = jnp.take(b, keep, axis=0)
    b = lax.all_gather(b, "occ", axis=0, tiled=True)
    b = b.reshape(-1, nb)

    partial_sum = jnp.dot(a, b, preferred_element_type=jnp.float32)
    return lax.psum_scatter(partial_sum, "rep", scatter_dimension=0, tiled=True)


def solution(mesh):
    n_rep = mesh.shape["rep"]
    in_specs = (P(("occ", "rep"), "virt"), P(("occ", "rep"), "virt"), P(("occ", "rep")), P("virt"))
    out_specs = P(("occ", "rep"), "virt")

    def body(amplitudes, integrals, cd_irrep, ab_irrep):
        return local(amplitudes, integrals, cd_irrep, ab_irrep, n_rep)

    return jax.shard_map(body, mesh=mesh, in_specs=in_specs, out_specs=out_specs, check_vma=False)
```

time: 315 us -> 168 us (0.53)
  waiting for transfers between devices: 223 us -> 121 us
  blocking collectives: 61.5 us -> 16.5 us
  local copies, waits for them, and re-layouts: 12.9 us -> 4.37 us
  starting transfers between devices: 0.04 us -> 5.43 us
  other arithmetic: 0 us -> 4.53 us
    reduce_scatter x1, waiting for transfers between devices: 152 us -> 27.7 us  [local(): return lax.psum_scatter(partial_sum, 'rep', scatter_dimension=0, tiled=True)]
    all_to_all x1, blocking collectives: 61.5 us -> 16.5 us  [local(): a = lax.all_to_all(a, 'rep', split_axis=2, concat_axis=0, tiled=True)]
    all_gather x1 -> x2, waiting for transfers between devices: 70.1 us -> 91.8 us  [the longest x1 48 us: local(): a = lax.all_gather(a, 'virt', axis=1, tiled=True)]
    all_to_all x2 -> x0, local copies, waits for them, and re-layouts: 7.25 us -> none  [local(): lax.all_to_all(columns, ('occ', 'rep'), split_axis=1, concat_axis=0, tile...]
    all_to_all x0 -> x1, starting transfers between devices: none -> 5.39 us  [local(): b = lax.all_to_all(b, 'rep', split_axis=0, concat_axis=0, tiled=True)]
    unnamed x7, local copies, waits for them, and re-layouts: 5.65 us -> 0.84 us
  transfers between devices with their start and end apart: 2 -> 4, of which waited for: 2 -> 4; matrix products, arithmetic and copies ran while one was open for 0% -> 3% of each run, Pallas kernels for 0% -> 0%
where the time goes in v1:
time: 168 us
  waiting for transfers between devices  121 us (72%)
  blocking collectives  16.5 us (10%)
  between operations  13.2 us (8%)
  starting transfers between devices  5.43 us (3%)
  other arithmetic  4.53 us (3%)
  local copies, waits for them, and re-layouts  4.37 us (3%)
  matrix products  2.84 us (2%)
    all_gather x1, waiting for transfers between devices, local(): a = lax.all_gather(a, 'virt', axis=1, tiled=True)  48 us
    all_gather x1, waiting for transfers between devices, local(): b = lax.all_gather(b, 'occ', axis=0, tiled=True)  43.8 us
    reduce_scatter x1, waiting for transfers between devices, local(): return lax.psum_scatter(partial_sum, 'rep', scatter_dimension=0, tiled=True)  27.7 us
    all_to_all x1, blocking collectives, local(): a = lax.all_to_all(a, 'rep', split_axis=2, concat_axis=0, tiled=True)  16.5 us
    all_to_all x1, starting transfers between devices, local(): b = lax.all_to_all(b, 'rep', split_axis=0, concat_axis=0, tiled=True)  5.39 us
  transfers between devices with their start and end apart: 4, of which 4 were waited for; matrix products, arithmetic and copies ran while one was open for 3% of the time, Pallas kernels for 0%

profile of v1, /device:TPU:6, one launch (start us, length us, event | category | flops | bytes accessed | tf_op | source)
XLA Modules:
  0.0 167.5 jit_solution(85859755080935862)
XLA Ops:
  6.5 1.3 reshape.213
  7.9 0.1 copy.8
  8.0 16.5 %all_to_all.20 = bf16[64,4,4,80]{3,1,0,2:T(4,128)(2,1)S(1)} all-to-all(bf16[64,4,4,80]{3,1,0,2:T(4,128)(2,1)S(1)} %copy.8), channel_id=1, replica_groups=mesh['occ'=16,'virt'=12,'rep'=4] {'rep'}, dimensions={2} | all-to-all | bytes 327680 | tf_op jit(solution)/shard_map/all_to_all | solution.py:21
  24.4 0.2 reshape.214
  24.6 0.8 copy.9
  25.5 0.1 compare_select_fusion
  25.7 0.6 gather_fusion
  26.2 0.7 broadcast_select_fusion
  27.0 5.4 %all-to-all-start = ((bf16[4,80,256]{2,1,0:T(8,128)(2,1)}), bf16[4,80,256]{2,1,0:T(8,128)(2,1)S(1)}, u32[]{:S(2)}, u32[]{:S(2)}) async-start(bf16[4,80,256]{2,1,0:T(8,128)(2,1)} %broadcast_select_fusion), calls=%async_computation | async-start | bytes 327680 | tf_op jit(solution)/shard_map/all_to_all | solution.py:30
  32.4 0.2 reduce-window.6
  32.6 0.6 scatter_custom_fusion
  33.2 0.2 select_n.131
  33.4 0.6 fusion
  34.0 0.7 fusion.9
  34.7 0.7 compare_and_fusion.1
  35.3 1.1 all-to-all-done
  36.5 0.6 gather_fusion.1
  37.0 0.7 broadcast_select_fusion.1
  37.8 0.0 reduce-scatter.4.cloned.1.call-start
  37.8 48.0 %all-gather.5.cloned.1.call-done = bf16[256,3840]{0,1:T(8,128)(2,1)} async-done(((bf16[256,320]{0,1:T(8,128)(2,1)}), bf16[256,3840]{0,1:T(8,128)(2,1)}) %all-gather.5.cloned.1.call-update) | async-done | bytes 1966096 | tf_op jit(solution)/shard_map/all_gather | solution.py:23
  85.8 43.8 %all-gather.3.cloned.1.call-done = bf16[48,80,256]{2,1,0:T(8,128)(2,1)} async-done(((bf16[3,80,256]{2,1,0:T(8,128)(2,1)}), bf16[48,80,256]{2,1,0:T(8,128)(2,1)}) %all-gather.3.cloned.1.call-update) | async-done | bytes 1966096 | tf_op jit(solution)/shard_map/all_gather | solution.py:34
  129.6 2.8 %convolution_bitcast_fusion = f32[256,256]{0,1:T(8,128)S(1)} fusion(bf16[3840,256]{1,0:T(8,128)(2,1)} %bitcast.25, bf16[256,3840]{0,1:T(8,128)(2,1)} %all-gather.5.cloned.1.call-done), kind=kOutput, calls=%fused_computation.3 | convolution fusion | flops 503316480 | bytes 4194304 | tf_op jit(solution)/shard_map/dot_general | solution.py:37
  132.4 0.8 copy.11
  133.3 27.7 %reduce-scatter.4.cloned.1.call-done = f32[64,256]{1,0:T(8,128)} async-done(((f32[256,256]{1,0:T(8,128)}), f32[64,256]{1,0:T(8,128)}) %reduce-scatter.4.cloned.1.call-update) | async-done | bytes 65552 | tf_op jit(solution)/shard_map/reduce_scatter | solution.py:38
  (19 shorter events, 0.1 us)
Async XLA Ops:
  6.5 18.9 %copy-start.1 = (s32[256]{0:T(256)S(1)}, s32[256]{0:T(256)}, u32[]{:S(2)}) copy-start(s32[256]{0:T(256)} %param.7) | copy-start | bytes 3076
  6.5 18.9 %copy-start.2 = (s32[240]{0:T(256)S(1)}, s32[240]{0:T(256)}, u32[]{:S(2)}) copy-start(s32[240]{0:T(256)} %param.6) | copy-start | bytes 2884
  6.5 18.9 %copy-start = (bf16[240,256]{1,0:T(8,128)(2,1)S(1)}, bf16[240,256]{1,0:T(8,128)(2,1)}, u32[]{:S(2)}) copy-start(bf16[240,256]{1,0:T(8,128)(2,1)} %param.5) | copy-start | bytes 368644
  6.5 79.2 %all-gather.5.cloned.1.call-start = ((), (), s32[]{:S(2)}) async-start(), calls=%async_computation.4 | async-start | bytes 2129920 | tf_op jit(solution)/shard_map/all_gather | solution.py:23
  27.0 9.5 %all-to-all-start = ((bf16[4,80,256]{2,1,0:T(8,128)(2,1)}), bf16[4,80,256]{2,1,0:T(8,128)(2,1)S(1)}, u32[]{:S(2)}, u32[]{:S(2)}) async-start(bf16[4,80,256]{2,1,0:T(8,128)(2,1)} %broadcast_select_fusion), calls=%async_computation | async-start | bytes 327680 | tf_op jit(solution)/shard_map/all_to_all | solution.py:30
  32.4 97.2 %all-gather.3.cloned.1.call-start = ((), (), s32[]{:S(2)}) async-start(), calls=%async_computation.3 | async-start | bytes 2088960 | tf_op jit(solution)/shard_map/all_gather | solution.py:34
  37.8 123.2 %reduce-scatter.4.cloned.1.call-start = ((), (), s32[]{:S(2)}) async-start(), calls=%async_computation.5 | async-start | bytes 327680 | tf_op jit(solution)/shard_map/reduce_scatter | solution.py:38
Sparse Core Ops, SparseCore 0:
  25.6 60.1 all-gather.4
  88.2 41.3 all-gather.2
  133.4 27.5 reduce-scatter.3

commit v2 on v1

--- a/solution.py
+++ b/solution.py
@@ -31,11 +31,15 @@
     got = (r - per_k * dest) % n_rep
     keep = jnp.nonzero(got < per_k, size=per_k)[0]
     b = jnp.take(b, keep, axis=0)
-    b = lax.all_gather(b, "occ", axis=0, tiled=True)
+    n_occ = lax.axis_size("occ")
+    b = jnp.broadcast_to(b[None], (n_occ,) + b.shape)
+    b = lax.all_to_all(b, "occ", split_axis=0, concat_axis=0, tiled=True)
     b = b.reshape(-1, nb)
 
     partial_sum = jnp.dot(a, b, preferred_element_type=jnp.float32)
-    return lax.psum_scatter(partial_sum, "rep", scatter_dimension=0, tiled=True)
+    partial_sum = partial_sum.reshape(n_rep, rows, nb)
+    partial_sum = lax.all_to_all(partial_sum, "rep", split_axis=0, concat_axis=0, tiled=True)
+    return jnp.sum(partial_sum, axis=0)
 
 
 def solution(mesh):

time: 168 us -> 129 us (0.77); the launches traced: 168 us -> 127 us
  waiting for transfers between devices: 121 us -> 68.7 us
  starting transfers between devices: 5.43 us -> 21.9 us
  blocking collectives: 16.5 us -> 9.2 us
    all_gather x1 -> x0, waiting for transfers between devices: 43.8 us -> none  [local(): b = lax.all_gather(b, 'occ', axis=0, tiled=True)]
    reduce_scatter x1 -> x0, waiting for transfers between devices: 27.7 us -> none  [local(): return lax.psum_scatter(partial_sum, 'rep', scatter_dimension=0, tiled=True)]
    all_gather x1, waiting for transfers between devices: 48 us -> 64.7 us  [local(): a = lax.all_gather(a, 'virt', axis=1, tiled=True)]
    all_to_all x0 -> x2, starting transfers between devices: none -> 9.07 us  [the longest x1 5.36 us: local(): a = lax.all_to_all(a, 'rep', split_axis=2, concat_axis=0, tiled=True)]
    all_to_all x1, starting transfers between devices: 5.39 us -> 12.8 us  [local(): b = lax.all_to_all(b, 'rep', split_axis=0, concat_axis=0, tiled=True)]
    all_to_all x1, blocking collectives: 16.5 us -> 9.2 us  [local(): lax.all_to_all(partial_sum, 'rep', split_axis=0, concat_axis=0, tiled=True)]
    all_to_all x0 -> x2, waiting for transfers between devices: none -> 3.96 us  [the longest x1 3.96 us: local(): a = lax.all_to_all(a, 'rep', split_axis=2, concat_axis=0, tiled=True)]
  transfers between devices with their start and end apart: 4 -> 4, of which waited for: 4 -> 2; matrix products, arithmetic and copies ran while one was open for 3% -> 5% of each run, Pallas kernels for 0% -> 0%
where the time goes in v2:
time: 129 us; the launch traced here: 127 us
  waiting for transfers between devices  68.7 us (53%)
  starting transfers between devices  21.9 us (17%)
  between operations  13.5 us (10%)
  blocking collectives  9.2 us (7%)
  local copies, waits for them, and re-layouts  5.6 us (4%)
  other arithmetic  5.45 us (4%)
  matrix products  2.44 us (2%)
    all_gather x1, waiting for transfers between devices, local(): a = lax.all_gather(a, 'virt', axis=1, tiled=True)  64.7 us
    all_to_all x1, starting transfers between devices, local(): b = lax.all_to_all(b, 'rep', split_axis=0, concat_axis=0, tiled=True)  12.8 us
    all_to_all x1, blocking collectives, local(): lax.all_to_all(partial_sum, 'rep', split_axis=0, concat_axis=0, tiled=True)  9.2 us
    all_to_all x1, starting transfers between devices, local(): a = lax.all_to_all(a, 'rep', split_axis=2, concat_axis=0, tiled=True)  5.36 us
    all_to_all x1, waiting for transfers between devices, local(): a = lax.all_to_all(a, 'rep', split_axis=2, concat_axis=0, tiled=True)  3.96 us
    all_to_all x1, starting transfers between devices, local(): b = lax.all_to_all(b, 'occ', split_axis=0, concat_axis=0, tiled=True)  3.72 us
  transfers between devices with their start and end apart: 4, of which 2 were waited for; matrix products, arithmetic and copies ran while one was open for 5% of the time, Pallas kernels for 0%

profile of v2, /device:TPU:6, one launch (start us, length us, event | category | flops | bytes accessed | tf_op | source)
XLA Modules:
  0.0 126.7 jit_solution(8912482788116381193)
XLA Ops:
  6.6 1.0 compare_select_fusion
  7.6 0.6 gather_fusion
  8.2 0.7 broadcast_select_fusion
  8.9 12.8 %all-to-all-start = ((bf16[4,80,256]{2,1,0:T(8,128)(2,1)}), bf16[4,80,256]{2,1,0:T(8,128)(2,1)S(1)}, u32[]{:S(2)}, u32[]{:S(2)}) async-start(bf16[4,80,256]{2,1,0:T(8,128)(2,1)} %broadcast_select_fusion), calls=%async_computation | async-start | bytes 327680 | tf_op jit(solution)/shard_map/all_to_all | solution.py:30
  21.7 0.6 fusion
  22.4 0.2 reduce-window.6
  22.6 0.6 scatter_custom_fusion
  23.2 0.2 select_n.135
  23.3 0.7 fusion.9
  24.0 0.7 compare_and_fusion.1
  24.7 1.3 %reshape.219 = bf16[64,4,4,80]{3,2,1,0:T(4,128)(2,1)S(1)} reshape(bf16[64,1280]{1,0:T(8,128)(2,1)} %param.4) | data formatting | bytes 327680 | tf_op jit(solution)/shard_map/reshape | solution.py:20
  26.0 0.8 copy.6
  26.8 5.4 %all-to-all-start.2 = ((bf16[64,4,4,80]{3,1,0,2:T(4,128)(2,1)}), bf16[64,4,4,80]{3,1,0,2:T(4,128)(2,1)S(1)}, u32[]{:S(2)}, u32[]{:S(2)}) async-start(bf16[64,4,4,80]{3,1,0,2:T(4,128)(2,1)} %copy.6), calls=%async_computation.2 | async-start | bytes 524288 | tf_op jit(solution)/shard_map/all_to_all | solution.py:21
  32.1 0.6 gather_fusion.1
  32.7 0.1 broadcast_select_fusion.1
  32.8 4.0 %all-to-all-done.2 = bf16[64,4,4,80]{3,1,0,2:T(4,128)(2,1)S(1)} async-done(((bf16[64,4,4,80]{3,1,0,2:T(4,128)(2,1)}), bf16[64,4,4,80]{3,1,0,2:T(4,128)(2,1)S(1)}, u32[]{:S(2)}, u32[]{:S(2)}) %all-to-all-start.2) | async-done | bytes 163872 | tf_op jit(solution)/shard_map/all_to_all | solution.py:21
  36.7 1.4 %broadcast_in_dim.47 = bf16[16,3,80,256]{3,2,1,0:T(8,128)(2,1)} broadcast(bf16[3,80,256]{2,1,0:T(8,128)(2,1)S(1)} %broadcast_select_fusion.1), dimensions={1,2,3} | broadcast | bytes 2088960 | tf_op jit(solution)/shard_map/broadcast_in_dim | solution.py:35
  38.1 3.7 %all-to-all-start.1 = ((bf16[16,3,80,256]{3,2,1,0:T(8,128)(2,1)}), bf16[16,3,80,256]{3,2,1,0:T(8,128)(2,1)S(1)}, u32[]{:S(2)}, u32[]{:S(2)}) async-start(bf16[16,3,80,256]{3,2,1,0:T(8,128)(2,1)} %broadcast_in_dim.47), calls=%async_computation.1 | async-start | bytes 3932160 | tf_op jit(solution)/shard_map/all_to_all | solution.py:36
  41.9 0.2 reshape.220
  42.1 0.8 copy.7
  42.9 64.7 %all-gather.2.cloned.1.call-done = bf16[256,3840]{0,1:T(8,128)(2,1)} async-done(((bf16[256,320]{0,1:T(8,128)(2,1)}), bf16[256,3840]{0,1:T(8,128)(2,1)}) %all-gather.2.cloned.1.call-update) | async-done | bytes 1966096 | tf_op jit(solution)/shard_map/all_gather | solution.py:23
  107.6 2.4 %fusion.12 = f32[256,256]{0,1:T(8,128)S(1)} fusion(bf16[3840,256]{1,0:T(8,128)(2,1)S(1)} %bitcast.23, bf16[256,3840]{0,1:T(8,128)(2,1)} %all-gather.2.cloned.1.call-done), kind=kOutput, calls=%fused_computation.49 | convolution fusion | flops 503316480 | bytes 4194304 | tf_op jit(solution)/shard_map/dot_general | solution.py:39
  110.0 9.2 %all_to_all.30 = f32[4,64,256]{2,1,0:T(8,128)S(1)} all-to-all(f32[4,64,256]{2,1,0:T(8,128)S(1)} %bitcast.26), channel_id=1, replica_groups=mesh['occ'=16,'virt'=12,'rep'=4] {'rep'}, dimensions={0} | all-to-all | bytes 524288 | tf_op jit(solution)/shard_map/all_to_all | solution.py:41
  119.2 0.6 reduce_sum.19
  (12 shorter events, 0.1 us)
Async XLA Ops:
  8.9 17.8 %all-to-all-start = ((bf16[4,80,256]{2,1,0:T(8,128)(2,1)}), bf16[4,80,256]{2,1,0:T(8,128)(2,1)S(1)}, u32[]{:S(2)}, u32[]{:S(2)}) async-start(bf16[4,80,256]{2,1,0:T(8,128)(2,1)} %broadcast_select_fusion), calls=%async_computation | async-start | bytes 327680 | tf_op jit(solution)/shard_map/all_to_all | solution.py:30
  26.8 10.0 %all-to-all-start.2 = ((bf16[64,4,4,80]{3,1,0,2:T(4,128)(2,1)}), bf16[64,4,4,80]{3,1,0,2:T(4,128)(2,1)S(1)}, u32[]{:S(2)}, u32[]{:S(2)}) async-start(bf16[64,4,4,80]{3,1,0,2:T(4,128)(2,1)} %copy.6), calls=%async_computation.2 | async-start | bytes 524288 | tf_op jit(solution)/shard_map/all_to_all | solution.py:21
  38.1 69.5 %all-to-all-start.1 = ((bf16[16,3,80,256]{3,2,1,0:T(8,128)(2,1)}), bf16[16,3,80,256]{3,2,1,0:T(8,128)(2,1)S(1)}, u32[]{:S(2)}, u32[]{:S(2)}) async-start(bf16[16,3,80,256]{3,2,1,0:T(8,128)(2,1)} %broadcast_in_dim.47), calls=%async_computation.1 | async-start | bytes 3932160 | tf_op jit(solution)/shard_map/all_to_all | solution.py:36
  41.9 65.7 %all-gather.2.cloned.1.call-start = ((), (), s32[]{:S(2)}) async-start(), calls=%async_computation.4 | async-start | bytes 2129920 | tf_op jit(solution)/shard_map/all_gather | solution.py:23
Sparse Core Ops, SparseCore 0:
  45.1 62.4 all-gather.1

commit v3 on v2

v3 whole, which is shorter than its diff:
```python
import math

import jax
import jax.numpy as jnp
from jax import lax
from jax.sharding import Mesh
from jax.sharding import PartitionSpec as P


def local(amplitudes, integrals, cd_irrep, ab_irrep, n_rep, n_oy, n_oc):
    rows, cols = amplitudes.shape
    kb, nb = integrals.shape
    atom = math.gcd(cols, kb)
    per_v = cols // atom
    per_k = kb // atom
    assert per_v % n_rep == 0 and per_k == n_rep - 1
    r = lax.axis_index("rep")

    a = amplitudes.reshape(rows, per_v // n_rep, n_rep, atom)
    a = jnp.transpose(a, (2, 0, 1, 3)).reshape(n_rep, rows, (per_v // n_rep) * atom)
    a = lax.all_to_all(a, "rep", split_axis=0, concat_axis=0, tiled=True)
    a = a.reshape(n_rep * rows, (per_v // n_rep) * atom)
    a, integrals, cd_irrep, ab_irrep = lax.optimization_barrier((a, integrals, cd_irrep, ab_irrep))
    a = lax.all_gather(a, "virt", axis=1, tiled=True)

    masked = jnp.where(cd_irrep[:, None] == ab_irrep[None, :], integrals, jnp.zeros_like(integrals))
    b = masked.reshape(per_k, atom, nb)
    b = jnp.concatenate([b, jnp.zeros((n_rep - per_k, atom, nb), b.dtype)], axis=0)
    b = lax.dynamic_slice_in_dim(jnp.concatenate([b, b], axis=0), r, n_rep, axis=0)
    b = lax.all_to_all(b, "rep", split_axis=0, concat_axis=0, tiled=True)
    q = (n_rep - 1 - r) % n_rep
    skip = (jnp.arange(per_k) >= q)[:, None, None]
    b = jnp.where(skip, b[1:], b[:-1])
    b = jnp.broadcast_to(b[None], (n_oy,) + b.shape)
    b = lax.all_to_all(b, "oy", split_axis=0, concat_axis=0, tiled=True)
    b = jnp.broadcast_to(b[None], (n_oc,) + b.shape)
    b = lax.all_to_all(b, "oc", split_axis=0, concat_axis=0, tiled=True)
    b = jnp.moveaxis(b, 0, 1).reshape(-1, nb)

    partial_sum = jnp.dot(a, b, preferred_element_type=jnp.float32)
    partial_sum = partial_sum.reshape(n_rep, rows, nb)
    partial_sum = lax.all_to_all(partial_sum, "rep", split_axis=0, concat_axis=0, tiled=True)
    return jnp.sum(partial_sum, axis=0)


def solution(mesh):
    n_occ, n_virt, n_rep = mesh.shape["occ"], mesh.shape["virt"], mesh.shape["rep"]
    n_oc = 2 if n_occ % 2 == 0 else 1
    n_oy = n_occ // n_oc
    fine = Mesh(mesh.devices.reshape(n_oy, n_oc, n_virt, n_rep), ("oy", "oc", "virt", "rep"))
    rows_spec = ("oy", "oc", "rep")
    in_specs = (P(rows_spec, "virt"), P(rows_spec, "virt"), P(rows_spec), P("virt"))
    out_specs = P(rows_spec, "virt")

    def body(amplitudes, integrals, cd_irrep, ab_irrep):
        return local(amplitudes, integrals, cd_irrep, ab_irrep, n_rep, n_oy, n_oc)

    return jax.shard_map(body, mesh=fine, in_specs=in_specs, out_specs=out_specs, check_vma=False)
```

time: 129 us -> 110 us (0.85)
  blocking collectives: 9.2 us -> 55.1 us
  waiting for transfers between devices: 68.7 us -> 23.8 us
  starting transfers between devices: 21.9 us -> 5.39 us
  other arithmetic: 5.45 us -> 1.62 us
    all_to_all x0 -> x3, blocking collectives: none -> 45.8 us  [the longest x1 24.4 us: local(): b = lax.all_to_all(b, 'oy', split_axis=0, concat_axis=0, tiled=True)]
    all_gather x1, waiting for transfers between devices: 64.7 us -> 19.7 us  [local(): a = lax.all_gather(a, 'virt', axis=1, tiled=True)]
    all_to_all x2 -> x0, starting transfers between devices: 9.07 us -> none  [the longest x1 5.36 us: local(): a = lax.all_to_all(a, 'rep', split_axis=2, concat_axis=0, tiled=True)]
    all_to_all x1, starting transfers between devices: 12.8 us -> 5.39 us  [local(): b = lax.all_to_all(b, 'rep', split_axis=0, concat_axis=0, tiled=True)]
    all_to_all x1, waiting for transfers between devices: 0.01 us -> 4.08 us  [local(): b = lax.all_to_all(b, 'rep', split_axis=0, concat_axis=0, tiled=True)]
    all_gather x0 -> x1, local copies, waits for them, and re-layouts: none -> 3.98 us  [local(): a = lax.all_gather(a, 'virt', axis=1, tiled=True)]
    all_to_all x2 -> x0, waiting for transfers between devices: 3.96 us -> none  [the longest x1 3.96 us: local(): a = lax.all_to_all(a, 'rep', split_axis=2, concat_axis=0, tiled=True)]
    select_n x6 -> x1, other arithmetic: 1.68 us -> 0.08 us  [local(): b = jnp.where(skip, b[1:], b[:-1])]
  transfers between devices with their start and end apart: 4 -> 2, of which waited for: 2 -> 2; matrix products, arithmetic and copies ran while one was open for 5% -> 1% of each run, Pallas kernels for 0% -> 0%
where the time goes in v3:
time: 110 us; the launch traced here: 108 us
  blocking collectives  55.1 us (50%)
  waiting for transfers between devices  23.8 us (22%)
  between operations  13.5 us (12%)
  local copies, waits for them, and re-layouts  6.79 us (6%)
  starting transfers between devices  5.39 us (5%)
  matrix products  2.22 us (2%)
  other arithmetic  1.62 us (1%)
    all_to_all x1, blocking collectives, local(): b = lax.all_to_all(b, 'oy', split_axis=0, concat_axis=0, tiled=True)  24.4 us
    all_gather x1, waiting for transfers between devices, local(): a = lax.all_gather(a, 'virt', axis=1, tiled=True)  19.7 us
    all_to_all x1, blocking collectives, local(): a = lax.all_to_all(a, 'rep', split_axis=0, concat_axis=0, tiled=True)  16.1 us
    all_to_all x1, blocking collectives, local(): lax.all_to_all(partial_sum, 'rep', split_axis=0, concat_axis=0, tiled=True)  9.29 us
    all_to_all x1, starting transfers between devices, local(): b = lax.all_to_all(b, 'rep', split_axis=0, concat_axis=0, tiled=True)  5.39 us
    all_to_all x1, blocking collectives, local(): b = lax.all_to_all(b, 'oc', split_axis=0, concat_axis=0, tiled=True)  5.31 us
    all_to_all x1, waiting for transfers between devices, local(): b = lax.all_to_all(b, 'rep', split_axis=0, concat_axis=0, tiled=True)  4.08 us
    all_gather x1, local copies, waits for them, and re-layouts, local(): a = lax.all_gather(a, 'virt', axis=1, tiled=True)  3.98 us
  transfers between devices with their start and end apart: 2, of which 2 were waited for; matrix products, arithmetic and copies ran while one was open for 1% of the time, Pallas kernels for 0%

profile of v3, /device:TPU:6, one launch (start us, length us, event | category | flops | bytes accessed | tf_op | source)
XLA Modules:
  0.0 108.4 jit_solution(5150793519434451373)
XLA Ops:
  6.5 1.3 %reshape.25 = bf16[64,4,4,80]{3,2,1,0:T(4,128)(2,1)S(1)} reshape(bf16[64,1280]{1,0:T(8,128)(2,1)} %param.4) | data formatting | bytes 327680 | tf_op jit(solution)/shard_map/reshape | solution.py:19
  7.9 0.1 copy.11
  8.0 0.2 reshape.26
  8.2 16.1 %all_to_all.25 = bf16[4,64,320]{2,1,0:T(8,128)(2,1)S(1)} all-to-all(bf16[4,64,320]{2,1,0:T(8,128)(2,1)S(1)} %reshape.26), channel_id=1, replica_groups=mesh['oy'=8,'oc'=2,'virt'=12,'rep'=4] {'rep'}, dimensions={0} | all-to-all | bytes 327680 | tf_op jit(solution)/shard_map/all_to_all | solution.py:21
  24.3 0.8 copy.7
  25.1 0.0 all-gather.2.cloned.1.call-update
  25.1 0.0 copy-done
  25.1 0.0 copy-done.2
  25.1 0.0 copy-done.1
  25.1 0.1 compare_select_fusion
  25.3 0.8 fusion.2
  26.0 5.4 %all-to-all-start.1 = ((bf16[4,80,256]{2,1,0:T(8,128)(2,1)}), bf16[4,80,256]{2,1,0:T(8,128)(2,1)S(1)}, u32[]{:S(2)}, u32[]{:S(2)}) async-start(bf16[4,80,256]{2,1,0:T(8,128)(2,1)} %fusion.2), calls=%async_computation.1 | async-start | bytes 327680 | tf_op jit(solution)/shard_map/all_to_all | solution.py:30
  31.4 4.1 %all-to-all-done.1 = bf16[4,80,256]{2,1,0:T(8,128)(2,1)S(1)} async-done(((bf16[4,80,256]{2,1,0:T(8,128)(2,1)}), bf16[4,80,256]{2,1,0:T(8,128)(2,1)S(1)}, u32[]{:S(2)}, u32[]{:S(2)}) %all-to-all-start.1) | async-done | bytes 163872 | tf_op jit(solution)/shard_map/all_to_all | solution.py:30
  35.5 0.1 slice_select_fusion
  35.6 0.1 broadcast_in_dim.32
  35.7 24.4 %all_to_all.26 = bf16[8,3,80,256]{3,2,1,0:T(8,128)(2,1)S(1)} all-to-all(bf16[8,3,80,256]{3,2,1,0:T(8,128)(2,1)S(1)} %broadcast_in_dim.32), channel_id=1, replica_groups=mesh['oy'=8,'oc'=2,'virt'=12,'rep'=4] {'oy'}, dimensions={0} | all-to-all | bytes 1966080 | tf_op jit(solution)/shard_map/all_to_all | solution.py:35
  60.1 0.1 broadcast_in_dim.33
  60.2 5.3 %all_to_all.27 = bf16[2,8,3,80,256]{4,3,2,1,0:T(8,128)(2,1)S(1)} all-to-all(bf16[2,8,3,80,256]{4,3,2,1,0:T(8,128)(2,1)S(1)} %broadcast_in_dim.33), channel_id=1, replica_groups=mesh['oy'=8,'oc'=2,'virt'=12,'rep'=4] {'oc'}, dimensions={0} | all-to-all | bytes 3932160 | tf_op jit(solution)/shard_map/all_to_all | solution.py:37
  65.5 0.2 copy.9
  65.7 19.7 %all-gather.2.cloned.1.call-done = bf16[256,3840]{0,1:T(8,128)(2,1)} async-done(((bf16[256,320]{0,1:T(8,128)(2,1)}), bf16[256,3840]{0,1:T(8,128)(2,1)}) %all-gather.2.cloned.1.call-update) | async-done | bytes 1966096 | tf_op jit(solution)/shard_map/all_gather | solution.py:24
  85.4 4.0 %copy.8 = bf16[256,3840]{1,0:T(8,128)(2,1)} copy(bf16[256,3840]{0,1:T(8,128)(2,1)} %all-gather.2.cloned.1.call-done) | data formatting | bytes 3932160 | tf_op jit(solution)/shard_map/all_gather | solution.py:24
  89.4 2.2 %fusion.3 = f32[4,64,256]{2,1,0:T(8,128)S(1)} fusion(bf16[4,64,3840]{2,1,0:T(8,128)(2,1)} %bitcast.13, bf16[3840,256,1]{1,0,2:T(8,128)(2,1)S(1)} %bitcast.12), kind=kOutput, calls=%fused_computation.11 | convolution fusion | flops 503316480 | bytes 4194304 | tf_op jit(solution)/shard_map/dot_general | solution.py:40
  91.6 9.3 %all_to_all.28 = f32[4,64,256]{2,1,0:T(8,128)S(1)} all-to-all(f32[4,64,256]{2,1,0:T(8,128)S(1)} %fusion.3), channel_id=1, replica_groups=mesh['oy'=8,'oc'=2,'virt'=12,'rep'=4] {'rep'}, dimensions={0} | all-to-all | bytes 524288 | tf_op jit(solution)/shard_map/all_to_all | solution.py:42
  100.9 0.6 reduce_sum.9
  (6 shorter events, 0.0 us)
Async XLA Ops:
  6.5 18.6 %copy-start = (bf16[240,256]{1,0:T(8,128)(2,1)S(1)}, bf16[240,256]{1,0:T(8,128)(2,1)}, u32[]{:S(2)}) copy-start(bf16[240,256]{1,0:T(8,128)(2,1)} %param.5) | copy-start | bytes 368644
  6.5 18.6 %copy-start.2 = (s32[240]{0:T(256)S(1)}, s32[240]{0:T(256)}, u32[]{:S(2)}) copy-start(s32[240]{0:T(256)} %param.6) | copy-start | bytes 2884
  6.5 18.6 %copy-start.1 = (s32[256]{0:T(256)S(1)}, s32[256]{0:T(256)}, u32[]{:S(2)}) copy-start(s32[256]{0:T(256)} %param.7) | copy-start | bytes 3076
  6.5 78.9 %all-gather.2.cloned.1.call-start = ((), (), s32[]{:S(2)}) async-start(), calls=%async_computation.5 | async-start | bytes 2129920 | tf_op jit(solution)/shard_map/all_gather | solution.py:24
  26.0 9.5 %all-to-all-start.1 = ((bf16[4,80,256]{2,1,0:T(8,128)(2,1)}), bf16[4,80,256]{2,1,0:T(8,128)(2,1)S(1)}, u32[]{:S(2)}, u32[]{:S(2)}) async-start(bf16[4,80,256]{2,1,0:T(8,128)(2,1)} %fusion.2), calls=%async_computation.1 | async-start | bytes 327680 | tf_op jit(solution)/shard_map/all_to_all | solution.py:30
Sparse Core Ops, SparseCore 0:
  25.2 60.1 all-gather.1

commit v4 on v3

--- a/solution.py
+++ b/solution.py
@@ -21,7 +21,7 @@
     a = lax.all_to_all(a, "rep", split_axis=0, concat_axis=0, tiled=True)
     a = a.reshape(n_rep * rows, (per_v // n_rep) * atom)
     a, integrals, cd_irrep, ab_irrep = lax.optimization_barrier((a, integrals, cd_irrep, ab_irrep))
-    a = lax.all_gather(a, "virt", axis=1, tiled=True)
+    a = lax.all_gather(a, "virt", axis=0, tiled=False)
 
     masked = jnp.where(cd_irrep[:, None] == ab_irrep[None, :], integrals, jnp.zeros_like(integrals))
     b = masked.reshape(per_k, atom, nb)
@@ -35,9 +35,9 @@
     b = lax.all_to_all(b, "oy", split_axis=0, concat_axis=0, tiled=True)
     b = jnp.broadcast_to(b[None], (n_oc,) + b.shape)
     b = lax.all_to_all(b, "oc", split_axis=0, concat_axis=0, tiled=True)
-    b = jnp.moveaxis(b, 0, 1).reshape(-1, nb)
+    b = jnp.moveaxis(b, 0, 1).reshape(a.shape[0], a.shape[2], nb)
 
-    partial_sum = jnp.dot(a, b, preferred_element_type=jnp.float32)
+    partial_sum = jnp.einsum("vmc,vcn->mn", a, b, preferred_element_type=jnp.float32)
     partial_sum = partial_sum.reshape(n_rep, rows, nb)
     partial_sum = lax.all_to_all(partial_sum, "rep", split_axis=0, concat_axis=0, tiled=True)
     return jnp.sum(partial_sum, axis=0)

time: 110 us -> 107 us (0.973)
  local copies, waits for them, and re-layouts: 6.79 us -> 2.01 us
    all_gather x1 -> x0, local copies, waits for them, and re-layouts: 3.98 us -> none  [local(): a = lax.all_gather(a, 'virt', axis=1, tiled=True)]
    all_to_all x1, blocking collectives: 16.1 us -> 17.5 us  [local(): a = lax.all_to_all(a, 'rep', split_axis=0, concat_axis=0, tiled=True)]
    all_to_all x1, blocking collectives: 24.4 us -> 23.1 us  [local(): b = lax.all_to_all(b, 'oy', split_axis=0, concat_axis=0, tiled=True)]
    all_gather x1, waiting for transfers between devices: 19.7 us -> 20.8 us  [local(): a = lax.all_gather(a, 'virt', axis=0, tiled=False)]
where the time goes in v4:
time: 107 us; the launch traced here: 105 us
  blocking collectives  55.1 us (51%)
  waiting for transfers between devices  24.9 us (23%)
  between operations  13.5 us (13%)
  starting transfers between devices  5.39 us (5%)
  matrix products  2.37 us (2%)
  local copies, waits for them, and re-layouts  2.01 us (2%)
  other arithmetic  1.61 us (2%)
    all_to_all x1, blocking collectives, local(): b = lax.all_to_all(b, 'oy', split_axis=0, concat_axis=0, tiled=True)  23.1 us
    all_gather x1, waiting for transfers between devices, local(): a = lax.all_gather(a, 'virt', axis=0, tiled=False)  20.8 us
    all_to_all x1, blocking collectives, local(): a = lax.all_to_all(a, 'rep', split_axis=0, concat_axis=0, tiled=True)  17.5 us
    all_to_all x1, blocking collectives, local(): lax.all_to_all(partial_sum, 'rep', split_axis=0, concat_axis=0, tiled=True)  9.25 us
    all_to_all x1, starting transfers between devices, local(): b = lax.all_to_all(b, 'rep', split_axis=0, concat_axis=0, tiled=True)  5.39 us
    all_to_all x1, blocking collectives, local(): b = lax.all_to_all(b, 'oc', split_axis=0, concat_axis=0, tiled=True)  5.31 us
    all_to_all x1, waiting for transfers between devices, local(): b = lax.all_to_all(b, 'rep', split_axis=0, concat_axis=0, tiled=True)  4.08 us
    dot_general x1, matrix products, local(): jnp.einsum('vmc,vcn->mn', a, b, preferred_element_type=jnp.float32)  2.37 us
  transfers between devices with their start and end apart: 2, of which 2 were waited for; matrix products, arithmetic and copies ran while one was open for 1% of the time, Pallas kernels for 0%

profile of v4, /device:TPU:6, one launch (start us, length us, event | category | flops | bytes accessed | tf_op | source)
XLA Modules:
  0.0 105.0 jit_solution(2808136457842295227)
XLA Ops:
  6.5 0.0 copy-start
  6.5 0.0 all-gather.3.cloned.1.call-start
  6.5 1.3 %reshape.25 = bf16[64,4,4,80]{3,2,1,0:T(4,128)(2,1)S(1)} reshape(bf16[64,1280]{1,0:T(8,128)(2,1)} %param.4) | data formatting | bytes 327680 | tf_op jit(solution)/shard_map/reshape | solution.py:19
  7.9 0.1 copy.11
  8.0 0.2 reshape.26
  8.2 17.5 %all_to_all.25 = bf16[4,64,320]{2,1,0:T(8,128)(2,1)} all-to-all(bf16[4,64,320]{2,1,0:T(8,128)(2,1)S(1)} %reshape.26), channel_id=1, replica_groups=mesh['oy'=8,'oc'=2,'virt'=12,'rep'=4] {'rep'}, dimensions={0} | all-to-all | bytes 327680 | tf_op jit(solution)/shard_map/all_to_all | solution.py:21
  25.7 0.0 all-gather.3.cloned.1.call-update
  25.7 0.0 copy-done
  25.7 0.0 copy-done.2
  25.8 0.0 copy-done.1
  25.8 0.1 compare_select_fusion
  25.9 0.8 fusion.2
  26.7 5.4 %all-to-all-start.1 = ((bf16[4,80,256]{2,1,0:T(8,128)(2,1)}), bf16[4,80,256]{2,1,0:T(8,128)(2,1)S(1)}, u32[]{:S(2)}, u32[]{:S(2)}) async-start(bf16[4,80,256]{2,1,0:T(8,128)(2,1)} %fusion.2), calls=%async_computation.1 | async-start | bytes 327680 | tf_op jit(solution)/shard_map/all_to_all | solution.py:30
  32.1 4.1 %all-to-all-done.1 = bf16[4,80,256]{2,1,0:T(8,128)(2,1)S(1)} async-done(((bf16[4,80,256]{2,1,0:T(8,128)(2,1)}), bf16[4,80,256]{2,1,0:T(8,128)(2,1)S(1)}, u32[]{:S(2)}, u32[]{:S(2)}) %all-to-all-start.1) | async-done | bytes 163872 | tf_op jit(solution)/shard_map/all_to_all | solution.py:30
  36.1 0.1 slice_select_fusion
  36.2 0.1 broadcast_in_dim.32
  36.3 23.1 %all_to_all.26 = bf16[8,3,80,256]{3,2,1,0:T(8,128)(2,1)S(1)} all-to-all(bf16[8,3,80,256]{3,2,1,0:T(8,128)(2,1)S(1)} %broadcast_in_dim.32), channel_id=1, replica_groups=mesh['oy'=8,'oc'=2,'virt'=12,'rep'=4] {'oy'}, dimensions={0} | all-to-all | bytes 1966080 | tf_op jit(solution)/shard_map/all_to_all | solution.py:35
  59.4 0.1 broadcast_in_dim.33
  59.5 5.3 %all_to_all.27 = bf16[2,8,3,80,256]{4,3,2,1,0:T(8,128)(2,1)S(1)} all-to-all(bf16[2,8,3,80,256]{4,3,2,1,0:T(8,128)(2,1)S(1)} %broadcast_in_dim.33), channel_id=1, replica_groups=mesh['oy'=8,'oc'=2,'virt'=12,'rep'=4] {'oc'}, dimensions={0} | all-to-all | bytes 3932160 | tf_op jit(solution)/shard_map/all_to_all | solution.py:37
  64.8 0.2 copy.8
  65.0 20.8 %all-gather.3.cloned.1.call-done = bf16[3072,320]{1,0:T(8,128)(2,1)} async-done(((bf16[256,320]{1,0:T(8,128)(2,1)}), bf16[3072,320]{1,0:T(8,128)(2,1)}) %all-gather.3.cloned.1.call-update) | async-done | bytes 1966096 | tf_op jit(solution)/shard_map/all_gather | solution.py:24
  85.8 2.4 %convolution_bitcast_fusion = f32[4,64,256]{2,1,0:T(8,128)S(1)} fusion(bf16[4,64,320,12]{2,1,0,3:T(8,128)(2,1)} %bitcast.25, bf16[12,320,256,1]{2,1,3,0:T(8,128)(2,1)S(1)} %bitcast.21), kind=kOutput, calls=%fused_computation | convolution fusion | flops 503316480 | bytes 4194304 | tf_op jit(solution)/shard_map/vmc,vcn->mn/dot_general | solution.py:40
  88.2 9.2 %all_to_all.28 = f32[4,64,256]{2,1,0:T(8,128)S(1)} all-to-all(f32[4,64,256]{2,1,0:T(8,128)S(1)} %convolution_bitcast_fusion), channel_id=1, replica_groups=mesh['oy'=8,'oc'=2,'virt'=12,'rep'=4] {'rep'}, dimensions={0} | all-to-all | bytes 524288 | tf_op jit(solution)/shard_map/all_to_all | solution.py:42
  97.5 0.6 reduce_sum.9
  (4 shorter events, 0.0 us)
Async XLA Ops:
  6.5 19.2 %copy-start = (bf16[240,256]{1,0:T(8,128)(2,1)S(1)}, bf16[240,256]{1,0:T(8,128)(2,1)}, u32[]{:S(2)}) copy-start(bf16[240,256]{1,0:T(8,128)(2,1)} %param.5) | copy-start | bytes 368644
  6.5 19.2 %copy-start.2 = (s32[240]{0:T(256)S(1)}, s32[240]{0:T(256)}, u32[]{:S(2)}) copy-start(s32[240]{0:T(256)} %param.6) | copy-start | bytes 2884
  6.5 19.2 %copy-start.1 = (s32[256]{0:T(256)S(1)}, s32[256]{0:T(256)}, u32[]{:S(2)}) copy-start(s32[256]{0:T(256)} %param.7) | copy-start | bytes 3076
  6.5 79.3 %all-gather.3.cloned.1.call-start = ((), (), s32[]{:S(2)}) async-start(), calls=%async_computation.5 | async-start | bytes 2555904 | tf_op jit(solution)/shard_map/all_gather | solution.py:24
  26.7 9.5 %all-to-all-start.1 = ((bf16[4,80,256]{2,1,0:T(8,128)(2,1)}), bf16[4,80,256]{2,1,0:T(8,128)(2,1)S(1)}, u32[]{:S(2)}, u32[]{:S(2)}) async-start(bf16[4,80,256]{2,1,0:T(8,128)(2,1)} %fusion.2), calls=%async_computation.1 | async-start | bytes 327680 | tf_op jit(solution)/shard_map/all_to_all | solution.py:30
Sparse Core Ops, SparseCore 0:
  25.8 59.9 all-gather.2

commit v5 on v4

--- a/solution.py
+++ b/solution.py
@@ -21,7 +21,10 @@
     a = lax.all_to_all(a, "rep", split_axis=0, concat_axis=0, tiled=True)
     a = a.reshape(n_rep * rows, (per_v // n_rep) * atom)
     a, integrals, cd_irrep, ab_irrep = lax.optimization_barrier((a, integrals, cd_irrep, ab_irrep))
-    a = lax.all_gather(a, "virt", axis=0, tiled=False)
+    h = a.shape[0] // 2
+    a1 = lax.all_gather(a[:h], "virt", axis=0, tiled=False)
+    a1, a_rest = lax.optimization_barrier((a1, a[h:]))
+    a2 = lax.all_gather(a_rest, "virt", axis=0, tiled=False)
 
     masked = jnp.where(cd_irrep[:, None] == ab_irrep[None, :], integrals, jnp.zeros_like(integrals))
     b = masked.reshape(per_k, atom, nb)
@@ -35,9 +38,11 @@
     b = lax.all_to_all(b, "oy", split_axis=0, concat_axis=0, tiled=True)
     b = jnp.broadcast_to(b[None], (n_oc,) + b.shape)
     b = lax.all_to_all(b, "oc", split_axis=0, concat_axis=0, tiled=True)
-    b = jnp.moveaxis(b, 0, 1).reshape(a.shape[0], a.shape[2], nb)
+    b = jnp.moveaxis(b, 0, 1).reshape(a1.shape[0], a1.shape[2], nb)
 
-    partial_sum = jnp.einsum("vmc,vcn->mn", a, b, preferred_element_type=jnp.float32)
+    partial_sum = jnp.concatenate([
+        jnp.einsum("vmc,vcn->mn", a1, b, preferred_element_type=jnp.float32),
+        jnp.einsum("vmc,vcn->mn", a2, b, preferred_element_type=jnp.float32)], axis=0)
     partial_sum = partial_sum.reshape(n_rep, rows, nb)
     partial_sum = lax.all_to_all(partial_sum, "rep", split_axis=0, concat_axis=0, tiled=True)
     return jnp.sum(partial_sum, axis=0)

time: 107 us -> 118 us (1.10)
  the two profiles are of different devices: /device:TPU:6 before, /device:TPU:8 now
where the time goes in v5:
time: 118 us; the launch traced here: 117 us
  blocking collectives  77.7 us (66%)
  starting transfers between devices  19.8 us (17%)
  waiting for transfers between devices  12.4 us (11%)
  local copies, waits for them, and re-layouts  3.63 us (3%)
  other arithmetic  2.55 us (2%)
    all_gather x1, blocking collectives, local(): a1 = lax.all_gather(a[:h], 'virt', axis=0, tiled=False)  34.2 us
    all_gather x1, blocking collectives, local(): a2 = lax.all_gather(a_rest, 'virt', axis=0, tiled=False)  28.6 us
    all_to_all x1, starting transfers between devices, local(): b = lax.all_to_all(b, 'oy', split_axis=0, concat_axis=0, tiled=True)  12.1 us
    all_to_all x1, blocking collectives, local(): lax.all_to_all(partial_sum, 'rep', split_axis=0, concat_axis=0, tiled=True)  9.64 us
    all_to_all x1, waiting for transfers between devices, local(): a = lax.all_to_all(a, 'rep', split_axis=0, concat_axis=0, tiled=True)  6.33 us
    all_to_all x1, waiting for transfers between devices, local(): b = lax.all_to_all(b, 'rep', split_axis=0, concat_axis=0, tiled=True)  6.09 us
    all_to_all x1, blocking collectives, local(): b = lax.all_to_all(b, 'oc', split_axis=0, concat_axis=0, tiled=True)  5.31 us
    all_to_all x1, starting transfers between devices, local(): a = lax.all_to_all(a, 'rep', split_axis=0, concat_axis=0, tiled=True)  4.29 us
  transfers between devices with their start and end apart: 3, of which 2 were waited for; matrix products, arithmetic and copies ran while one was open for 0% of the time, Pallas kernels for 0%

profile of v5, /device:TPU:8, one launch (start us, length us, event | category | flops | bytes accessed | tf_op | source)
XLA Modules:
  0.0 117.1 jit_solution(3398378489119301668)
XLA Ops:
  0.0 1.3 %reshape.26 = bf16[64,4,4,80]{3,2,1,0:T(4,128)(2,1)S(1)} reshape(bf16[64,1280]{1,0:T(8,128)(2,1)} %param.4) | data formatting | bytes 327680 | tf_op jit(solution)/shard_map/reshape | solution.py:19
  1.3 0.1 copy.15
  1.4 0.9 reshape.27
  2.3 4.3 %all-to-all-start = ((bf16[4,64,320]{2,1,0:T(8,128)(2,1)}), bf16[4,64,320]{2,1,0:T(8,128)(2,1)S(1)}, u32[]{:S(2)}, u32[]{:S(2)}) async-start(bf16[4,64,320]{2,1,0:T(8,128)(2,1)} %reshape.27), calls=%async_computation | async-start | bytes 393216 | tf_op jit(solution)/shard_map/all_to_all | solution.py:21
  6.6 6.3 %all-to-all-done = bf16[4,64,320]{2,1,0:T(8,128)(2,1)S(1)} async-done(((bf16[4,64,320]{2,1,0:T(8,128)(2,1)}), bf16[4,64,320]{2,1,0:T(8,128)(2,1)S(1)}, u32[]{:S(2)}, u32[]{:S(2)}) %all-to-all-start) | async-done | bytes 163872 | tf_op jit(solution)/shard_map/all_to_all | solution.py:21
  12.9 1.0 compare_select_fusion
  13.9 0.8 fusion.2
  14.7 3.3 %all-to-all-start.1 = ((bf16[4,80,256]{2,1,0:T(8,128)(2,1)}), bf16[4,80,256]{2,1,0:T(8,128)(2,1)S(1)}, u32[]{:S(2)}, u32[]{:S(2)}) async-start(bf16[4,80,256]{2,1,0:T(8,128)(2,1)} %fusion.2), calls=%async_computation.1 | async-start | bytes 327680 | tf_op jit(solution)/shard_map/all_to_all | solution.py:33
  18.1 6.1 %all-to-all-done.1 = bf16[4,80,256]{2,1,0:T(8,128)(2,1)S(1)} async-done(((bf16[4,80,256]{2,1,0:T(8,128)(2,1)}), bf16[4,80,256]{2,1,0:T(8,128)(2,1)S(1)}, u32[]{:S(2)}, u32[]{:S(2)}) %all-to-all-start.1) | async-done | bytes 163872 | tf_op jit(solution)/shard_map/all_to_all | solution.py:33
  24.2 0.1 slice_select_fusion
  24.3 1.0 broadcast_in_dim.32
  25.3 12.1 %all-to-all-start.2 = ((bf16[8,3,80,256]{3,2,1,0:T(8,128)(2,1)}), bf16[8,3,80,256]{3,2,1,0:T(8,128)(2,1)S(1)}, u32[]{:S(2)}, u32[]{:S(2)}) async-start(bf16[8,3,80,256]{3,2,1,0:T(8,128)(2,1)} %broadcast_in_dim.32), calls=%async_computation.2 | async-start | bytes 1966080 | tf_op jit(solution)/shard_map/all_to_all | solution.py:38
  37.4 34.2 %all-gather = bf16[1536,320]{1,0:T(8,128)(2,1)S(1)} all-gather(bf16[128,320]{1,0:T(8,128)(2,1)S(1)} %get-tuple-element.18), channel_id=2, replica_groups=mesh['oy'=8,'oc'=2,'virt'=12,'rep'=4] {'virt'}, dimensions={0}, use_global_device_ids=true | all-gather | bytes 1064960 | tf_op jit(solution)/shard_map/all_gather | solution.py:25
  71.6 28.6 %all-gather.1 = bf16[1536,320]{1,0:T(8,128)(2,1)S(1)} all-gather(bf16[128,320]{1,0:T(8,128)(2,1)S(1)} %get-tuple-element.16), channel_id=3, replica_groups=mesh['oy'=8,'oc'=2,'virt'=12,'rep'=4] {'virt'}, dimensions={0}, use_global_device_ids=true | all-gather | bytes 1064960 | tf_op jit(solution)/shard_map/all_gather | solution.py:27
  100.2 0.0 all-to-all-done.2
  100.2 0.1 broadcast_in_dim.33
  100.3 5.3 %all_to_all.25 = bf16[2,8,3,80,256]{4,3,2,1,0:T(8,128)(2,1)S(1)} all-to-all(bf16[2,8,3,80,256]{4,3,2,1,0:T(8,128)(2,1)S(1)} %broadcast_in_dim.33), channel_id=1, replica_groups=mesh['oy'=8,'oc'=2,'virt'=12,'rep'=4] {'oc'}, dimensions={0} | all-to-all | bytes 3932160 | tf_op jit(solution)/shard_map/all_to_all | solution.py:40
  105.6 0.2 copy.9
  105.8 0.5 convolution_bitcast_fusion.1
  106.3 0.5 convolution_bitcast_fusion
  106.8 9.6 %all_to_all.26 = f32[4,64,256]{2,1,0:T(8,128)S(1)} all-to-all(f32[4,64,256]{2,1,0:T(8,128)S(1)} %bitcast.24), channel_id=1, replica_groups=mesh['oy'=8,'oc'=2,'virt'=12,'rep'=4] {'rep'}, dimensions={0} | all-to-all | bytes 524288 | tf_op jit(solution)/shard_map/all_to_all | solution.py:47
  116.5 0.6 reduce_sum.9
  (4 shorter events, 0.1 us)
Async XLA Ops:
  2.3 10.6 %all-to-all-start = ((bf16[4,64,320]{2,1,0:T(8,128)(2,1)}), bf16[4,64,320]{2,1,0:T(8,128)(2,1)S(1)}, u32[]{:S(2)}, u32[]{:S(2)}) async-start(bf16[4,64,320]{2,1,0:T(8,128)(2,1)} %reshape.27), calls=%async_computation | async-start | bytes 393216 | tf_op jit(solution)/shard_map/all_to_all | solution.py:21
  14.7 9.5 %all-to-all-start.1 = ((bf16[4,80,256]{2,1,0:T(8,128)(2,1)}), bf16[4,80,256]{2,1,0:T(8,128)(2,1)S(1)}, u32[]{:S(2)}, u32[]{:S(2)}) async-start(bf16[4,80,256]{2,1,0:T(8,128)(2,1)} %fusion.2), calls=%async_computation.1 | async-start | bytes 327680 | tf_op jit(solution)/shard_map/all_to_all | solution.py:33
  25.3 74.9 %all-to-all-start.2 = ((bf16[8,3,80,256]{3,2,1,0:T(8,128)(2,1)}), bf16[8,3,80,256]{3,2,1,0:T(8,128)(2,1)S(1)}, u32[]{:S(2)}, u32[]{:S(2)}) async-start(bf16[8,3,80,256]{3,2,1,0:T(8,128)(2,1)} %broadcast_in_dim.32), calls=%async_computation.2 | async-start | bytes 1966080 | tf_op jit(solution)/shard_map/all_to_all | solution.py:38

commit v6 on v4

--- a/solution.py
+++ b/solution.py
@@ -37,10 +37,15 @@
     b = lax.all_to_all(b, "oc", split_axis=0, concat_axis=0, tiled=True)
     b = jnp.moveaxis(b, 0, 1).reshape(a.shape[0], a.shape[2], nb)
 
-    partial_sum = jnp.einsum("vmc,vcn->mn", a, b, preferred_element_type=jnp.float32)
-    partial_sum = partial_sum.reshape(n_rep, rows, nb)
-    partial_sum = lax.all_to_all(partial_sum, "rep", split_axis=0, concat_axis=0, tiled=True)
-    return jnp.sum(partial_sum, axis=0)
+    a = a.reshape(a.shape[0], n_rep, rows, a.shape[2])
+    def part(g):
+        rows_g = lax.dynamic_index_in_dim(a, g, axis=1, keepdims=False)
+        return jnp.einsum("vmc,vcn->mn", rows_g, b, preferred_element_type=jnp.float32)
+    total = None
+    for s in range(1, n_rep):
+        sent = lax.ppermute(part((r + s) % n_rep), "rep", [(j, (j + s) % n_rep) for j in range(n_rep)])
+        total = sent if total is None else total + sent
+    return total + part(r)
 
 
 def solution(mesh):

time: 107 us -> 113 us (1.056); the launches traced: 105 us -> 112 us
  blocking collectives: 55.1 us -> 22.8 us
  waiting for transfers between devices: 24.9 us -> 48.9 us
  starting transfers between devices: 5.39 us -> 18.2 us
  matrix products: 2.37 us -> 4.7 us
    all_to_all x2 -> x0, blocking collectives: 32.3 us -> none  [the longest x1 23.1 us: local(): b = lax.all_to_all(b, 'oy', split_axis=0, concat_axis=0, tiled=True)]
    all_to_all x0 -> x1, waiting for transfers between devices: none -> 19.7 us  [local(): b = lax.all_to_all(b, 'oy', split_axis=0, concat_axis=0, tiled=True)]
    ppermute x0 -> x3, starting transfers between devices: none -> 9.28 us  [local(): lax.ppermute(part((r + s) % n_rep), 'rep', [(j, (j + s) % n_rep) for j in...]
    ppermute x0 -> x3, waiting for transfers between devices: none -> 5.43 us  [local(): lax.ppermute(part((r + s) % n_rep), 'rep', [(j, (j + s) % n_rep) for j in...]
    all_to_all x0 -> x1, starting transfers between devices: none -> 3.55 us  [local(): b = lax.all_to_all(b, 'oy', split_axis=0, concat_axis=0, tiled=True)]
    dot_general x1 -> x4, matrix products: 2.37 us -> 4.7 us  [part(): jnp.einsum('vmc,vcn->mn', rows_g, b, preferred_element_type=jnp.float32)]
    all_gather x1, waiting for transfers between devices: 20.8 us -> 19.7 us  [local(): a = lax.all_gather(a, 'virt', axis=0, tiled=False)]
  transfers between devices with their start and end apart: 2 -> 6, of which waited for: 2 -> 4; matrix products, arithmetic and copies ran while one was open for 1% -> 3% of each run, Pallas kernels for 0% -> 0%
where the time goes in v6:
time: 113 us; the launch traced here: 112 us
  waiting for transfers between devices  48.9 us (43%)
  blocking collectives  22.8 us (20%)
  starting transfers between devices  18.2 us (16%)
  between operations  13.6 us (12%)
  matrix products  4.7 us (4%)
  local copies, waits for them, and re-layouts  2.98 us (3%)
    all_to_all x1, waiting for transfers between devices, local(): b = lax.all_to_all(b, 'oy', split_axis=0, concat_axis=0, tiled=True)  19.7 us
    all_gather x1, waiting for transfers between devices, local(): a = lax.all_gather(a, 'virt', axis=0, tiled=False)  19.7 us
    all_to_all x1, blocking collectives, local(): a = lax.all_to_all(a, 'rep', split_axis=0, concat_axis=0, tiled=True)  17.5 us
    ppermute x3, starting transfers between devices, local(): lax.ppermute(part((r + s) % n_rep), 'rep', [(j, (j + s) % n_rep) for j in...  9.28 us
    ppermute x3, waiting for transfers between devices, local(): lax.ppermute(part((r + s) % n_rep), 'rep', [(j, (j + s) % n_rep) for j in...  5.43 us
    all_to_all x1, starting transfers between devices, local(): b = lax.all_to_all(b, 'rep', split_axis=0, concat_axis=0, tiled=True)  5.39 us
    all_to_all x1, blocking collectives, local(): b = lax.all_to_all(b, 'oc', split_axis=0, concat_axis=0, tiled=True)  5.31 us
    dot_general x4, matrix products, part(): jnp.einsum('vmc,vcn->mn', rows_g, b, preferred_element_type=jnp.float32)  4.7 us
  transfers between devices with their start and end apart: 6, of which 4 were waited for; matrix products, arithmetic and copies ran while one was open for 3% of the time, Pallas kernels for 0%

profile of v6, /device:TPU:6, one launch (start us, length us, event | category | flops | bytes accessed | tf_op | source)
XLA Modules:
  0.0 112.2 jit_solution(7610456009231369763)
XLA Ops:
  6.5 1.3 %reshape.26 = bf16[64,4,4,80]{3,2,1,0:T(4,128)(2,1)S(1)} reshape(bf16[64,1280]{1,0:T(8,128)(2,1)} %param.4) | data formatting | bytes 327680 | tf_op jit(solution)/shard_map/reshape | solution.py:19
  7.9 0.1 copy.9
  8.0 0.2 reshape.27
  8.2 17.5 %all_to_all.20 = bf16[4,64,320]{2,1,0:T(8,128)(2,1)} all-to-all(bf16[4,64,320]{2,1,0:T(8,128)(2,1)S(1)} %reshape.27), channel_id=1, replica_groups=mesh['oy'=8,'oc'=2,'virt'=12,'rep'=4] {'rep'}, dimensions={0} | all-to-all | bytes 327680 | tf_op jit(solution)/shard_map/all_to_all | solution.py:21
  25.8 0.1 compare_select_fusion
  25.9 0.8 fusion.10
  26.7 5.4 %all-to-all-start.1 = ((bf16[4,80,256]{2,1,0:T(8,128)(2,1)}), bf16[4,80,256]{2,1,0:T(8,128)(2,1)S(1)}, u32[]{:S(2)}, u32[]{:S(2)}) async-start(bf16[4,80,256]{2,1,0:T(8,128)(2,1)} %fusion.10), calls=%async_computation.1 | async-start | bytes 327680 | tf_op jit(solution)/shard_map/all_to_all | solution.py:30
  32.1 4.1 %all-to-all-done.1 = bf16[4,80,256]{2,1,0:T(8,128)(2,1)S(1)} async-done(((bf16[4,80,256]{2,1,0:T(8,128)(2,1)}), bf16[4,80,256]{2,1,0:T(8,128)(2,1)S(1)}, u32[]{:S(2)}, u32[]{:S(2)}) %all-to-all-start.1) | async-done | bytes 163872 | tf_op jit(solution)/shard_map/all_to_all | solution.py:30
  36.1 0.1 slice_select_fusion
  36.2 1.0 broadcast_in_dim.32
  37.3 3.6 %all-to-all-start.2 = ((bf16[8,3,80,256]{3,2,1,0:T(8,128)(2,1)}), bf16[8,3,80,256]{3,2,1,0:T(8,128)(2,1)S(1)}, u32[]{:S(2)}, u32[]{:S(2)}) async-start(bf16[8,3,80,256]{3,2,1,0:T(8,128)(2,1)} %broadcast_in_dim.32), calls=%async_computation.2 | async-start | bytes 1966080 | tf_op jit(solution)/shard_map/all_to_all | solution.py:35
  40.9 19.7 %all-to-all-done.2 = bf16[8,3,80,256]{3,2,1,0:T(8,128)(2,1)S(1)} async-done(((bf16[8,3,80,256]{3,2,1,0:T(8,128)(2,1)}), bf16[8,3,80,256]{3,2,1,0:T(8,128)(2,1)S(1)}, u32[]{:S(2)}, u32[]{:S(2)}) %all-to-all-start.2) | async-done | bytes 983072 | tf_op jit(solution)/shard_map/all_to_all | solution.py:35
  60.6 0.1 broadcast_in_dim.33
  60.7 5.3 %all_to_all.21 = bf16[2,8,3,80,256]{4,3,2,1,0:T(8,128)(2,1)S(1)} all-to-all(bf16[2,8,3,80,256]{4,3,2,1,0:T(8,128)(2,1)S(1)} %broadcast_in_dim.33), channel_id=1, replica_groups=mesh['oy'=8,'oc'=2,'virt'=12,'rep'=4] {'oc'}, dimensions={0} | all-to-all | bytes 3932160 | tf_op jit(solution)/shard_map/all_to_all | solution.py:37
  66.0 0.2 copy.7
  66.2 19.7 %all-gather.3.cloned.1.call-done = bf16[3072,320]{1,0:T(8,128)(2,1)} async-done(((bf16[256,320]{1,0:T(8,128)(2,1)}), bf16[3072,320]{1,0:T(8,128)(2,1)}) %all-gather.3.cloned.1.call-update) | async-done | bytes 1966096 | tf_op jit(solution)/shard_map/all_gather | solution.py:24
  85.8 1.7 %convolution_bitcast_fusion.2 = f32[64,256]{1,0:T(8,128)S(1)} fusion(bf16[12,320,256]{2,1,0:T(8,128)(2,1)S(1)} %bitcast.36, bf16[12,4,64,320]{3,2,1,0:T(8,128)(2,1)} %bitcast.41, s32[]{:T(128)S(6)} %select_n.50), kind=kOutput, calls=%fused_computation.2 | convolution fusion | flops 125829120 | bytes 2621444 | tf_op jit(solution)/shard_map/vmc,vcn->mn/dot_general | solution.py:43
  87.5 3.4 %collective-permute-start.1 = (f32[64,256]{1,0:T(8,128)S(1)}, f32[64,256]{1,0:T(8,128)S(1)}, u32[]{:S(2)}, u32[]{:S(2)}) collective-permute-start(f32[64,256]{1,0:T(8,128)S(1)} %convolution_bitcast_fusion.2), channel_id=1, source_target_pairs={{0,2},{1,3},{2,0},{3,1},{4,6},{5,7},{6,4},{7,5},{8,10},{9,11},{10,... | collective-permute-start | bytes 196616 | tf_op jit(solution)/shard_map/ppermute | solution.py:46
  90.9 0.4 convolution_bitcast_fusion.3
  91.3 4.0 %collective-permute-start = (f32[64,256]{1,0:T(8,128)S(1)}, f32[64,256]{1,0:T(8,128)S(1)}, u32[]{:S(2)}, u32[]{:S(2)}) collective-permute-start(f32[64,256]{1,0:T(8,128)S(1)} %convolution_bitcast_fusion.3), channel_id=1, source_target_pairs={{0,1},{1,2},{2,3},{3,0},{4,5},{5,6},{6,7},{7,4},{8,9},{9,10},{10,1... | collective-permute-start | bytes 196616 | tf_op jit(solution)/shard_map/ppermute | solution.py:46
  95.3 0.4 convolution_bitcast_fusion.1
  95.8 1.9 %collective-permute-start.2 = (f32[64,256]{1,0:T(8,128)S(1)}, f32[64,256]{1,0:T(8,128)S(1)}, u32[]{:S(2)}, u32[]{:S(2)}) collective-permute-start(f32[64,256]{1,0:T(8,128)S(1)} %convolution_bitcast_fusion.1), channel_id=1, source_target_pairs={{0,3},{1,0},{2,1},{3,2},{4,7},{5,4},{6,5},{7,6},{8,11},{9,8},{10,9... | collective-permute-start | bytes 196616 | tf_op jit(solution)/shard_map/ppermute | solution.py:46
  97.7 5.4 %collective-permute-done.2 = f32[64,256]{1,0:T(8,128)S(1)} collective-permute-done((f32[64,256]{1,0:T(8,128)S(1)}, f32[64,256]{1,0:T(8,128)S(1)}, u32[]{:S(2)}, u32[]{:S(2)}) %collective-permute-start.2) | collective-permute-done | bytes 65568 | tf_op jit(solution)/shard_map/ppermute | solution.py:46
  103.2 2.2 %add_add_fusion = f32[64,256]{1,0:T(8,128)} fusion(f32[64,256]{1,0:T(8,128)S(1)} %collective-permute-done.2, f32[64,256]{1,0:T(8,128)S(1)} %collective-permute-done, f32[64,256]{1,0:T(8,128)S(1)} %collective-permute-done.1, bf16[12,320,256]{2,1,0:T(8,128)(2,1)S(1)} %bitcast.39, bf16[12,4,64,320]{3,2,1,0:T(8,128)(2,1)} %bitcast.42, s32[]{:T(128)S(6)} %select_n.53), kind=kOutput, calls=%fused_computation.22 | convolution fusion | flops 125878272 | bytes 2818052 | tf_op jit(solution)/shard_map/vmc,vcn->mn/dot_general | solution.py:43
  (14 shorter events, 0.1 us)
Async XLA Ops:
  6.5 19.2 %copy-start.1 = (bf16[240,256]{1,0:T(8,128)(2,1)S(1)}, bf16[240,256]{1,0:T(8,128)(2,1)}, u32[]{:S(2)}) copy-start(bf16[240,256]{1,0:T(8,128)(2,1)} %param.5) | copy-start | bytes 368644
  6.5 19.2 %copy-start.3 = (s32[240]{0:T(256)S(1)}, s32[240]{0:T(256)}, u32[]{:S(2)}) copy-start(s32[240]{0:T(256)} %param.6) | copy-start | bytes 2884
  6.5 19.2 %copy-start.2 = (s32[256]{0:T(256)S(1)}, s32[256]{0:T(256)}, u32[]{:S(2)}) copy-start(s32[256]{0:T(256)} %param.7) | copy-start | bytes 3076
  6.5 79.3 %all-gather.3.cloned.1.call-start = ((), (), s32[]{:S(2)}) async-start(), calls=%async_computation.4 | async-start | bytes 2555904 | tf_op jit(solution)/shard_map/all_gather | solution.py:24
  26.7 9.5 %all-to-all-start.1 = ((bf16[4,80,256]{2,1,0:T(8,128)(2,1)}), bf16[4,80,256]{2,1,0:T(8,128)(2,1)S(1)}, u32[]{:S(2)}, u32[]{:S(2)}) async-start(bf16[4,80,256]{2,1,0:T(8,128)(2,1)} %fusion.10), calls=%async_computation.1 | async-start | bytes 327680 | tf_op jit(solution)/shard_map/all_to_all | solution.py:30
  37.3 23.3 %all-to-all-start.2 = ((bf16[8,3,80,256]{3,2,1,0:T(8,128)(2,1)}), bf16[8,3,80,256]{3,2,1,0:T(8,128)(2,1)S(1)}, u32[]{:S(2)}, u32[]{:S(2)}) async-start(bf16[8,3,80,256]{3,2,1,0:T(8,128)(2,1)} %broadcast_in_dim.32), calls=%async_computation.2 | async-start | bytes 1966080 | tf_op jit(solution)/shard_map/all_to_all | solution.py:35
  85.8 5.0 %copy-start = (bf16[3072,320]{1,0:T(8,128)(2,1)S(1)}, bf16[3072,320]{1,0:T(8,128)(2,1)}, u32[]{:S(2)}) copy-start(bf16[3072,320]{1,0:T(8,128)(2,1)} %all-gather.3.cloned.1.call-done) | copy-start | bytes 5898244
  87.5 10.2 %collective-permute-start.1 = (f32[64,256]{1,0:T(8,128)S(1)}, f32[64,256]{1,0:T(8,128)S(1)}, u32[]{:S(2)}, u32[]{:S(2)}) collective-permute-start(f32[64,256]{1,0:T(8,128)S(1)} %convolution_bitcast_fusion.2), channel_id=1, source_target_pairs={{0,2},{1,3},{2,0},{3,1},{4,6},{5,7},{6,4},{7,5},{8,10},{9,11},{10,... | collective-permute-start | bytes 196616 | tf_op jit(solution)/shard_map/ppermute | solution.py:46
  91.3 6.4 %collective-permute-start = (f32[64,256]{1,0:T(8,128)S(1)}, f32[64,256]{1,0:T(8,128)S(1)}, u32[]{:S(2)}, u32[]{:S(2)}) collective-permute-start(f32[64,256]{1,0:T(8,128)S(1)} %convolution_bitcast_fusion.3), channel_id=1, source_target_pairs={{0,1},{1,2},{2,3},{3,0},{4,5},{5,6},{6,7},{7,4},{8,9},{9,10},{10,1... | collective-permute-start | bytes 196616 | tf_op jit(solution)/shard_map/ppermute | solution.py:46
  95.8 7.4 %collective-permute-start.2 = (f32[64,256]{1,0:T(8,128)S(1)}, f32[64,256]{1,0:T(8,128)S(1)}, u32[]{:S(2)}, u32[]{:S(2)}) collective-permute-start(f32[64,256]{1,0:T(8,128)S(1)} %convolution_bitcast_fusion.1), channel_id=1, source_target_pairs={{0,3},{1,0},{2,1},{3,2},{4,7},{5,4},{6,5},{7,6},{8,11},{9,8},{10,9... | collective-permute-start | bytes 196616 | tf_op jit(solution)/shard_map/ppermute | solution.py:46
Sparse Core Ops, SparseCore 0:
  25.9 59.9 all-gather.2

commit v7 on v4

v7 whole, which is shorter than its diff:
```python
import math

import jax
import jax.numpy as jnp
from jax import lax
from jax.sharding import Mesh
from jax.sharding import PartitionSpec as P


def local(amplitudes, integrals, cd_irrep, ab_irrep, n_rep, n_virt, n_oy, n_oc):
    rows, cols = amplitudes.shape
    kb, nb = integrals.shape
    atom = math.gcd(cols, kb)
    per_v = cols // atom
    per_k = kb // atom
    assert per_v % n_rep == 0 and per_k == n_rep - 1
    r = lax.axis_index("rep")
    v = lax.axis_index("virt")

    a = amplitudes.reshape(rows, per_v // n_rep, n_rep, atom)
    a = jnp.transpose(a, (2, 0, 1, 3)).reshape(n_rep, rows, (per_v // n_rep) * atom)
    masked = jnp.where(cd_irrep[:, None] == ab_irrep[None, :], integrals, jnp.zeros_like(integrals))
    b = masked.reshape(per_k, atom, nb)
    b = jnp.concatenate([b, jnp.zeros((n_rep - per_k, atom, nb), b.dtype)], axis=0)
    b = lax.dynamic_slice_in_dim(jnp.concatenate([b, b], axis=0), r, n_rep, axis=0)
    na = a[0].size
    both = jnp.concatenate([a.reshape(n_rep, -1), b.reshape(n_rep, -1)], axis=1)
    both = lax.all_to_all(both, "rep", split_axis=0, concat_axis=0, tiled=True)
    a = both[:, :na].reshape(n_rep * rows, (per_v // n_rep) * atom)
    b = both[:, na:].reshape(n_rep, atom, nb)

    q = (n_rep - 1 - r) % n_rep
    skip = (jnp.arange(per_k) >= q)[:, None, None]
    b = jnp.where(skip, b[1:], b[:-1])
    b = jnp.broadcast_to(b[None], (n_oy * n_oc,) + b.shape)
    b = lax.all_to_all(b, ("oy", "oc"), split_axis=0, concat_axis=0, tiled=True)
    b = b.reshape(n_virt, -1, nb)
    b = lax.dynamic_slice_in_dim(jnp.concatenate([b, b], axis=0), v, n_virt, axis=0)

    fwd = [(i, (i + 1) % n_virt) for i in range(n_virt)]
    bwd = [(i, (i - 1) % n_virt) for i in range(n_virt)]
    ahead, behind = [], []
    f, g = a, a
    for s in range(1, n_virt // 2 + 1):
        f = lax.ppermute(f, "virt", fwd)
        behind.append(f)
        if s < n_virt - s:
            g = lax.ppermute(g, "virt", bwd)
            ahead.append(g)
    pieces = [a] + ahead + behind[::-1]
    a = jnp.stack(pieces, axis=0)

    partial_sum = jnp.einsum("vmc,vcn->mn", a, b, preferred_element_type=jnp.float32)
    partial_sum = partial_sum.reshape(n_rep, rows, nb)
    partial_sum = lax.all_to_all(partial_sum, "rep", split_axis=0, concat_axis=0, tiled=True)
    return jnp.sum(partial_sum, axis=0)


def solution(mesh):
    n_occ, n_virt, n_rep = mesh.shape["occ"], mesh.shape["virt"], mesh.shape["rep"]
    n_oc = 2 if n_occ % 2 == 0 else 1
    n_oy = n_occ // n_oc
    fine = Mesh(mesh.devices.reshape(n_oy, n_oc, n_virt, n_rep), ("oy", "oc", "virt", "rep"))
    rows_spec = ("oy", "oc", "rep")
    in_specs = (P(rows_spec, "virt"), P(rows_spec, "virt"), P(rows_spec), P("virt"))
    out_specs = P(rows_spec, "virt")

    def body(amplitudes, integrals, cd_irrep, ab_irrep):
        return local(amplitudes, integrals, cd_irrep, ab_irrep, n_rep, n_virt, n_oy, n_oc)

    return jax.shard_map(body, mesh=fine, in_specs=in_specs, out_specs=out_specs, check_vma=False)
```

time: 107 us -> 106 us (level)
  starting transfers between devices: 5.39 us -> 58.9 us
  blocking collectives: 55.1 us -> 9.06 us
  between operations: 13.5 us -> 0.29 us
  local copies, waits for them, and re-layouts: 2.01 us -> 14.7 us
  waiting for transfers between devices: 24.9 us -> 15.8 us
  other arithmetic: 1.61 us -> 3.08 us
    all_to_all x3 -> x0, blocking collectives: 45.9 us -> none  [the longest x1 23.1 us: local(): b = lax.all_to_all(b, 'oy', split_axis=0, concat_axis=0, tiled=True)]
    ppermute x0 -> x11, starting transfers between devices: none -> 42.3 us  [the longest x5 30.8 us: local(): g = lax.ppermute(g, 'virt', bwd)]
    all_gather x1 -> x0, waiting for transfers between devices: 20.8 us -> none  [local(): a = lax.all_gather(a, 'virt', axis=0, tiled=False)]
    all_to_all x1 -> x2, starting transfers between devices: 5.39 us -> 16.6 us  [the longest x1 12.9 us: local(): both = lax.all_to_all(both, 'rep', split_axis=0, concat_axis=0, tiled=True)]
    ppermute x0 -> x11, waiting for transfers between devices: none -> 10.9 us  [the longest x6 10.9 us: local(): f = lax.ppermute(f, 'virt', fwd)]
    unnamed x6 -> x15, local copies, waits for them, and re-layouts: 0.01 us -> 9.38 us
    another operation x0 -> x4, local copies, waits for them, and re-layouts: none -> 1.44 us  [the longest x3 1.01 us: local(): a = jnp.stack(pieces, axis=0)]
    broadcast_in_dim x2 -> x1, local copies, waits for them, and re-layouts: 0.2 us -> 1.43 us  [local(): b = jnp.broadcast_to(b[None], (n_oy * n_oc,) + b.shape)]
  transfers between devices with their start and end apart: 2 -> 13, of which waited for: 2 -> 7; matrix products, arithmetic and copies ran while one was open for 1% -> 8% of each run, Pallas kernels for 0% -> 0%
where the time goes in v7:
time: 106 us; the launch traced here: 104 us
  starting transfers between devices  58.9 us (56%)
  waiting for transfers between devices  15.8 us (15%)
  local copies, waits for them, and re-layouts  14.7 us (14%)
  blocking collectives  9.06 us (9%)
  other arithmetic  3.08 us (3%)
  matrix products  2.54 us (2%)
    ppermute x5, starting transfers between devices, local(): g = lax.ppermute(g, 'virt', bwd)  30.8 us
    all_to_all x1, starting transfers between devices, local(): both = lax.all_to_all(both, 'rep', split_axis=0, concat_axis=0, tiled=True)  12.9 us
    ppermute x6, starting transfers between devices, local(): f = lax.ppermute(f, 'virt', fwd)  11.5 us
    ppermute x6, waiting for transfers between devices, local(): f = lax.ppermute(f, 'virt', fwd)  10.9 us
    unnamed x15, local copies, waits for them, and re-layouts  9.38 us
    all_to_all x1, blocking collectives, local(): lax.all_to_all(partial_sum, 'rep', split_axis=0, concat_axis=0, tiled=True)  9.06 us
    all_to_all x1, waiting for transfers between devices, local(): both = lax.all_to_all(both, 'rep', split_axis=0, concat_axis=0, tiled=True)  4.95 us
    all_to_all x1, starting transfers between devices, local(): b = lax.all_to_all(b, ('oy', 'oc'), split_axis=0, concat_axis=0, tiled=True)  3.72 us
  transfers between devices with their start and end apart: 13, of which 7 were waited for; matrix products, arithmetic and copies ran while one was open for 8% of the time, Pallas kernels for 0%

profile of v7, /device:TPU:6, one launch (start us, length us, event | category | flops | bytes accessed | tf_op | source)
XLA Modules:
  0.0 104.4 jit_solution(3945251287084186295)
XLA Ops:
  0.0 1.0 compare_select_fusion
  1.3 1.3 %reshape.38 = bf16[64,4,4,80]{3,2,1,0:T(4,128)(2,1)S(1)} reshape(bf16[64,1280]{1,0:T(8,128)(2,1)} %param.4) | data formatting | bytes 327680 | tf_op jit(solution)/shard_map/reshape | solution.py:20
  3.8 1.1 %reduce = bf16[4,40960]{1,0:T(4,128)(2,1)S(1)} reduce(bf16[4,1,40960]{2,0,1:T(4,128)(2,1)S(1)} %maximum_bitcast_fusion, bf16[]{:T(256)} %broadcast.11), dimensions={1}, to_apply=%copy.15.reduce_sub_computation | reduce | bytes 655362 | tf_op jit(solution)/shard_map/all_to_all | solution.py:28
  4.8 1.1 %reshape.45 = bf16[4,2,20480]{2,1,0:T(2,128)(2,1)} reshape(bf16[4,40960]{1,0:T(4,128)(2,1)S(1)} %reduce) | data formatting | bytes 655360
  5.9 12.9 %all-to-all-start = ((bf16[4,2,20480]{2,1,0:T(2,128)(2,1)}), bf16[4,2,20480]{2,1,0:T(2,128)(2,1)S(1)}, u32[]{:S(2)}, u32[]{:S(2)}) async-start(bf16[4,2,20480]{2,1,0:T(2,128)(2,1)} %reshape.45), calls=%async_computation | async-start | bytes 655360 | tf_op jit(solution)/shard_map/all_to_all | solution.py:28
  18.8 5.0 %all-to-all-done = bf16[4,2,20480]{2,1,0:T(2,128)(2,1)S(1)} async-done(((bf16[4,2,20480]{2,1,0:T(2,128)(2,1)}), bf16[4,2,20480]{2,1,0:T(2,128)(2,1)S(1)}, u32[]{:S(2)}, u32[]{:S(2)}) %all-to-all-start) | async-done | bytes 327712 | tf_op jit(solution)/shard_map/all_to_all | solution.py:28
  24.8 1.4 %broadcast_in_dim.26 = bf16[16,3,80,256]{3,2,1,0:T(8,128)(2,1)} broadcast(bf16[3,80,256]{2,1,0:T(8,128)(2,1)S(1)} %bitcast_select_fusion), dimensions={1,2,3} | broadcast | bytes 2088960 | tf_op jit(solution)/shard_map/broadcast_in_dim | solution.py:35
  26.2 3.7 %all-to-all-start.1 = ((bf16[16,3,80,256]{3,2,1,0:T(8,128)(2,1)}), bf16[16,3,80,256]{3,2,1,0:T(8,128)(2,1)S(1)}, u32[]{:S(2)}, u32[]{:S(2)}) async-start(bf16[16,3,80,256]{3,2,1,0:T(8,128)(2,1)} %broadcast_in_dim.26), calls=%async_computation.1 | async-start | bytes 3932160 | tf_op jit(solution)/shard_map/all_to_all | solution.py:36
  30.3 1.9 %collective-permute-start.5 = (bf16[256,320]{0,1:T(8,128)(2,1)S(1)}, bf16[256,320]{0,1:T(8,128)(2,1)S(1)}, u32[]{:S(2)}, u32[]{:S(2)}) collective-permute-start(bf16[256,320]{0,1:T(8,128)(2,1)S(1)} %copy.16), channel_id=1, source_target_pairs={{0,4},{4,8},{8,12},{12,16},{16,20},{20,24},{24,28},{28,32},{32,36}... | collective-permute-start | bytes 491528 | tf_op jit(solution)/shard_map/ppermute | solution.py:45
  32.2 10.3 %collective-permute-start = (bf16[256,320]{0,1:T(8,128)(2,1)S(1)}, bf16[256,320]{0,1:T(8,128)(2,1)S(1)}, u32[]{:S(2)}, u32[]{:S(2)}) collective-permute-start(bf16[256,320]{0,1:T(8,128)(2,1)S(1)} %copy.16), channel_id=1, source_target_pairs={{0,44},{4,0},{8,4},{12,8},{16,12},{20,16},{24,20},{28,24},{32,28},... | collective-permute-start | bytes 491528 | tf_op jit(solution)/shard_map/ppermute | solution.py:48
  43.6 1.8 %collective-permute-done.5 = bf16[256,320]{0,1:T(8,128)(2,1)S(1)} collective-permute-done((bf16[256,320]{0,1:T(8,128)(2,1)S(1)}, bf16[256,320]{0,1:T(8,128)(2,1)S(1)}, u32[]{:S(2)}, u32[]{:S(2)}) %collective-permute-start.5) | collective-permute-done | bytes 163872 | tf_op jit(solution)/shard_map/ppermute | solution.py:45
  45.4 1.9 %collective-permute-start.6 = (bf16[256,320]{0,1:T(8,128)(2,1)S(1)}, bf16[256,320]{0,1:T(8,128)(2,1)S(1)}, u32[]{:S(2)}, u32[]{:S(2)}) collective-permute-start(bf16[256,320]{0,1:T(8,128)(2,1)S(1)} %collective-permute-done.5), channel_id=1, source_target_pairs={{0,4},{4,8},{8,12},{12,16},{16,20},{20,24},{24,28},{28,32},{32,36}... | collective-permute-start | bytes 491528 | tf_op jit(solution)/shard_map/ppermute | solution.py:45
  47.3 5.1 %collective-permute-start.1 = (bf16[256,320]{0,1:T(8,128)(2,1)S(1)}, bf16[256,320]{0,1:T(8,128)(2,1)S(1)}, u32[]{:S(2)}, u32[]{:S(2)}) collective-permute-start(bf16[256,320]{0,1:T(8,128)(2,1)S(1)} %collective-permute-done), channel_id=1, source_target_pairs={{0,44},{4,0},{8,4},{12,8},{16,12},{20,16},{24,20},{28,24},{32,28},... | collective-permute-start | bytes 491528 | tf_op jit(solution)/shard_map/ppermute | solution.py:48
  53.1 1.3 %collective-permute-done.6 = bf16[256,320]{0,1:T(8,128)(2,1)S(1)} collective-permute-done((bf16[256,320]{0,1:T(8,128)(2,1)S(1)}, bf16[256,320]{0,1:T(8,128)(2,1)S(1)}, u32[]{:S(2)}, u32[]{:S(2)}) %collective-permute-start.6) | collective-permute-done | bytes 163872 | tf_op jit(solution)/shard_map/ppermute | solution.py:45
  54.4 1.9 %collective-permute-start.7 = (bf16[256,320]{0,1:T(8,128)(2,1)S(1)}, bf16[256,320]{0,1:T(8,128)(2,1)S(1)}, u32[]{:S(2)}, u32[]{:S(2)}) collective-permute-start(bf16[256,320]{0,1:T(8,128)(2,1)S(1)} %collective-permute-done.6), channel_id=1, source_target_pairs={{0,4},{4,8},{8,12},{12,16},{16,20},{20,24},{24,28},{28,32},{32,36}... | collective-permute-start | bytes 491528 | tf_op jit(solution)/shard_map/ppermute | solution.py:45
  56.3 5.1 %collective-permute-start.2 = (bf16[256,320]{0,1:T(8,128)(2,1)S(1)}, bf16[256,320]{0,1:T(8,128)(2,1)S(1)}, u32[]{:S(2)}, u32[]{:S(2)}) collective-permute-start(bf16[256,320]{0,1:T(8,128)(2,1)S(1)} %collective-permute-done.1), channel_id=1, source_target_pairs={{0,44},{4,0},{8,4},{12,8},{16,12},{20,16},{24,20},{28,24},{32,28},... | collective-permute-start | bytes 491528 | tf_op jit(solution)/shard_map/ppermute | solution.py:48
  62.8 1.9 %collective-permute-start.8 = (bf16[256,320]{0,1:T(8,128)(2,1)S(1)}, bf16[256,320]{0,1:T(8,128)(2,1)S(1)}, u32[]{:S(2)}, u32[]{:S(2)}) collective-permute-start(bf16[256,320]{0,1:T(8,128)(2,1)S(1)} %collective-permute-done.7), channel_id=1, source_target_pairs={{0,4},{4,8},{8,12},{12,16},{16,20},{20,24},{24,28},{28,32},{32,36}... | collective-permute-start | bytes 491528 | tf_op jit(solution)/shard_map/ppermute | solution.py:45
  64.7 5.1 %collective-permute-start.3 = (bf16[256,320]{0,1:T(8,128)(2,1)S(1)}, bf16[256,320]{0,1:T(8,128)(2,1)S(1)}, u32[]{:S(2)}, u32[]{:S(2)}) collective-permute-start(bf16[256,320]{0,1:T(8,128)(2,1)S(1)} %collective-permute-done.2), channel_id=1, source_target_pairs={{0,44},{4,0},{8,4},{12,8},{16,12},{20,16},{24,20},{28,24},{32,28},... | collective-permute-start | bytes 491528 | tf_op jit(solution)/shard_map/ppermute | solution.py:48
  71.2 1.9 %collective-permute-start.9 = (bf16[256,320]{0,1:T(8,128)(2,1)S(1)}, bf16[256,320]{0,1:T(8,128)(2,1)S(1)}, u32[]{:S(2)}, u32[]{:S(2)}) collective-permute-start(bf16[256,320]{0,1:T(8,128)(2,1)S(1)} %collective-permute-done.8), channel_id=1, source_target_pairs={{0,4},{4,8},{8,12},{12,16},{16,20},{20,24},{24,28},{28,32},{32,36}... | collective-permute-start | bytes 491528 | tf_op jit(solution)/shard_map/ppermute | solution.py:45
  73.2 5.1 %collective-permute-start.4 = (bf16[256,320]{0,1:T(8,128)(2,1)S(1)}, bf16[256,320]{0,1:T(8,128)(2,1)S(1)}, u32[]{:S(2)}, u32[]{:S(2)}) collective-permute-start(bf16[256,320]{0,1:T(8,128)(2,1)S(1)} %collective-permute-done.3), channel_id=1, source_target_pairs={{0,44},{4,0},{8,4},{12,8},{16,12},{20,16},{24,20},{28,24},{32,28},... | collective-permute-start | bytes 491528 | tf_op jit(solution)/shard_map/ppermute | solution.py:48
  79.6 1.9 %collective-permute-start.10 = (bf16[256,320]{0,1:T(8,128)(2,1)S(1)}, bf16[256,320]{0,1:T(8,128)(2,1)S(1)}, u32[]{:S(2)}, u32[]{:S(2)}) collective-permute-start(bf16[256,320]{0,1:T(8,128)(2,1)S(1)} %collective-permute-done.9), channel_id=1, source_target_pairs={{0,4},{4,8},{8,12},{12,16},{16,20},{20,24},{24,28},{28,32},{32,36}... | collective-permute-start | bytes 491528 | tf_op jit(solution)/shard_map/ppermute | solution.py:45
  82.3 5.8 %collective-permute-done.10 = bf16[256,320]{0,1:T(8,128)(2,1)S(1)} collective-permute-done((bf16[256,320]{0,1:T(8,128)(2,1)S(1)}, bf16[256,320]{0,1:T(8,128)(2,1)S(1)}, u32[]{:S(2)}, u32[]{:S(2)}) %collective-permute-start.10) | collective-permute-done | bytes 163872 | tf_op jit(solution)/shard_map/ppermute | solution.py:45
  92.1 2.5 %fusion.1 = f32[256,256,1]{1,0,2:T(8,128)S(1)} fusion(bf16[12,256,320]{1,2,0:T(8,128)(2,1)} %bitcast_dynamic-update-slice_fusion, s32[]{:T(128)S(6)} %select_n.29, bf16[12,320,256]{2,1,0:T(8,128)(2,1)S(1)} %bitcast.47), kind=kOutput, calls=%fused_computation.3 | convolution fusion | flops 504299520 | bytes 4194308 | tf_op jit(solution)/shard_map/vmc,vcn->mn/dot_general | solution.py:53
  94.7 9.1 %all_to_all.22 = f32[4,64,256]{2,1,0:T(8,128)S(1)} all-to-all(f32[4,64,256]{2,1,0:T(8,128)S(1)} %bitcast.53), channel_id=1, replica_groups=mesh['oy'=8,'oc'=2,'virt'=12,'rep'=4] {'rep'}, dimensions={0} | all-to-all | bytes 524288 | tf_op jit(solution)/shard_map/all_to_all | solution.py:55
  (39 shorter events, 13.9 us)
Async XLA Ops:
  5.9 17.8 %all-to-all-start = ((bf16[4,2,20480]{2,1,0:T(2,128)(2,1)}), bf16[4,2,20480]{2,1,0:T(2,128)(2,1)S(1)}, u32[]{:S(2)}, u32[]{:S(2)}) async-start(bf16[4,2,20480]{2,1,0:T(2,128)(2,1)} %reshape.45), calls=%async_computation | async-start | bytes 655360 | tf_op jit(solution)/shard_map/all_to_all | solution.py:28
  26.2 65.9 %all-to-all-start.1 = ((bf16[16,3,80,256]{3,2,1,0:T(8,128)(2,1)}), bf16[16,3,80,256]{3,2,1,0:T(8,128)(2,1)S(1)}, u32[]{:S(2)}, u32[]{:S(2)}) async-start(bf16[16,3,80,256]{3,2,1,0:T(8,128)(2,1)} %broadcast_in_dim.26), calls=%async_computation.1 | async-start | bytes 3932160 | tf_op jit(solution)/shard_map/all_to_all | solution.py:36
  30.3 15.1 %collective-permute-start.5 = (bf16[256,320]{0,1:T(8,128)(2,1)S(1)}, bf16[256,320]{0,1:T(8,128)(2,1)S(1)}, u32[]{:S(2)}, u32[]{:S(2)}) collective-permute-start(bf16[256,320]{0,1:T(8,128)(2,1)S(1)} %copy.16), channel_id=1, source_target_pairs={{0,4},{4,8},{8,12},{12,16},{16,20},{20,24},{24,28},{28,32},{32,36}... | collective-permute-start | bytes 491528 | tf_op jit(solution)/shard_map/ppermute | solution.py:45
  32.2 15.1 %collective-permute-start = (bf16[256,320]{0,1:T(8,128)(2,1)S(1)}, bf16[256,320]{0,1:T(8,128)(2,1)S(1)}, u32[]{:S(2)}, u32[]{:S(2)}) collective-permute-start(bf16[256,320]{0,1:T(8,128)(2,1)S(1)} %copy.16), channel_id=1, source_target_pairs={{0,44},{4,0},{8,4},{12,8},{16,12},{20,16},{24,20},{28,24},{32,28},... | collective-permute-start | bytes 491528 | tf_op jit(solution)/shard_map/ppermute | solution.py:48
  45.4 9.0 %collective-permute-start.6 = (bf16[256,320]{0,1:T(8,128)(2,1)S(1)}, bf16[256,320]{0,1:T(8,128)(2,1)S(1)}, u32[]{:S(2)}, u32[]{:S(2)}) collective-permute-start(bf16[256,320]{0,1:T(8,128)(2,1)S(1)} %collective-permute-done.5), channel_id=1, source_target_pairs={{0,4},{4,8},{8,12},{12,16},{16,20},{20,24},{24,28},{28,32},{32,36}... | collective-permute-start | bytes 491528 | tf_op jit(solution)/shard_map/ppermute | solution.py:45
  47.3 9.0 %collective-permute-start.1 = (bf16[256,320]{0,1:T(8,128)(2,1)S(1)}, bf16[256,320]{0,1:T(8,128)(2,1)S(1)}, u32[]{:S(2)}, u32[]{:S(2)}) collective-permute-start(bf16[256,320]{0,1:T(8,128)(2,1)S(1)} %collective-permute-done), channel_id=1, source_target_pairs={{0,44},{4,0},{8,4},{12,8},{16,12},{20,16},{24,20},{28,24},{32,28},... | collective-permute-start | bytes 491528 | tf_op jit(solution)/shard_map/ppermute | solution.py:48
  54.4 8.4 %collective-permute-start.7 = (bf16[256,320]{0,1:T(8,128)(2,1)S(1)}, bf16[256,320]{0,1:T(8,128)(2,1)S(1)}, u32[]{:S(2)}, u32[]{:S(2)}) collective-permute-start(bf16[256,320]{0,1:T(8,128)(2,1)S(1)} %collective-permute-done.6), channel_id=1, source_target_pairs={{0,4},{4,8},{8,12},{12,16},{16,20},{20,24},{24,28},{28,32},{32,36}... | collective-permute-start | bytes 491528 | tf_op jit(solution)/shard_map/ppermute | solution.py:45
  56.3 8.4 %collective-permute-start.2 = (bf16[256,320]{0,1:T(8,128)(2,1)S(1)}, bf16[256,320]{0,1:T(8,128)(2,1)S(1)}, u32[]{:S(2)}, u32[]{:S(2)}) collective-permute-start(bf16[256,320]{0,1:T(8,128)(2,1)S(1)} %collective-permute-done.1), channel_id=1, source_target_pairs={{0,44},{4,0},{8,4},{12,8},{16,12},{20,16},{24,20},{28,24},{32,28},... | collective-permute-start | bytes 491528 | tf_op jit(solution)/shard_map/ppermute | solution.py:48
  62.8 8.4 %collective-permute-start.8 = (bf16[256,320]{0,1:T(8,128)(2,1)S(1)}, bf16[256,320]{0,1:T(8,128)(2,1)S(1)}, u32[]{:S(2)}, u32[]{:S(2)}) collective-permute-start(bf16[256,320]{0,1:T(8,128)(2,1)S(1)} %collective-permute-done.7), channel_id=1, source_target_pairs={{0,4},{4,8},{8,12},{12,16},{16,20},{20,24},{24,28},{28,32},{32,36}... | collective-permute-start | bytes 491528 | tf_op jit(solution)/shard_map/ppermute | solution.py:45
  64.7 8.4 %collective-permute-start.3 = (bf16[256,320]{0,1:T(8,128)(2,1)S(1)}, bf16[256,320]{0,1:T(8,128)(2,1)S(1)}, u32[]{:S(2)}, u32[]{:S(2)}) collective-permute-start(bf16[256,320]{0,1:T(8,128)(2,1)S(1)} %collective-permute-done.2), channel_id=1, source_target_pairs={{0,44},{4,0},{8,4},{12,8},{16,12},{20,16},{24,20},{28,24},{32,28},... | collective-permute-start | bytes 491528 | tf_op jit(solution)/shard_map/ppermute | solution.py:48
  71.2 8.4 %collective-permute-start.9 = (bf16[256,320]{0,1:T(8,128)(2,1)S(1)}, bf16[256,320]{0,1:T(8,128)(2,1)S(1)}, u32[]{:S(2)}, u32[]{:S(2)}) collective-permute-start(bf16[256,320]{0,1:T(8,128)(2,1)S(1)} %collective-permute-done.8), channel_id=1, source_target_pairs={{0,4},{4,8},{8,12},{12,16},{16,20},{20,24},{24,28},{28,32},{32,36}... | collective-permute-start | bytes 491528 | tf_op jit(solution)/shard_map/ppermute | solution.py:45
  73.2 8.4 %collective-permute-start.4 = (bf16[256,320]{0,1:T(8,128)(2,1)S(1)}, bf16[256,320]{0,1:T(8,128)(2,1)S(1)}, u32[]{:S(2)}, u32[]{:S(2)}) collective-permute-start(bf16[256,320]{0,1:T(8,128)(2,1)S(1)} %collective-permute-done.3), channel_id=1, source_target_pairs={{0,44},{4,0},{8,4},{12,8},{16,12},{20,16},{24,20},{28,24},{32,28},... | collective-permute-start | bytes 491528 | tf_op jit(solution)/shard_map/ppermute | solution.py:48
  79.6 8.4 %collective-permute-start.10 = (bf16[256,320]{0,1:T(8,128)(2,1)S(1)}, bf16[256,320]{0,1:T(8,128)(2,1)S(1)}, u32[]{:S(2)}, u32[]{:S(2)}) collective-permute-start(bf16[256,320]{0,1:T(8,128)(2,1)S(1)} %collective-permute-done.9), channel_id=1, source_target_pairs={{0,4},{4,8},{8,12},{12,16},{16,20},{20,24},{24,28},{28,32},{32,36}... | collective-permute-start | bytes 491528 | tf_op jit(solution)/shard_map/ppermute | solution.py:45

commit v8 on v7

--- a/solution.py
+++ b/solution.py
@@ -47,10 +47,9 @@
         if s < n_virt - s:
             g = lax.ppermute(g, "virt", bwd)
             ahead.append(g)
-    pieces = [a] + ahead + behind[::-1]
-    a = jnp.stack(pieces, axis=0)
+    pieces = lax.optimization_barrier([a] + ahead + behind[::-1])
 
-    partial_sum = jnp.einsum("vmc,vcn->mn", a, b, preferred_element_type=jnp.float32)
+    partial_sum = sum(jnp.dot(p, b[j], preferred_element_type=jnp.float32) for j, p in enumerate(pieces))
     partial_sum = partial_sum.reshape(n_rep, rows, nb)
     partial_sum = lax.all_to_all(partial_sum, "rep", split_axis=0, concat_axis=0, tiled=True)
     return jnp.sum(partial_sum, axis=0)

time: 106 us -> 110 us (1.038)
  local copies, waits for them, and re-layouts: 14.7 us -> 6.08 us
  waiting for transfers between devices: 15.8 us -> 23.5 us
  matrix products: 2.54 us -> 6.43 us
    ppermute x6, waiting for transfers between devices: 10.9 us -> 18.5 us  [local(): f = lax.ppermute(f, 'virt', fwd)]
    unnamed x15 -> x4, local copies, waits for them, and re-layouts: 9.38 us -> 1.93 us
    dot_general x1 -> x12, matrix products: 2.54 us -> 6.43 us  [local(): jnp.dot(p, b[j], preferred_element_type=jnp.float32)]
  transfers between devices with their start and end apart: 13 -> 13, of which waited for: 7 -> 7; matrix products, arithmetic and copies ran while one was open for 8% -> 0% of each run, Pallas kernels for 0% -> 0%
where the time goes in v8:
time: 110 us; the launch traced here: 108 us
  starting transfers between devices  59 us (54%)
  waiting for transfers between devices  23.5 us (21%)
  blocking collectives  9.06 us (8%)
  matrix products  6.43 us (6%)
  local copies, waits for them, and re-layouts  6.08 us (6%)
  other arithmetic  3.78 us (3%)
    ppermute x5, starting transfers between devices, local(): g = lax.ppermute(g, 'virt', bwd)  30.9 us
    ppermute x6, waiting for transfers between devices, local(): f = lax.ppermute(f, 'virt', fwd)  18.5 us
    all_to_all x1, starting transfers between devices, local(): both = lax.all_to_all(both, 'rep', split_axis=0, concat_axis=0, tiled=True)  12.9 us
    ppermute x6, starting transfers between devices, local(): f = lax.ppermute(f, 'virt', fwd)  11.5 us
    all_to_all x1, blocking collectives, local(): lax.all_to_all(partial_sum, 'rep', split_axis=0, concat_axis=0, tiled=True)  9.06 us
    dot_general x12, matrix products, local(): jnp.dot(p, b[j], preferred_element_type=jnp.float32)  6.43 us
    all_to_all x1, waiting for transfers between devices, local(): both = lax.all_to_all(both, 'rep', split_axis=0, concat_axis=0, tiled=True)  4.95 us
    all_to_all x1, starting transfers between devices, local(): b = lax.all_to_all(b, ('oy', 'oc'), split_axis=0, concat_axis=0, tiled=True)  3.72 us
  transfers between devices with their start and end apart: 13, of which 7 were waited for; matrix products, arithmetic and copies ran while one was open for 0% of the time, Pallas kernels for 0%

profile of v8, /device:TPU:6, one launch (start us, length us, event | category | flops | bytes accessed | tf_op | source)
XLA Modules:
  0.0 108.2 jit_solution(7950999972589187992)
XLA Ops:
  1.3 1.3 %reshape.38 = bf16[64,4,4,80]{3,2,1,0:T(4,128)(2,1)S(1)} reshape(bf16[64,1280]{1,0:T(8,128)(2,1)} %param.4) | data formatting | bytes 327680 | tf_op jit(solution)/shard_map/reshape | solution.py:20
  5.9 12.9 %all-to-all-start = ((bf16[4,2,20480]{2,1,0:T(2,128)(2,1)}), bf16[4,2,20480]{2,1,0:T(2,128)(2,1)S(1)}, u32[]{:S(2)}, u32[]{:S(2)}) async-start(bf16[4,2,20480]{2,1,0:T(2,128)(2,1)} %reshape.44), calls=%async_computation | async-start | bytes 655360 | tf_op jit(solution)/shard_map/all_to_all | solution.py:28
  18.8 5.0 %all-to-all-done = bf16[4,2,20480]{2,1,0:T(2,128)(2,1)S(1)} async-done(((bf16[4,2,20480]{2,1,0:T(2,128)(2,1)}), bf16[4,2,20480]{2,1,0:T(2,128)(2,1)S(1)}, u32[]{:S(2)}, u32[]{:S(2)}) %all-to-all-start) | async-done | bytes 327712 | tf_op jit(solution)/shard_map/all_to_all | solution.py:28
  24.8 1.4 %broadcast_in_dim.26 = bf16[16,3,80,256]{3,2,1,0:T(8,128)(2,1)} broadcast(bf16[3,80,256]{2,1,0:T(8,128)(2,1)S(1)} %bitcast_select_fusion), dimensions={1,2,3} | broadcast | bytes 2088960 | tf_op jit(solution)/shard_map/broadcast_in_dim | solution.py:35
  26.2 3.7 %all-to-all-start.1 = ((bf16[16,3,80,256]{3,2,1,0:T(8,128)(2,1)}), bf16[16,3,80,256]{3,2,1,0:T(8,128)(2,1)S(1)}, u32[]{:S(2)}, u32[]{:S(2)}) async-start(bf16[16,3,80,256]{3,2,1,0:T(8,128)(2,1)} %broadcast_in_dim.26), calls=%async_computation.1 | async-start | bytes 3932160 | tf_op jit(solution)/shard_map/all_to_all | solution.py:36
  30.2 1.9 %collective-permute-start.5 = (bf16[256,320]{1,0:T(8,128)(2,1)S(1)}, bf16[256,320]{1,0:T(8,128)(2,1)S(1)}, u32[]{:S(2)}, u32[]{:S(2)}) collective-permute-start(bf16[256,320]{1,0:T(8,128)(2,1)S(1)} %reshape.41), channel_id=1, source_target_pairs={{0,4},{4,8},{8,12},{12,16},{16,20},{20,24},{24,28},{28,32},{32,36}... | collective-permute-start | bytes 491528 | tf_op jit(solution)/shard_map/ppermute | solution.py:45
  32.1 10.3 %collective-permute-start = (bf16[256,320]{1,0:T(8,128)(2,1)S(1)}, bf16[256,320]{1,0:T(8,128)(2,1)S(1)}, u32[]{:S(2)}, u32[]{:S(2)}) collective-permute-start(bf16[256,320]{1,0:T(8,128)(2,1)S(1)} %reshape.41), channel_id=1, source_target_pairs={{0,44},{4,0},{8,4},{12,8},{16,12},{20,16},{24,20},{28,24},{32,28},... | collective-permute-start | bytes 491528 | tf_op jit(solution)/shard_map/ppermute | solution.py:48
  42.4 3.5 %collective-permute-done.5 = bf16[256,320]{1,0:T(8,128)(2,1)S(1)} collective-permute-done((bf16[256,320]{1,0:T(8,128)(2,1)S(1)}, bf16[256,320]{1,0:T(8,128)(2,1)S(1)}, u32[]{:S(2)}, u32[]{:S(2)}) %collective-permute-start.5) | collective-permute-done | bytes 163872 | tf_op jit(solution)/shard_map/ppermute | solution.py:45
  46.0 1.9 %collective-permute-start.6 = (bf16[256,320]{1,0:T(8,128)(2,1)S(1)}, bf16[256,320]{1,0:T(8,128)(2,1)S(1)}, u32[]{:S(2)}, u32[]{:S(2)}) collective-permute-start(bf16[256,320]{1,0:T(8,128)(2,1)S(1)} %collective-permute-done.5), channel_id=1, source_target_pairs={{0,4},{4,8},{8,12},{12,16},{16,20},{20,24},{24,28},{28,32},{32,36}... | collective-permute-start | bytes 491528 | tf_op jit(solution)/shard_map/ppermute | solution.py:45
  47.9 5.1 %collective-permute-start.1 = (bf16[256,320]{1,0:T(8,128)(2,1)S(1)}, bf16[256,320]{1,0:T(8,128)(2,1)S(1)}, u32[]{:S(2)}, u32[]{:S(2)}) collective-permute-start(bf16[256,320]{1,0:T(8,128)(2,1)S(1)} %collective-permute-done), channel_id=1, source_target_pairs={{0,44},{4,0},{8,4},{12,8},{16,12},{20,16},{24,20},{28,24},{32,28},... | collective-permute-start | bytes 491528 | tf_op jit(solution)/shard_map/ppermute | solution.py:48
  53.0 2.7 %collective-permute-done.6 = bf16[256,320]{1,0:T(8,128)(2,1)S(1)} collective-permute-done((bf16[256,320]{1,0:T(8,128)(2,1)S(1)}, bf16[256,320]{1,0:T(8,128)(2,1)S(1)}, u32[]{:S(2)}, u32[]{:S(2)}) %collective-permute-start.6) | collective-permute-done | bytes 163872 | tf_op jit(solution)/shard_map/ppermute | solution.py:45
  55.7 1.9 %collective-permute-start.7 = (bf16[256,320]{1,0:T(8,128)(2,1)S(1)}, bf16[256,320]{1,0:T(8,128)(2,1)S(1)}, u32[]{:S(2)}, u32[]{:S(2)}) collective-permute-start(bf16[256,320]{1,0:T(8,128)(2,1)S(1)} %collective-permute-done.6), channel_id=1, source_target_pairs={{0,4},{4,8},{8,12},{12,16},{16,20},{20,24},{24,28},{28,32},{32,36}... | collective-permute-start | bytes 491528 | tf_op jit(solution)/shard_map/ppermute | solution.py:45
  57.6 5.1 %collective-permute-start.2 = (bf16[256,320]{1,0:T(8,128)(2,1)S(1)}, bf16[256,320]{1,0:T(8,128)(2,1)S(1)}, u32[]{:S(2)}, u32[]{:S(2)}) collective-permute-start(bf16[256,320]{1,0:T(8,128)(2,1)S(1)} %collective-permute-done.1), channel_id=1, source_target_pairs={{0,44},{4,0},{8,4},{12,8},{16,12},{20,16},{24,20},{28,24},{32,28},... | collective-permute-start | bytes 491528 | tf_op jit(solution)/shard_map/ppermute | solution.py:48
  62.7 1.8 %collective-permute-done.7 = bf16[256,320]{1,0:T(8,128)(2,1)S(1)} collective-permute-done((bf16[256,320]{1,0:T(8,128)(2,1)S(1)}, bf16[256,320]{1,0:T(8,128)(2,1)S(1)}, u32[]{:S(2)}, u32[]{:S(2)}) %collective-permute-start.7) | collective-permute-done | bytes 163872 | tf_op jit(solution)/shard_map/ppermute | solution.py:45
  64.6 1.9 %collective-permute-start.8 = (bf16[256,320]{1,0:T(8,128)(2,1)S(1)}, bf16[256,320]{1,0:T(8,128)(2,1)S(1)}, u32[]{:S(2)}, u32[]{:S(2)}) collective-permute-start(bf16[256,320]{1,0:T(8,128)(2,1)S(1)} %collective-permute-done.7), channel_id=1, source_target_pairs={{0,4},{4,8},{8,12},{12,16},{16,20},{20,24},{24,28},{28,32},{32,36}... | collective-permute-start | bytes 491528 | tf_op jit(solution)/shard_map/ppermute | solution.py:45
  66.5 5.1 %collective-permute-start.3 = (bf16[256,320]{1,0:T(8,128)(2,1)S(1)}, bf16[256,320]{1,0:T(8,128)(2,1)}, u32[]{:S(2)}, u32[]{:S(2)}) collective-permute-start(bf16[256,320]{1,0:T(8,128)(2,1)S(1)} %collective-permute-done.2), channel_id=1, source_target_pairs={{0,44},{4,0},{8,4},{12,8},{16,12},{20,16},{24,20},{28,24},{32,28},... | collective-permute-start | bytes 491528 | tf_op jit(solution)/shard_map/ppermute | solution.py:48
  71.6 1.7 %collective-permute-done.8 = bf16[256,320]{1,0:T(8,128)(2,1)S(1)} collective-permute-done((bf16[256,320]{1,0:T(8,128)(2,1)S(1)}, bf16[256,320]{1,0:T(8,128)(2,1)S(1)}, u32[]{:S(2)}, u32[]{:S(2)}) %collective-permute-start.8) | collective-permute-done | bytes 163872 | tf_op jit(solution)/shard_map/ppermute | solution.py:45
  73.3 1.9 %collective-permute-start.9 = (bf16[256,320]{1,0:T(8,128)(2,1)S(1)}, bf16[256,320]{1,0:T(8,128)(2,1)}, u32[]{:S(2)}, u32[]{:S(2)}) collective-permute-start(bf16[256,320]{1,0:T(8,128)(2,1)S(1)} %collective-permute-done.8), channel_id=1, source_target_pairs={{0,4},{4,8},{8,12},{12,16},{16,20},{20,24},{24,28},{28,32},{32,36}... | collective-permute-start | bytes 491528 | tf_op jit(solution)/shard_map/ppermute | solution.py:45
  75.2 5.2 %collective-permute-start.4 = (bf16[256,320]{1,0:T(8,128)(2,1)}, bf16[256,320]{1,0:T(8,128)(2,1)}, u32[]{:S(2)}, u32[]{:S(2)}) collective-permute-start(bf16[256,320]{1,0:T(8,128)(2,1)} %collective-permute-done.3), channel_id=1, source_target_pairs={{0,44},{4,0},{8,4},{12,8},{16,12},{20,16},{24,20},{28,24},{32,28},... | collective-permute-start | bytes 491528 | tf_op jit(solution)/shard_map/ppermute | solution.py:48
  80.5 1.7 %collective-permute-done.9 = bf16[256,320]{1,0:T(8,128)(2,1)} collective-permute-done((bf16[256,320]{1,0:T(8,128)(2,1)S(1)}, bf16[256,320]{1,0:T(8,128)(2,1)}, u32[]{:S(2)}, u32[]{:S(2)}) %collective-permute-start.9) | collective-permute-done | bytes 163872 | tf_op jit(solution)/shard_map/ppermute | solution.py:45
  82.2 1.9 %collective-permute-start.10 = (bf16[256,320]{1,0:T(8,128)(2,1)}, bf16[256,320]{1,0:T(8,128)(2,1)}, u32[]{:S(2)}, u32[]{:S(2)}) collective-permute-start(bf16[256,320]{1,0:T(8,128)(2,1)} %collective-permute-done.9), channel_id=1, source_target_pairs={{0,4},{4,8},{8,12},{12,16},{16,20},{20,24},{24,28},{28,32},{32,36}... | collective-permute-start | bytes 491528 | tf_op jit(solution)/shard_map/ppermute | solution.py:45
  84.1 7.1 %collective-permute-done.10 = bf16[256,320]{1,0:T(8,128)(2,1)} collective-permute-done((bf16[256,320]{1,0:T(8,128)(2,1)}, bf16[256,320]{1,0:T(8,128)(2,1)}, u32[]{:S(2)}, u32[]{:S(2)}) %collective-permute-start.10) | collective-permute-done | bytes 163872 | tf_op jit(solution)/shard_map/ppermute | solution.py:45
  92.7 1.1 %fusion.22 = f32[256,256]{1,0:T(8,128)S(1)} fusion(bf16[256,320]{1,0:T(8,128)(2,1)} %collective-permute-done.3, bf16[12,320,256]{2,1,0:T(8,128)(2,1)S(1)} %fusion), kind=kOutput, calls=%fused_computation.41 | convolution fusion | flops 41943040 | bytes 589824 | tf_op jit(solution)/shard_map/dot_general | solution.py:52
  98.5 9.1 %all_to_all.22 = f32[4,64,256]{2,1,0:T(8,128)S(1)} all-to-all(f32[4,64,256]{2,1,0:T(8,128)S(1)} %bitcast.72), channel_id=1, replica_groups=mesh['oy'=8,'oc'=2,'virt'=12,'rep'=4] {'rep'}, dimensions={0} | all-to-all | bytes 524288 | tf_op jit(solution)/shard_map/all_to_all | solution.py:54
  (36 shorter events, 12.4 us)
Async XLA Ops:
  5.9 17.8 %all-to-all-start = ((bf16[4,2,20480]{2,1,0:T(2,128)(2,1)}), bf16[4,2,20480]{2,1,0:T(2,128)(2,1)S(1)}, u32[]{:S(2)}, u32[]{:S(2)}) async-start(bf16[4,2,20480]{2,1,0:T(2,128)(2,1)} %reshape.44), calls=%async_computation | async-start | bytes 655360 | tf_op jit(solution)/shard_map/all_to_all | solution.py:28
  26.2 65.1 %all-to-all-start.1 = ((bf16[16,3,80,256]{3,2,1,0:T(8,128)(2,1)}), bf16[16,3,80,256]{3,2,1,0:T(8,128)(2,1)S(1)}, u32[]{:S(2)}, u32[]{:S(2)}) async-start(bf16[16,3,80,256]{3,2,1,0:T(8,128)(2,1)} %broadcast_in_dim.26), calls=%async_computation.1 | async-start | bytes 3932160 | tf_op jit(solution)/shard_map/all_to_all | solution.py:36
  30.2 15.8 %collective-permute-start.5 = (bf16[256,320]{1,0:T(8,128)(2,1)S(1)}, bf16[256,320]{1,0:T(8,128)(2,1)S(1)}, u32[]{:S(2)}, u32[]{:S(2)}) collective-permute-start(bf16[256,320]{1,0:T(8,128)(2,1)S(1)} %reshape.41), channel_id=1, source_target_pairs={{0,4},{4,8},{8,12},{12,16},{16,20},{20,24},{24,28},{28,32},{32,36}... | collective-permute-start | bytes 491528 | tf_op jit(solution)/shard_map/ppermute | solution.py:45
  32.1 15.8 %collective-permute-start = (bf16[256,320]{1,0:T(8,128)(2,1)S(1)}, bf16[256,320]{1,0:T(8,128)(2,1)S(1)}, u32[]{:S(2)}, u32[]{:S(2)}) collective-permute-start(bf16[256,320]{1,0:T(8,128)(2,1)S(1)} %reshape.41), channel_id=1, source_target_pairs={{0,44},{4,0},{8,4},{12,8},{16,12},{20,16},{24,20},{28,24},{32,28},... | collective-permute-start | bytes 491528 | tf_op jit(solution)/shard_map/ppermute | solution.py:48
  46.0 9.7 %collective-permute-start.6 = (bf16[256,320]{1,0:T(8,128)(2,1)S(1)}, bf16[256,320]{1,0:T(8,128)(2,1)S(1)}, u32[]{:S(2)}, u32[]{:S(2)}) collective-permute-start(bf16[256,320]{1,0:T(8,128)(2,1)S(1)} %collective-permute-done.5), channel_id=1, source_target_pairs={{0,4},{4,8},{8,12},{12,16},{16,20},{20,24},{24,28},{28,32},{32,36}... | collective-permute-start | bytes 491528 | tf_op jit(solution)/shard_map/ppermute | solution.py:45
  47.9 9.7 %collective-permute-start.1 = (bf16[256,320]{1,0:T(8,128)(2,1)S(1)}, bf16[256,320]{1,0:T(8,128)(2,1)S(1)}, u32[]{:S(2)}, u32[]{:S(2)}) collective-permute-start(bf16[256,320]{1,0:T(8,128)(2,1)S(1)} %collective-permute-done), channel_id=1, source_target_pairs={{0,44},{4,0},{8,4},{12,8},{16,12},{20,16},{24,20},{28,24},{32,28},... | collective-permute-start | bytes 491528 | tf_op jit(solution)/shard_map/ppermute | solution.py:48
  55.7 8.9 %collective-permute-start.7 = (bf16[256,320]{1,0:T(8,128)(2,1)S(1)}, bf16[256,320]{1,0:T(8,128)(2,1)S(1)}, u32[]{:S(2)}, u32[]{:S(2)}) collective-permute-start(bf16[256,320]{1,0:T(8,128)(2,1)S(1)} %collective-permute-done.6), channel_id=1, source_target_pairs={{0,4},{4,8},{8,12},{12,16},{16,20},{20,24},{24,28},{28,32},{32,36}... | collective-permute-start | bytes 491528 | tf_op jit(solution)/shard_map/ppermute | solution.py:45
  57.6 8.9 %collective-permute-start.2 = (bf16[256,320]{1,0:T(8,128)(2,1)S(1)}, bf16[256,320]{1,0:T(8,128)(2,1)S(1)}, u32[]{:S(2)}, u32[]{:S(2)}) collective-permute-start(bf16[256,320]{1,0:T(8,128)(2,1)S(1)} %collective-permute-done.1), channel_id=1, source_target_pairs={{0,44},{4,0},{8,4},{12,8},{16,12},{20,16},{24,20},{28,24},{32,28},... | collective-permute-start | bytes 491528 | tf_op jit(solution)/shard_map/ppermute | solution.py:48
  64.6 8.8 %collective-permute-start.8 = (bf16[256,320]{1,0:T(8,128)(2,1)S(1)}, bf16[256,320]{1,0:T(8,128)(2,1)S(1)}, u32[]{:S(2)}, u32[]{:S(2)}) collective-permute-start(bf16[256,320]{1,0:T(8,128)(2,1)S(1)} %collective-permute-done.7), channel_id=1, source_target_pairs={{0,4},{4,8},{8,12},{12,16},{16,20},{20,24},{24,28},{28,32},{32,36}... | collective-permute-start | bytes 491528 | tf_op jit(solution)/shard_map/ppermute | solution.py:45
  66.5 8.8 %collective-permute-start.3 = (bf16[256,320]{1,0:T(8,128)(2,1)S(1)}, bf16[256,320]{1,0:T(8,128)(2,1)}, u32[]{:S(2)}, u32[]{:S(2)}) collective-permute-start(bf16[256,320]{1,0:T(8,128)(2,1)S(1)} %collective-permute-done.2), channel_id=1, source_target_pairs={{0,44},{4,0},{8,4},{12,8},{16,12},{20,16},{24,20},{28,24},{32,28},... | collective-permute-start | bytes 491528 | tf_op jit(solution)/shard_map/ppermute | solution.py:48
  73.3 8.9 %collective-permute-start.9 = (bf16[256,320]{1,0:T(8,128)(2,1)S(1)}, bf16[256,320]{1,0:T(8,128)(2,1)}, u32[]{:S(2)}, u32[]{:S(2)}) collective-permute-start(bf16[256,320]{1,0:T(8,128)(2,1)S(1)} %collective-permute-done.8), channel_id=1, source_target_pairs={{0,4},{4,8},{8,12},{12,16},{16,20},{20,24},{24,28},{28,32},{32,36}... | collective-permute-start | bytes 491528 | tf_op jit(solution)/shard_map/ppermute | solution.py:45
  75.2 8.9 %collective-permute-start.4 = (bf16[256,320]{1,0:T(8,128)(2,1)}, bf16[256,320]{1,0:T(8,128)(2,1)}, u32[]{:S(2)}, u32[]{:S(2)}) collective-permute-start(bf16[256,320]{1,0:T(8,128)(2,1)} %collective-permute-done.3), channel_id=1, source_target_pairs={{0,44},{4,0},{8,4},{12,8},{16,12},{20,16},{24,20},{28,24},{32,28},... | collective-permute-start | bytes 491528 | tf_op jit(solution)/shard_map/ppermute | solution.py:48
  82.2 9.1 %collective-permute-start.10 = (bf16[256,320]{1,0:T(8,128)(2,1)}, bf16[256,320]{1,0:T(8,128)(2,1)}, u32[]{:S(2)}, u32[]{:S(2)}) collective-permute-start(bf16[256,320]{1,0:T(8,128)(2,1)} %collective-permute-done.9), channel_id=1, source_target_pairs={{0,4},{4,8},{8,12},{12,16},{16,20},{20,24},{24,28},{28,32},{32,36}... | collective-permute-start | bytes 491528 | tf_op jit(solution)/shard_map/ppermute | solution.py:45

commit v9 on v7

--- a/solution.py
+++ b/solution.py
@@ -32,17 +32,18 @@
     q = (n_rep - 1 - r) % n_rep
     skip = (jnp.arange(per_k) >= q)[:, None, None]
     b = jnp.where(skip, b[1:], b[:-1])
-    b = jnp.broadcast_to(b[None], (n_oy * n_oc,) + b.shape)
-    b = lax.all_to_all(b, ("oy", "oc"), split_axis=0, concat_axis=0, tiled=True)
-    b = b.reshape(n_virt, -1, nb)
-    b = lax.dynamic_slice_in_dim(jnp.concatenate([b, b], axis=0), v, n_virt, axis=0)
-
     fwd = [(i, (i + 1) % n_virt) for i in range(n_virt)]
     bwd = [(i, (i - 1) % n_virt) for i in range(n_virt)]
     ahead, behind = [], []
     f, g = a, a
     for s in range(1, n_virt // 2 + 1):
         f = lax.ppermute(f, "virt", fwd)
+        if s == 1:
+            f, b = lax.optimization_barrier((f, b))
+            b = jnp.broadcast_to(b[None], (n_oy * n_oc,) + b.shape)
+            b = lax.all_to_all(b, ("oy", "oc"), split_axis=0, concat_axis=0, tiled=True)
+            b = b.reshape(n_virt, -1, nb)
+            b = lax.dynamic_slice_in_dim(jnp.concatenate([b, b], axis=0), v, n_virt, axis=0)
         behind.append(f)
         if s < n_virt - s:
             g = lax.ppermute(g, "virt", bwd)

time: 106 us -> 110 us (1.038)
  waiting for transfers between devices: 15.8 us -> 21.4 us
  starting transfers between devices: 58.9 us -> 57.4 us
    ppermute x5, starting transfers between devices: 30.8 us -> 25.8 us  [local(): g = lax.ppermute(g, 'virt', bwd)]
    all_to_all x1, starting transfers between devices: 3.72 us -> 7.21 us  [local(): b = lax.all_to_all(b, ('oy', 'oc'), split_axis=0, concat_axis=0, tiled=True)]
    ppermute x6, waiting for transfers between devices: 10.9 us -> 13.8 us  [local(): f = lax.ppermute(f, 'virt', fwd)]
    ppermute x5, waiting for transfers between devices: 0.01 us -> 2.58 us  [local(): g = lax.ppermute(g, 'virt', bwd)]
  transfers between devices with their start and end apart: 13 -> 13, of which waited for: 7 -> 9; matrix products, arithmetic and copies ran while one was open for 8% -> 8% of each run, Pallas kernels for 0% -> 0%
where the time goes in v9:
time: 110 us; the launch traced here: 108 us
  starting transfers between devices  57.4 us (52%)
  waiting for transfers between devices  21.4 us (19%)
  local copies, waits for them, and re-layouts  14.7 us (13%)
  blocking collectives  9.06 us (8%)
  other arithmetic  3.08 us (3%)
  matrix products  2.55 us (2%)
    ppermute x5, starting transfers between devices, local(): g = lax.ppermute(g, 'virt', bwd)  25.8 us
    ppermute x6, waiting for transfers between devices, local(): f = lax.ppermute(f, 'virt', fwd)  13.8 us
    all_to_all x1, starting transfers between devices, local(): both = lax.all_to_all(both, 'rep', split_axis=0, concat_axis=0, tiled=True)  12.9 us
    ppermute x6, starting transfers between devices, local(): f = lax.ppermute(f, 'virt', fwd)  11.5 us
    unnamed x15, local copies, waits for them, and re-layouts  9.38 us
    all_to_all x1, blocking collectives, local(): lax.all_to_all(partial_sum, 'rep', split_axis=0, concat_axis=0, tiled=True)  9.06 us
    all_to_all x1, starting transfers between devices, local(): b = lax.all_to_all(b, ('oy', 'oc'), split_axis=0, concat_axis=0, tiled=True)  7.21 us
    all_to_all x1, waiting for transfers between devices, local(): both = lax.all_to_all(both, 'rep', split_axis=0, concat_axis=0, tiled=True)  4.95 us
  transfers between devices with their start and end apart: 13, of which 9 were waited for; matrix products, arithmetic and copies ran while one was open for 8% of the time, Pallas kernels for 0%

profile of v9, /device:TPU:6, one launch (start us, length us, event | category | flops | bytes accessed | tf_op | source)
XLA Modules:
  0.0 108.3 jit_solution(12320417260434842286)
XLA Ops:
  0.0 1.0 compare_select_fusion
  1.3 1.3 %reshape.30 = bf16[64,4,4,80]{3,2,1,0:T(4,128)(2,1)S(1)} reshape(bf16[64,1280]{1,0:T(8,128)(2,1)} %param.4) | data formatting | bytes 327680 | tf_op jit(solution)/shard_map/reshape | solution.py:20
  3.8 1.1 reduce
  4.8 1.1 %reshape.37 = bf16[4,2,20480]{2,1,0:T(2,128)(2,1)} reshape(bf16[4,40960]{1,0:T(4,128)(2,1)S(1)} %reduce) | data formatting | bytes 655360
  5.9 12.9 %all-to-all-start = ((bf16[4,2,20480]{2,1,0:T(2,128)(2,1)}), bf16[4,2,20480]{2,1,0:T(2,128)(2,1)S(1)}, u32[]{:S(2)}, u32[]{:S(2)}) async-start(bf16[4,2,20480]{2,1,0:T(2,128)(2,1)} %reshape.37), calls=%async_computation | async-start | bytes 655360 | tf_op jit(solution)/shard_map/all_to_all | solution.py:28
  18.8 5.0 %all-to-all-done = bf16[4,2,20480]{2,1,0:T(2,128)(2,1)S(1)} async-done(((bf16[4,2,20480]{2,1,0:T(2,128)(2,1)}), bf16[4,2,20480]{2,1,0:T(2,128)(2,1)S(1)}, u32[]{:S(2)}, u32[]{:S(2)}) %all-to-all-start) | async-done | bytes 327712 | tf_op jit(solution)/shard_map/all_to_all | solution.py:28
  25.1 1.9 %collective-permute-start.5 = (bf16[256,320]{0,1:T(8,128)(2,1)S(1)}, bf16[256,320]{0,1:T(8,128)(2,1)S(1)}, u32[]{:S(2)}, u32[]{:S(2)}) collective-permute-start(bf16[256,320]{0,1:T(8,128)(2,1)S(1)} %copy.16), channel_id=1, source_target_pairs={{0,4},{4,8},{8,12},{12,16},{16,20},{20,24},{24,28},{28,32},{32,36}... | collective-permute-start | bytes 491528 | tf_op jit(solution)/shard_map/ppermute | solution.py:40
  27.1 8.1 %collective-permute-done.5 = bf16[256,320]{0,1:T(8,128)(2,1)S(1)} collective-permute-done((bf16[256,320]{0,1:T(8,128)(2,1)S(1)}, bf16[256,320]{0,1:T(8,128)(2,1)S(1)}, u32[]{:S(2)}, u32[]{:S(2)}) %collective-permute-start.5) | collective-permute-done | bytes 163872 | tf_op jit(solution)/shard_map/ppermute | solution.py:40
  35.2 1.4 %broadcast_in_dim.26 = bf16[16,3,80,256]{3,2,1,0:T(8,128)(2,1)} broadcast(bf16[3,80,256]{2,1,0:T(8,128)(2,1)S(1)} %bitcast_select_fusion), dimensions={1,2,3} | broadcast | bytes 2088960 | tf_op jit(solution)/shard_map/broadcast_in_dim | solution.py:43
  36.6 7.2 %all-to-all-start.1 = ((bf16[16,3,80,256]{3,2,1,0:T(8,128)(2,1)}), bf16[16,3,80,256]{3,2,1,0:T(8,128)(2,1)S(1)}, u32[]{:S(2)}, u32[]{:S(2)}) async-start(bf16[16,3,80,256]{3,2,1,0:T(8,128)(2,1)} %broadcast_in_dim.26), calls=%async_computation.1 | async-start | bytes 3932160 | tf_op jit(solution)/shard_map/all_to_all | solution.py:44
  43.8 3.9 %collective-permute-start = (bf16[256,320]{0,1:T(8,128)(2,1)S(1)}, bf16[256,320]{0,1:T(8,128)(2,1)S(1)}, u32[]{:S(2)}, u32[]{:S(2)}) collective-permute-start(bf16[256,320]{0,1:T(8,128)(2,1)S(1)} %copy.16), channel_id=1, source_target_pairs={{0,44},{4,0},{8,4},{12,8},{16,12},{20,16},{24,20},{28,24},{32,28},... | collective-permute-start | bytes 491528 | tf_op jit(solution)/shard_map/ppermute | solution.py:49
  48.8 1.9 %collective-permute-start.6 = (bf16[256,320]{0,1:T(8,128)(2,1)S(1)}, bf16[256,320]{0,1:T(8,128)(2,1)S(1)}, u32[]{:S(2)}, u32[]{:S(2)}) collective-permute-start(bf16[256,320]{0,1:T(8,128)(2,1)S(1)} %collective-permute-done.5), channel_id=1, source_target_pairs={{0,4},{4,8},{8,12},{12,16},{16,20},{20,24},{24,28},{28,32},{32,36}... | collective-permute-start | bytes 491528 | tf_op jit(solution)/shard_map/ppermute | solution.py:40
  50.7 1.5 %collective-permute-done = bf16[256,320]{0,1:T(8,128)(2,1)S(1)} collective-permute-done((bf16[256,320]{0,1:T(8,128)(2,1)S(1)}, bf16[256,320]{0,1:T(8,128)(2,1)S(1)}, u32[]{:S(2)}, u32[]{:S(2)}) %collective-permute-start) | collective-permute-done | bytes 163872 | tf_op jit(solution)/shard_map/ppermute | solution.py:49
  52.2 5.1 %collective-permute-start.1 = (bf16[256,320]{0,1:T(8,128)(2,1)S(1)}, bf16[256,320]{0,1:T(8,128)(2,1)S(1)}, u32[]{:S(2)}, u32[]{:S(2)}) collective-permute-start(bf16[256,320]{0,1:T(8,128)(2,1)S(1)} %collective-permute-done), channel_id=1, source_target_pairs={{0,44},{4,0},{8,4},{12,8},{16,12},{20,16},{24,20},{28,24},{32,28},... | collective-permute-start | bytes 491528 | tf_op jit(solution)/shard_map/ppermute | solution.py:49
  58.1 1.9 %collective-permute-start.7 = (bf16[256,320]{0,1:T(8,128)(2,1)S(1)}, bf16[256,320]{0,1:T(8,128)(2,1)S(1)}, u32[]{:S(2)}, u32[]{:S(2)}) collective-permute-start(bf16[256,320]{0,1:T(8,128)(2,1)S(1)} %collective-permute-done.6), channel_id=1, source_target_pairs={{0,4},{4,8},{8,12},{12,16},{16,20},{20,24},{24,28},{28,32},{32,36}... | collective-permute-start | bytes 491528 | tf_op jit(solution)/shard_map/ppermute | solution.py:40
  60.5 5.6 %collective-permute-start.2 = (bf16[256,320]{0,1:T(8,128)(2,1)S(1)}, bf16[256,320]{0,1:T(8,128)(2,1)S(1)}, u32[]{:S(2)}, u32[]{:S(2)}) collective-permute-start(bf16[256,320]{0,1:T(8,128)(2,1)S(1)} %collective-permute-done.1), channel_id=1, source_target_pairs={{0,44},{4,0},{8,4},{12,8},{16,12},{20,16},{24,20},{28,24},{32,28},... | collective-permute-start | bytes 491528 | tf_op jit(solution)/shard_map/ppermute | solution.py:49
  66.8 1.9 %collective-permute-start.8 = (bf16[256,320]{0,1:T(8,128)(2,1)S(1)}, bf16[256,320]{0,1:T(8,128)(2,1)S(1)}, u32[]{:S(2)}, u32[]{:S(2)}) collective-permute-start(bf16[256,320]{0,1:T(8,128)(2,1)S(1)} %collective-permute-done.7), channel_id=1, source_target_pairs={{0,4},{4,8},{8,12},{12,16},{16,20},{20,24},{24,28},{28,32},{32,36}... | collective-permute-start | bytes 491528 | tf_op jit(solution)/shard_map/ppermute | solution.py:40
  68.9 5.6 %collective-permute-start.3 = (bf16[256,320]{0,1:T(8,128)(2,1)S(1)}, bf16[256,320]{0,1:T(8,128)(2,1)S(1)}, u32[]{:S(2)}, u32[]{:S(2)}) collective-permute-start(bf16[256,320]{0,1:T(8,128)(2,1)S(1)} %collective-permute-done.2), channel_id=1, source_target_pairs={{0,44},{4,0},{8,4},{12,8},{16,12},{20,16},{24,20},{28,24},{32,28},... | collective-permute-start | bytes 491528 | tf_op jit(solution)/shard_map/ppermute | solution.py:49
  75.2 1.9 %collective-permute-start.9 = (bf16[256,320]{0,1:T(8,128)(2,1)S(1)}, bf16[256,320]{0,1:T(8,128)(2,1)S(1)}, u32[]{:S(2)}, u32[]{:S(2)}) collective-permute-start(bf16[256,320]{0,1:T(8,128)(2,1)S(1)} %collective-permute-done.8), channel_id=1, source_target_pairs={{0,4},{4,8},{8,12},{12,16},{16,20},{20,24},{24,28},{28,32},{32,36}... | collective-permute-start | bytes 491528 | tf_op jit(solution)/shard_map/ppermute | solution.py:40
  77.3 5.6 %collective-permute-start.4 = (bf16[256,320]{0,1:T(8,128)(2,1)S(1)}, bf16[256,320]{0,1:T(8,128)(2,1)S(1)}, u32[]{:S(2)}, u32[]{:S(2)}) collective-permute-start(bf16[256,320]{0,1:T(8,128)(2,1)S(1)} %collective-permute-done.3), channel_id=1, source_target_pairs={{0,44},{4,0},{8,4},{12,8},{16,12},{20,16},{24,20},{28,24},{32,28},... | collective-permute-start | bytes 491528 | tf_op jit(solution)/shard_map/ppermute | solution.py:49
  83.6 1.9 %collective-permute-start.10 = (bf16[256,320]{0,1:T(8,128)(2,1)S(1)}, bf16[256,320]{0,1:T(8,128)(2,1)S(1)}, u32[]{:S(2)}, u32[]{:S(2)}) collective-permute-start(bf16[256,320]{0,1:T(8,128)(2,1)S(1)} %collective-permute-done.9), channel_id=1, source_target_pairs={{0,4},{4,8},{8,12},{12,16},{16,20},{20,24},{24,28},{28,32},{32,36}... | collective-permute-start | bytes 491528 | tf_op jit(solution)/shard_map/ppermute | solution.py:40
  86.4 5.6 %collective-permute-done.10 = bf16[256,320]{0,1:T(8,128)(2,1)S(1)} collective-permute-done((bf16[256,320]{0,1:T(8,128)(2,1)S(1)}, bf16[256,320]{0,1:T(8,128)(2,1)S(1)}, u32[]{:S(2)}, u32[]{:S(2)}) %collective-permute-start.10) | collective-permute-done | bytes 163872 | tf_op jit(solution)/shard_map/ppermute | solution.py:40
  96.1 2.5 %fusion.1 = f32[256,256,1]{1,0,2:T(8,128)S(1)} fusion(bf16[12,256,320]{1,2,0:T(8,128)(2,1)} %bitcast_dynamic-update-slice_fusion, s32[]{:T(128)S(6)} %select_n.25, bf16[12,320,256]{2,1,0:T(8,128)(2,1)S(1)} %bitcast.47), kind=kOutput, calls=%fused_computation.3 | convolution fusion | flops 504299520 | bytes 4194308 | tf_op jit(solution)/shard_map/vmc,vcn->mn/dot_general | solution.py:54
  98.6 9.1 %all_to_all.22 = f32[4,64,256]{2,1,0:T(8,128)S(1)} all-to-all(f32[4,64,256]{2,1,0:T(8,128)S(1)} %bitcast.53), channel_id=1, replica_groups=mesh['oy'=8,'oc'=2,'virt'=12,'rep'=4] {'rep'}, dimensions={0} | all-to-all | bytes 524288 | tf_op jit(solution)/shard_map/all_to_all | solution.py:56
  (39 shorter events, 13.1 us)
Async XLA Ops:
  5.9 17.8 %all-to-all-start = ((bf16[4,2,20480]{2,1,0:T(2,128)(2,1)}), bf16[4,2,20480]{2,1,0:T(2,128)(2,1)S(1)}, u32[]{:S(2)}, u32[]{:S(2)}) async-start(bf16[4,2,20480]{2,1,0:T(2,128)(2,1)} %reshape.37), calls=%async_computation | async-start | bytes 655360 | tf_op jit(solution)/shard_map/all_to_all | solution.py:28
  25.1 10.1 %collective-permute-start.5 = (bf16[256,320]{0,1:T(8,128)(2,1)S(1)}, bf16[256,320]{0,1:T(8,128)(2,1)S(1)}, u32[]{:S(2)}, u32[]{:S(2)}) collective-permute-start(bf16[256,320]{0,1:T(8,128)(2,1)S(1)} %copy.16), channel_id=1, source_target_pairs={{0,4},{4,8},{8,12},{12,16},{16,20},{20,24},{24,28},{28,32},{32,36}... | collective-permute-start | bytes 491528 | tf_op jit(solution)/shard_map/ppermute | solution.py:40
  36.6 59.5 %all-to-all-start.1 = ((bf16[16,3,80,256]{3,2,1,0:T(8,128)(2,1)}), bf16[16,3,80,256]{3,2,1,0:T(8,128)(2,1)S(1)}, u32[]{:S(2)}, u32[]{:S(2)}) async-start(bf16[16,3,80,256]{3,2,1,0:T(8,128)(2,1)} %broadcast_in_dim.26), calls=%async_computation.1 | async-start | bytes 3932160 | tf_op jit(solution)/shard_map/all_to_all | solution.py:44
  43.8 8.4 %collective-permute-start = (bf16[256,320]{0,1:T(8,128)(2,1)S(1)}, bf16[256,320]{0,1:T(8,128)(2,1)S(1)}, u32[]{:S(2)}, u32[]{:S(2)}) collective-permute-start(bf16[256,320]{0,1:T(8,128)(2,1)S(1)} %copy.16), channel_id=1, source_target_pairs={{0,44},{4,0},{8,4},{12,8},{16,12},{20,16},{24,20},{28,24},{32,28},... | collective-permute-start | bytes 491528 | tf_op jit(solution)/shard_map/ppermute | solution.py:49
  48.8 9.3 %collective-permute-start.6 = (bf16[256,320]{0,1:T(8,128)(2,1)S(1)}, bf16[256,320]{0,1:T(8,128)(2,1)S(1)}, u32[]{:S(2)}, u32[]{:S(2)}) collective-permute-start(bf16[256,320]{0,1:T(8,128)(2,1)S(1)} %collective-permute-done.5), channel_id=1, source_target_pairs={{0,4},{4,8},{8,12},{12,16},{16,20},{20,24},{24,28},{28,32},{32,36}... | collective-permute-start | bytes 491528 | tf_op jit(solution)/shard_map/ppermute | solution.py:40
  52.2 8.3 %collective-permute-start.1 = (bf16[256,320]{0,1:T(8,128)(2,1)S(1)}, bf16[256,320]{0,1:T(8,128)(2,1)S(1)}, u32[]{:S(2)}, u32[]{:S(2)}) collective-permute-start(bf16[256,320]{0,1:T(8,128)(2,1)S(1)} %collective-permute-done), channel_id=1, source_target_pairs={{0,44},{4,0},{8,4},{12,8},{16,12},{20,16},{24,20},{28,24},{32,28},... | collective-permute-start | bytes 491528 | tf_op jit(solution)/shard_map/ppermute | solution.py:49
  58.1 8.7 %collective-permute-start.7 = (bf16[256,320]{0,1:T(8,128)(2,1)S(1)}, bf16[256,320]{0,1:T(8,128)(2,1)S(1)}, u32[]{:S(2)}, u32[]{:S(2)}) collective-permute-start(bf16[256,320]{0,1:T(8,128)(2,1)S(1)} %collective-permute-done.6), channel_id=1, source_target_pairs={{0,4},{4,8},{8,12},{12,16},{16,20},{20,24},{24,28},{28,32},{32,36}... | collective-permute-start | bytes 491528 | tf_op jit(solution)/shard_map/ppermute | solution.py:40
  60.5 8.4 %collective-permute-start.2 = (bf16[256,320]{0,1:T(8,128)(2,1)S(1)}, bf16[256,320]{0,1:T(8,128)(2,1)S(1)}, u32[]{:S(2)}, u32[]{:S(2)}) collective-permute-start(bf16[256,320]{0,1:T(8,128)(2,1)S(1)} %collective-permute-done.1), channel_id=1, source_target_pairs={{0,44},{4,0},{8,4},{12,8},{16,12},{20,16},{24,20},{28,24},{32,28},... | collective-permute-start | bytes 491528 | tf_op jit(solution)/shard_map/ppermute | solution.py:49
  66.8 8.4 %collective-permute-start.8 = (bf16[256,320]{0,1:T(8,128)(2,1)S(1)}, bf16[256,320]{0,1:T(8,128)(2,1)S(1)}, u32[]{:S(2)}, u32[]{:S(2)}) collective-permute-start(bf16[256,320]{0,1:T(8,128)(2,1)S(1)} %collective-permute-done.7), channel_id=1, source_target_pairs={{0,4},{4,8},{8,12},{12,16},{16,20},{20,24},{24,28},{28,32},{32,36}... | collective-permute-start | bytes 491528 | tf_op jit(solution)/shard_map/ppermute | solution.py:40
  68.9 8.4 %collective-permute-start.3 = (bf16[256,320]{0,1:T(8,128)(2,1)S(1)}, bf16[256,320]{0,1:T(8,128)(2,1)S(1)}, u32[]{:S(2)}, u32[]{:S(2)}) collective-permute-start(bf16[256,320]{0,1:T(8,128)(2,1)S(1)} %collective-permute-done.2), channel_id=1, source_target_pairs={{0,44},{4,0},{8,4},{12,8},{16,12},{20,16},{24,20},{28,24},{32,28},... | collective-permute-start | bytes 491528 | tf_op jit(solution)/shard_map/ppermute | solution.py:49
  75.2 8.4 %collective-permute-start.9 = (bf16[256,320]{0,1:T(8,128)(2,1)S(1)}, bf16[256,320]{0,1:T(8,128)(2,1)S(1)}, u32[]{:S(2)}, u32[]{:S(2)}) collective-permute-start(bf16[256,320]{0,1:T(8,128)(2,1)S(1)} %collective-permute-done.8), channel_id=1, source_target_pairs={{0,4},{4,8},{8,12},{12,16},{16,20},{20,24},{24,28},{28,32},{32,36}... | collective-permute-start | bytes 491528 | tf_op jit(solution)/shard_map/ppermute | solution.py:40
  77.3 8.4 %collective-permute-start.4 = (bf16[256,320]{0,1:T(8,128)(2,1)S(1)}, bf16[256,320]{0,1:T(8,128)(2,1)S(1)}, u32[]{:S(2)}, u32[]{:S(2)}) collective-permute-start(bf16[256,320]{0,1:T(8,128)(2,1)S(1)} %collective-permute-done.3), channel_id=1, source_target_pairs={{0,44},{4,0},{8,4},{12,8},{16,12},{20,16},{24,20},{28,24},{32,28},... | collective-permute-start | bytes 491528 | tf_op jit(solution)/shard_map/ppermute | solution.py:49
  83.6 8.4 %collective-permute-start.10 = (bf16[256,320]{0,1:T(8,128)(2,1)S(1)}, bf16[256,320]{0,1:T(8,128)(2,1)S(1)}, u32[]{:S(2)}, u32[]{:S(2)}) collective-permute-start(bf16[256,320]{0,1:T(8,128)(2,1)S(1)} %collective-permute-done.9), channel_id=1, source_target_pairs={{0,4},{4,8},{8,12},{12,16},{16,20},{20,24},{24,28},{28,32},{32,36}... | collective-permute-start | bytes 491528 | tf_op jit(solution)/shard_map/ppermute | solution.py:40

commit v10 on v7

--- a/solution.py
+++ b/solution.py
@@ -39,16 +39,16 @@
 
     fwd = [(i, (i + 1) % n_virt) for i in range(n_virt)]
     bwd = [(i, (i - 1) % n_virt) for i in range(n_virt)]
-    ahead, behind = [], []
+    stack = jnp.zeros((n_virt,) + a.shape, a.dtype).at[0].set(a)
     f, g = a, a
     for s in range(1, n_virt // 2 + 1):
         f = lax.ppermute(f, "virt", fwd)
-        behind.append(f)
+        stack = stack.at[n_virt - s].set(f)
         if s < n_virt - s:
             g = lax.ppermute(g, "virt", bwd)
-            ahead.append(g)
-    pieces = [a] + ahead + behind[::-1]
-    a = jnp.stack(pieces, axis=0)
+            stack = stack.at[s].set(g)
+        stack, f, g = lax.optimization_barrier((stack, f, g))
+    a = stack
 
     partial_sum = jnp.einsum("vmc,vcn->mn", a, b, preferred_element_type=jnp.float32)
     partial_sum = partial_sum.reshape(n_rep, rows, nb)

time: 106 us -> 115 us (1.085)
  waiting for transfers between devices: 15.8 us -> 28.2 us
  local copies, waits for them, and re-layouts: 14.7 us -> 6.86 us
  starting transfers between devices: 58.9 us -> 62.6 us
    unnamed x15 -> x4, local copies, waits for them, and re-layouts: 9.38 us -> 1.93 us
    ppermute x5, waiting for transfers between devices: 0.01 us -> 6.5 us  [local(): g = lax.ppermute(g, 'virt', bwd)]
    ppermute x6, waiting for transfers between devices: 10.9 us -> 16.7 us  [local(): f = lax.ppermute(f, 'virt', fwd)]
    ppermute x6, starting transfers between devices: 11.5 us -> 13.8 us  [local(): f = lax.ppermute(f, 'virt', fwd)]
  transfers between devices with their start and end apart: 13 -> 13, of which waited for: 7 -> 12; matrix products, arithmetic and copies ran while one was open for 8% -> 1% of each run, Pallas kernels for 0% -> 0%
where the time goes in v10:
time: 115 us; the launch traced here: 113 us
  starting transfers between devices  62.6 us (54%)
  waiting for transfers between devices  28.2 us (25%)
  blocking collectives  9.06 us (8%)
  local copies, waits for them, and re-layouts  6.86 us (6%)
  other arithmetic  3.08 us (3%)
  matrix products  2.7 us (2%)
    ppermute x5, starting transfers between devices, local(): g = lax.ppermute(g, 'virt', bwd)  31.5 us
    ppermute x6, waiting for transfers between devices, local(): f = lax.ppermute(f, 'virt', fwd)  16.7 us
    ppermute x6, starting transfers between devices, local(): f = lax.ppermute(f, 'virt', fwd)  13.8 us
    all_to_all x1, starting transfers between devices, local(): both = lax.all_to_all(both, 'rep', split_axis=0, concat_axis=0, tiled=True)  12.9 us
    all_to_all x1, blocking collectives, local(): lax.all_to_all(partial_sum, 'rep', split_axis=0, concat_axis=0, tiled=True)  9.06 us
    ppermute x5, waiting for transfers between devices, local(): g = lax.ppermute(g, 'virt', bwd)  6.5 us
    all_to_all x1, waiting for transfers between devices, local(): both = lax.all_to_all(both, 'rep', split_axis=0, concat_axis=0, tiled=True)  4.95 us
    all_to_all x1, starting transfers between devices, local(): b = lax.all_to_all(b, ('oy', 'oc'), split_axis=0, concat_axis=0, tiled=True)  4.42 us
  transfers between devices with their start and end apart: 13, of which 12 were waited for; matrix products, arithmetic and copies ran while one was open for 1% of the time, Pallas kernels for 0%

profile of v10, /device:TPU:6, one launch (start us, length us, event | category | flops | bytes accessed | tf_op | source)
XLA Modules:
  0.0 112.7 jit_solution(7912540965462101476)
XLA Ops:
  5.9 12.9 %all-to-all-start = ((bf16[4,2,20480]{2,1,0:T(2,128)(2,1)}), bf16[4,2,20480]{2,1,0:T(2,128)(2,1)S(1)}, u32[]{:S(2)}, u32[]{:S(2)}) async-start(bf16[4,2,20480]{2,1,0:T(2,128)(2,1)} %reshape.412), calls=%async_computation | async-start | bytes 655360 | tf_op jit(solution)/shard_map/all_to_all | solution.py:28
  18.8 5.0 %all-to-all-done = bf16[4,2,20480]{2,1,0:T(2,128)(2,1)S(1)} async-done(((bf16[4,2,20480]{2,1,0:T(2,128)(2,1)}), bf16[4,2,20480]{2,1,0:T(2,128)(2,1)S(1)}, u32[]{:S(2)}, u32[]{:S(2)}) %all-to-all-start) | async-done | bytes 327712 | tf_op jit(solution)/shard_map/all_to_all | solution.py:28
  26.1 4.4 %all-to-all-start.1 = ((bf16[16,3,80,256]{3,2,1,0:T(8,128)(2,1)}), bf16[16,3,80,256]{3,2,1,0:T(8,128)(2,1)}, u32[]{:S(2)}, u32[]{:S(2)}) async-start(bf16[16,3,80,256]{3,2,1,0:T(8,128)(2,1)} %broadcast_in_dim.27), calls=%async_computation.1 | async-start | bytes 3932160 | tf_op jit(solution)/shard_map/all_to_all | solution.py:36
  30.9 1.9 %collective-permute-start = (bf16[256,320]{1,0:T(8,128)(2,1)S(1)}, bf16[256,320]{1,0:T(8,128)(2,1)S(1)}, u32[]{:S(2)}, u32[]{:S(2)}) collective-permute-start(bf16[256,320]{1,0:T(8,128)(2,1)S(1)} %reshape.397), channel_id=1, source_target_pairs={{0,4},{4,8},{8,12},{12,16},{16,20},{20,24},{24,28},{28,32},{32,36}... | collective-permute-start | bytes 491528 | tf_op jit(solution)/shard_map/ppermute | solution.py:45
  33.0 9.6 %collective-permute-start.1 = (bf16[256,320]{1,0:T(8,128)(2,1)S(1)}, bf16[256,320]{1,0:T(8,128)(2,1)S(1)}, u32[]{:S(2)}, u32[]{:S(2)}) collective-permute-start(bf16[256,320]{1,0:T(8,128)(2,1)S(1)} %reshape.397), channel_id=1, source_target_pairs={{0,44},{4,0},{8,4},{12,8},{16,12},{20,16},{24,20},{28,24},{32,28},... | collective-permute-start | bytes 491528 | tf_op jit(solution)/shard_map/ppermute | solution.py:48
  42.9 3.0 %collective-permute-done = bf16[256,320]{1,0:T(8,128)(2,1)S(1)} collective-permute-done((bf16[256,320]{1,0:T(8,128)(2,1)S(1)}, bf16[256,320]{1,0:T(8,128)(2,1)S(1)}, u32[]{:S(2)}, u32[]{:S(2)}) %collective-permute-start) | collective-permute-done | bytes 163872 | tf_op jit(solution)/shard_map/ppermute | solution.py:45
  47.3 1.9 %collective-permute-start.2 = (bf16[256,320]{1,0:T(8,128)(2,1)S(1)}, bf16[256,320]{1,0:T(8,128)(2,1)S(1)}, u32[]{:S(2)}, u32[]{:S(2)}) collective-permute-start(bf16[256,320]{1,0:T(8,128)(2,1)S(1)} %collective-permute-done), channel_id=1, source_target_pairs={{0,4},{4,8},{8,12},{12,16},{16,20},{20,24},{24,28},{28,32},{32,36}... | collective-permute-start | bytes 491528 | tf_op jit(solution)/shard_map/ppermute | solution.py:45
  49.3 5.6 %collective-permute-start.3 = (bf16[256,320]{1,0:T(8,128)(2,1)S(1)}, bf16[256,320]{1,0:T(8,128)(2,1)S(1)}, u32[]{:S(2)}, u32[]{:S(2)}) collective-permute-start(bf16[256,320]{1,0:T(8,128)(2,1)S(1)} %collective-permute-done.1), channel_id=1, source_target_pairs={{0,44},{4,0},{8,4},{12,8},{16,12},{20,16},{24,20},{28,24},{32,28},... | collective-permute-start | bytes 491528 | tf_op jit(solution)/shard_map/ppermute | solution.py:48
  54.9 2.7 %collective-permute-done.2 = bf16[256,320]{1,0:T(8,128)(2,1)S(1)} collective-permute-done((bf16[256,320]{1,0:T(8,128)(2,1)S(1)}, bf16[256,320]{1,0:T(8,128)(2,1)S(1)}, u32[]{:S(2)}, u32[]{:S(2)}) %collective-permute-start.2) | collective-permute-done | bytes 163872 | tf_op jit(solution)/shard_map/ppermute | solution.py:45
  58.8 1.9 %collective-permute-start.4 = (bf16[256,320]{1,0:T(8,128)(2,1)S(1)}, bf16[256,320]{1,0:T(8,128)(2,1)S(1)}, u32[]{:S(2)}, u32[]{:S(2)}) collective-permute-start(bf16[256,320]{1,0:T(8,128)(2,1)S(1)} %collective-permute-done.2), channel_id=1, source_target_pairs={{0,4},{4,8},{8,12},{12,16},{16,20},{20,24},{24,28},{28,32},{32,36}... | collective-permute-start | bytes 491528 | tf_op jit(solution)/shard_map/ppermute | solution.py:45
  60.7 5.6 %collective-permute-start.5 = (bf16[256,320]{1,0:T(8,128)(2,1)S(1)}, bf16[256,320]{1,0:T(8,128)(2,1)S(1)}, u32[]{:S(2)}, u32[]{:S(2)}) collective-permute-start(bf16[256,320]{1,0:T(8,128)(2,1)S(1)} %collective-permute-done.3), channel_id=1, source_target_pairs={{0,44},{4,0},{8,4},{12,8},{16,12},{20,16},{24,20},{28,24},{32,28},... | collective-permute-start | bytes 491528 | tf_op jit(solution)/shard_map/ppermute | solution.py:48
  66.4 2.0 %collective-permute-done.4 = bf16[256,320]{1,0:T(8,128)(2,1)S(1)} collective-permute-done((bf16[256,320]{1,0:T(8,128)(2,1)S(1)}, bf16[256,320]{1,0:T(8,128)(2,1)S(1)}, u32[]{:S(2)}, u32[]{:S(2)}) %collective-permute-start.4) | collective-permute-done | bytes 163872 | tf_op jit(solution)/shard_map/ppermute | solution.py:45
  69.6 1.9 %collective-permute-start.6 = (bf16[256,320]{1,0:T(8,128)(2,1)S(1)}, bf16[256,320]{1,0:T(8,128)(2,1)S(1)}, u32[]{:S(2)}, u32[]{:S(2)}) collective-permute-start(bf16[256,320]{1,0:T(8,128)(2,1)S(1)} %collective-permute-done.4), channel_id=1, source_target_pairs={{0,4},{4,8},{8,12},{12,16},{16,20},{20,24},{24,28},{28,32},{32,36}... | collective-permute-start | bytes 491528 | tf_op jit(solution)/shard_map/ppermute | solution.py:45
  71.5 5.6 %collective-permute-start.7 = (bf16[256,320]{1,0:T(8,128)(2,1)S(1)}, bf16[256,320]{1,0:T(8,128)(2,1)S(1)}, u32[]{:S(2)}, u32[]{:S(2)}) collective-permute-start(bf16[256,320]{1,0:T(8,128)(2,1)S(1)} %collective-permute-done.5), channel_id=1, source_target_pairs={{0,44},{4,0},{8,4},{12,8},{16,12},{20,16},{24,20},{28,24},{32,28},... | collective-permute-start | bytes 491528 | tf_op jit(solution)/shard_map/ppermute | solution.py:48
  77.1 1.7 %collective-permute-done.6 = bf16[256,320]{1,0:T(8,128)(2,1)S(1)} collective-permute-done((bf16[256,320]{1,0:T(8,128)(2,1)S(1)}, bf16[256,320]{1,0:T(8,128)(2,1)S(1)}, u32[]{:S(2)}, u32[]{:S(2)}) %collective-permute-start.6) | collective-permute-done | bytes 163872 | tf_op jit(solution)/shard_map/ppermute | solution.py:45
  78.8 1.4 %collective-permute-done.7 = bf16[256,320]{1,0:T(8,128)(2,1)S(1)} collective-permute-done((bf16[256,320]{1,0:T(8,128)(2,1)S(1)}, bf16[256,320]{1,0:T(8,128)(2,1)S(1)}, u32[]{:S(2)}, u32[]{:S(2)}) %collective-permute-start.7) | collective-permute-done | bytes 163872 | tf_op jit(solution)/shard_map/ppermute | solution.py:48
  80.3 2.5 %collective-permute-start.8 = (bf16[256,320]{1,0:T(8,128)(2,1)S(1)}, bf16[256,320]{1,0:T(8,128)(2,1)S(1)}, u32[]{:S(2)}, u32[]{:S(2)}) collective-permute-start(bf16[256,320]{1,0:T(8,128)(2,1)S(1)} %collective-permute-done.6), channel_id=1, source_target_pairs={{0,4},{4,8},{8,12},{12,16},{16,20},{20,24},{24,28},{28,32},{32,36}... | collective-permute-start | bytes 491528 | tf_op jit(solution)/shard_map/ppermute | solution.py:45
  82.8 5.1 %collective-permute-start.9 = (bf16[256,320]{1,0:T(8,128)(2,1)S(1)}, bf16[256,320]{1,0:T(8,128)(2,1)S(1)}, u32[]{:S(2)}, u32[]{:S(2)}) collective-permute-start(bf16[256,320]{1,0:T(8,128)(2,1)S(1)} %collective-permute-done.7), channel_id=1, source_target_pairs={{0,44},{4,0},{8,4},{12,8},{16,12},{20,16},{24,20},{28,24},{32,28},... | collective-permute-start | bytes 491528 | tf_op jit(solution)/shard_map/ppermute | solution.py:48
  87.8 1.7 %collective-permute-done.8 = bf16[256,320]{1,0:T(8,128)(2,1)S(1)} collective-permute-done((bf16[256,320]{1,0:T(8,128)(2,1)S(1)}, bf16[256,320]{1,0:T(8,128)(2,1)S(1)}, u32[]{:S(2)}, u32[]{:S(2)}) %collective-permute-start.8) | collective-permute-done | bytes 163872 | tf_op jit(solution)/shard_map/ppermute | solution.py:45
  89.6 1.4 %collective-permute-done.9 = bf16[256,320]{1,0:T(8,128)(2,1)S(1)} collective-permute-done((bf16[256,320]{1,0:T(8,128)(2,1)S(1)}, bf16[256,320]{1,0:T(8,128)(2,1)S(1)}, u32[]{:S(2)}, u32[]{:S(2)}) %collective-permute-start.9) | collective-permute-done | bytes 163872 | tf_op jit(solution)/shard_map/ppermute | solution.py:48
  91.0 3.6 %collective-permute-start.10 = (bf16[256,320]{1,0:T(8,128)(2,1)S(1)}, bf16[256,320]{1,0:T(8,128)(2,1)S(1)}, u32[]{:S(2)}, u32[]{:S(2)}) collective-permute-start(bf16[256,320]{1,0:T(8,128)(2,1)S(1)} %collective-permute-done.8), channel_id=1, source_target_pairs={{0,4},{4,8},{8,12},{12,16},{16,20},{20,24},{24,28},{28,32},{32,36}... | collective-permute-start | bytes 491528 | tf_op jit(solution)/shard_map/ppermute | solution.py:45
  94.7 5.6 %collective-permute-done.10 = bf16[256,320]{1,0:T(8,128)(2,1)S(1)} collective-permute-done((bf16[256,320]{1,0:T(8,128)(2,1)S(1)}, bf16[256,320]{1,0:T(8,128)(2,1)S(1)}, u32[]{:S(2)}, u32[]{:S(2)}) %collective-permute-start.10) | collective-permute-done | bytes 163872 | tf_op jit(solution)/shard_map/ppermute | solution.py:45
  100.3 2.7 %fusion.1 = f32[256,256,1]{1,0,2:T(8,128)S(1)} fusion(bf16[12,256,320]{2,1,0:T(8,128)(2,1)S(1)} %bitcast_dynamic-update-slice_fusion, s32[]{:T(128)S(6)} %select_n.29, bf16[12,320,256]{2,1,0:T(8,128)(2,1)} %bitcast.14), kind=kOutput, calls=%fused_computation.3 | convolution fusion | flops 504299520 | bytes 4194308 | tf_op jit(solution)/shard_map/vmc,vcn->mn/dot_general | solution.py:53
  103.0 9.1 %all_to_all.22 = f32[4,64,256]{2,1,0:T(8,128)S(1)} all-to-all(f32[4,64,256]{2,1,0:T(8,128)S(1)} %bitcast.52), channel_id=1, replica_groups=mesh['oy'=8,'oc'=2,'virt'=12,'rep'=4] {'rep'}, dimensions={0} | all-to-all | bytes 524288 | tf_op jit(solution)/shard_map/all_to_all | solution.py:55
  (37 shorter events, 13.6 us)
Async XLA Ops:
  5.9 17.8 %all-to-all-start = ((bf16[4,2,20480]{2,1,0:T(2,128)(2,1)}), bf16[4,2,20480]{2,1,0:T(2,128)(2,1)S(1)}, u32[]{:S(2)}, u32[]{:S(2)}) async-start(bf16[4,2,20480]{2,1,0:T(2,128)(2,1)} %reshape.412), calls=%async_computation | async-start | bytes 655360 | tf_op jit(solution)/shard_map/all_to_all | solution.py:28
  26.1 74.2 %all-to-all-start.1 = ((bf16[16,3,80,256]{3,2,1,0:T(8,128)(2,1)}), bf16[16,3,80,256]{3,2,1,0:T(8,128)(2,1)}, u32[]{:S(2)}, u32[]{:S(2)}) async-start(bf16[16,3,80,256]{3,2,1,0:T(8,128)(2,1)} %broadcast_in_dim.27), calls=%async_computation.1 | async-start | bytes 3932160 | tf_op jit(solution)/shard_map/all_to_all | solution.py:36
  30.9 15.1 %collective-permute-start = (bf16[256,320]{1,0:T(8,128)(2,1)S(1)}, bf16[256,320]{1,0:T(8,128)(2,1)S(1)}, u32[]{:S(2)}, u32[]{:S(2)}) collective-permute-start(bf16[256,320]{1,0:T(8,128)(2,1)S(1)} %reshape.397), channel_id=1, source_target_pairs={{0,4},{4,8},{8,12},{12,16},{16,20},{20,24},{24,28},{28,32},{32,36}... | collective-permute-start | bytes 491528 | tf_op jit(solution)/shard_map/ppermute | solution.py:45
  33.0 14.3 %collective-permute-start.1 = (bf16[256,320]{1,0:T(8,128)(2,1)S(1)}, bf16[256,320]{1,0:T(8,128)(2,1)S(1)}, u32[]{:S(2)}, u32[]{:S(2)}) collective-permute-start(bf16[256,320]{1,0:T(8,128)(2,1)S(1)} %reshape.397), channel_id=1, source_target_pairs={{0,44},{4,0},{8,4},{12,8},{16,12},{20,16},{24,20},{28,24},{32,28},... | collective-permute-start | bytes 491528 | tf_op jit(solution)/shard_map/ppermute | solution.py:48
  47.3 10.3 %collective-permute-start.2 = (bf16[256,320]{1,0:T(8,128)(2,1)S(1)}, bf16[256,320]{1,0:T(8,128)(2,1)S(1)}, u32[]{:S(2)}, u32[]{:S(2)}) collective-permute-start(bf16[256,320]{1,0:T(8,128)(2,1)S(1)} %collective-permute-done), channel_id=1, source_target_pairs={{0,4},{4,8},{8,12},{12,16},{16,20},{20,24},{24,28},{28,32},{32,36}... | collective-permute-start | bytes 491528 | tf_op jit(solution)/shard_map/ppermute | solution.py:45
  49.3 9.5 %collective-permute-start.3 = (bf16[256,320]{1,0:T(8,128)(2,1)S(1)}, bf16[256,320]{1,0:T(8,128)(2,1)S(1)}, u32[]{:S(2)}, u32[]{:S(2)}) collective-permute-start(bf16[256,320]{1,0:T(8,128)(2,1)S(1)} %collective-permute-done.1), channel_id=1, source_target_pairs={{0,44},{4,0},{8,4},{12,8},{16,12},{20,16},{24,20},{28,24},{32,28},... | collective-permute-start | bytes 491528 | tf_op jit(solution)/shard_map/ppermute | solution.py:48
  58.8 9.5 %collective-permute-start.4 = (bf16[256,320]{1,0:T(8,128)(2,1)S(1)}, bf16[256,320]{1,0:T(8,128)(2,1)S(1)}, u32[]{:S(2)}, u32[]{:S(2)}) collective-permute-start(bf16[256,320]{1,0:T(8,128)(2,1)S(1)} %collective-permute-done.2), channel_id=1, source_target_pairs={{0,4},{4,8},{8,12},{12,16},{16,20},{20,24},{24,28},{28,32},{32,36}... | collective-permute-start | bytes 491528 | tf_op jit(solution)/shard_map/ppermute | solution.py:45
  60.7 8.8 %collective-permute-start.5 = (bf16[256,320]{1,0:T(8,128)(2,1)S(1)}, bf16[256,320]{1,0:T(8,128)(2,1)S(1)}, u32[]{:S(2)}, u32[]{:S(2)}) collective-permute-start(bf16[256,320]{1,0:T(8,128)(2,1)S(1)} %collective-permute-done.3), channel_id=1, source_target_pairs={{0,44},{4,0},{8,4},{12,8},{16,12},{20,16},{24,20},{28,24},{32,28},... | collective-permute-start | bytes 491528 | tf_op jit(solution)/shard_map/ppermute | solution.py:48
  69.6 9.2 %collective-permute-start.6 = (bf16[256,320]{1,0:T(8,128)(2,1)S(1)}, bf16[256,320]{1,0:T(8,128)(2,1)S(1)}, u32[]{:S(2)}, u32[]{:S(2)}) collective-permute-start(bf16[256,320]{1,0:T(8,128)(2,1)S(1)} %collective-permute-done.4), channel_id=1, source_target_pairs={{0,4},{4,8},{8,12},{12,16},{16,20},{20,24},{24,28},{28,32},{32,36}... | collective-permute-start | bytes 491528 | tf_op jit(solution)/shard_map/ppermute | solution.py:45
  71.5 8.8 %collective-permute-start.7 = (bf16[256,320]{1,0:T(8,128)(2,1)S(1)}, bf16[256,320]{1,0:T(8,128)(2,1)S(1)}, u32[]{:S(2)}, u32[]{:S(2)}) collective-permute-start(bf16[256,320]{1,0:T(8,128)(2,1)S(1)} %collective-permute-done.5), channel_id=1, source_target_pairs={{0,44},{4,0},{8,4},{12,8},{16,12},{20,16},{24,20},{28,24},{32,28},... | collective-permute-start | bytes 491528 | tf_op jit(solution)/shard_map/ppermute | solution.py:48
  80.3 9.2 %collective-permute-start.8 = (bf16[256,320]{1,0:T(8,128)(2,1)S(1)}, bf16[256,320]{1,0:T(8,128)(2,1)S(1)}, u32[]{:S(2)}, u32[]{:S(2)}) collective-permute-start(bf16[256,320]{1,0:T(8,128)(2,1)S(1)} %collective-permute-done.6), channel_id=1, source_target_pairs={{0,4},{4,8},{8,12},{12,16},{16,20},{20,24},{24,28},{28,32},{32,36}... | collective-permute-start | bytes 491528 | tf_op jit(solution)/shard_map/ppermute | solution.py:45
  82.8 8.2 %collective-permute-start.9 = (bf16[256,320]{1,0:T(8,128)(2,1)S(1)}, bf16[256,320]{1,0:T(8,128)(2,1)S(1)}, u32[]{:S(2)}, u32[]{:S(2)}) collective-permute-start(bf16[256,320]{1,0:T(8,128)(2,1)S(1)} %collective-permute-done.7), channel_id=1, source_target_pairs={{0,44},{4,0},{8,4},{12,8},{16,12},{20,16},{24,20},{28,24},{32,28},... | collective-permute-start | bytes 491528 | tf_op jit(solution)/shard_map/ppermute | solution.py:48
  91.0 9.2 %collective-permute-start.10 = (bf16[256,320]{1,0:T(8,128)(2,1)S(1)}, bf16[256,320]{1,0:T(8,128)(2,1)S(1)}, u32[]{:S(2)}, u32[]{:S(2)}) collective-permute-start(bf16[256,320]{1,0:T(8,128)(2,1)S(1)} %collective-permute-done.8), channel_id=1, source_target_pairs={{0,4},{4,8},{8,12},{12,16},{16,20},{20,24},{24,28},{28,32},{32,36}... | collective-permute-start | bytes 491528 | tf_op jit(solution)/shard_map/ppermute | solution.py:45

commit v11 on v7

--- a/solution.py
+++ b/solution.py
@@ -42,6 +42,12 @@
     ahead, behind = [], []
     f, g = a, a
     for s in range(1, n_virt // 2 + 1):
+        if s % 2 == 0 and s < n_virt - s:
+            g, f = lax.optimization_barrier((lax.ppermute(g, "virt", bwd), f))
+            ahead.append(g)
+            f = lax.ppermute(f, "virt", fwd)
+            behind.append(f)
+            continue
         f = lax.ppermute(f, "virt", fwd)
         behind.append(f)
         if s < n_virt - s:

time: 106 us -> 116 us (1.094)
  waiting for transfers between devices: 15.8 us -> 24.3 us
  starting transfers between devices: 58.9 us -> 60.3 us
    ppermute x0 -> x2, starting transfers between devices: none -> 10.7 us  [local(): g, f = lax.optimization_barrier((lax.ppermute(g, 'virt', bwd), f))]
    ppermute x5 -> x3, starting transfers between devices: 30.8 us -> 21.5 us  [local(): g = lax.ppermute(g, 'virt', bwd)]
    ppermute x0 -> x2, waiting for transfers between devices: none -> 3.56 us  [local(): g, f = lax.optimization_barrier((lax.ppermute(g, 'virt', bwd), f))]
    ppermute x6, waiting for transfers between devices: 10.9 us -> 13.7 us  [local(): f = lax.ppermute(f, 'virt', fwd)]
    ppermute x5 -> x3, waiting for transfers between devices: 0.01 us -> 2.08 us  [local(): g = lax.ppermute(g, 'virt', bwd)]
  transfers between devices with their start and end apart: 13 -> 13, of which waited for: 7 -> 9; matrix products, arithmetic and copies ran while one was open for 8% -> 8% of each run, Pallas kernels for 0% -> 0%
where the time goes in v11:
time: 116 us; the launch traced here: 114 us
  starting transfers between devices  60.3 us (52%)
  waiting for transfers between devices  24.3 us (21%)
  local copies, waits for them, and re-layouts  14.7 us (13%)
  blocking collectives  9.06 us (8%)
  other arithmetic  3.08 us (3%)
  matrix products  2.54 us (2%)
    ppermute x3, starting transfers between devices, local(): g = lax.ppermute(g, 'virt', bwd)  21.5 us
    ppermute x6, waiting for transfers between devices, local(): f = lax.ppermute(f, 'virt', fwd)  13.7 us
    all_to_all x1, starting transfers between devices, local(): both = lax.all_to_all(both, 'rep', split_axis=0, concat_axis=0, tiled=True)  12.9 us
    ppermute x6, starting transfers between devices, local(): f = lax.ppermute(f, 'virt', fwd)  11.5 us
    ppermute x2, starting transfers between devices, local(): g, f = lax.optimization_barrier((lax.ppermute(g, 'virt', bwd), f))  10.7 us
    unnamed x15, local copies, waits for them, and re-layouts  9.38 us
    all_to_all x1, blocking collectives, local(): lax.all_to_all(partial_sum, 'rep', split_axis=0, concat_axis=0, tiled=True)  9.06 us
    all_to_all x1, waiting for transfers between devices, local(): both = lax.all_to_all(both, 'rep', split_axis=0, concat_axis=0, tiled=True)  4.95 us
  transfers between devices with their start and end apart: 13, of which 9 were waited for; matrix products, arithmetic and copies ran while one was open for 8% of the time, Pallas kernels for 0%

profile of v11, /device:TPU:6, one launch (start us, length us, event | category | flops | bytes accessed | tf_op | source)
XLA Modules:
  0.0 114.2 jit_solution(15473985975533091571)
XLA Ops:
  1.3 1.3 %reshape.38 = bf16[64,4,4,80]{3,2,1,0:T(4,128)(2,1)S(1)} reshape(bf16[64,1280]{1,0:T(8,128)(2,1)} %param.4) | data formatting | bytes 327680 | tf_op jit(solution)/shard_map/reshape | solution.py:20
  4.8 1.1 reshape.45
  5.9 12.9 %all-to-all-start = ((bf16[4,2,20480]{2,1,0:T(2,128)(2,1)}), bf16[4,2,20480]{2,1,0:T(2,128)(2,1)S(1)}, u32[]{:S(2)}, u32[]{:S(2)}) async-start(bf16[4,2,20480]{2,1,0:T(2,128)(2,1)} %reshape.45), calls=%async_computation | async-start | bytes 655360 | tf_op jit(solution)/shard_map/all_to_all | solution.py:28
  18.8 5.0 %all-to-all-done = bf16[4,2,20480]{2,1,0:T(2,128)(2,1)S(1)} async-done(((bf16[4,2,20480]{2,1,0:T(2,128)(2,1)}), bf16[4,2,20480]{2,1,0:T(2,128)(2,1)S(1)}, u32[]{:S(2)}, u32[]{:S(2)}) %all-to-all-start) | async-done | bytes 327712 | tf_op jit(solution)/shard_map/all_to_all | solution.py:28
  24.8 1.4 %broadcast_in_dim.26 = bf16[16,3,80,256]{3,2,1,0:T(8,128)(2,1)} broadcast(bf16[3,80,256]{2,1,0:T(8,128)(2,1)S(1)} %bitcast_select_fusion), dimensions={1,2,3} | broadcast | bytes 2088960 | tf_op jit(solution)/shard_map/broadcast_in_dim | solution.py:35
  26.2 3.7 %all-to-all-start.1 = ((bf16[16,3,80,256]{3,2,1,0:T(8,128)(2,1)}), bf16[16,3,80,256]{3,2,1,0:T(8,128)(2,1)S(1)}, u32[]{:S(2)}, u32[]{:S(2)}) async-start(bf16[16,3,80,256]{3,2,1,0:T(8,128)(2,1)} %broadcast_in_dim.26), calls=%async_computation.1 | async-start | bytes 3932160 | tf_op jit(solution)/shard_map/all_to_all | solution.py:36
  30.3 10.3 %collective-permute-start = (bf16[256,320]{0,1:T(8,128)(2,1)S(1)}, bf16[256,320]{0,1:T(8,128)(2,1)S(1)}, u32[]{:S(2)}, u32[]{:S(2)}) collective-permute-start(bf16[256,320]{0,1:T(8,128)(2,1)S(1)} %copy.16), channel_id=1, source_target_pairs={{0,44},{4,0},{8,4},{12,8},{16,12},{20,16},{24,20},{28,24},{32,28},... | collective-permute-start | bytes 491528 | tf_op jit(solution)/shard_map/ppermute | solution.py:54
  40.6 1.9 %collective-permute-start.2 = (bf16[256,320]{0,1:T(8,128)(2,1)S(1)}, bf16[256,320]{0,1:T(8,128)(2,1)S(1)}, u32[]{:S(2)}, u32[]{:S(2)}) collective-permute-start(bf16[256,320]{0,1:T(8,128)(2,1)S(1)} %copy.16), channel_id=1, source_target_pairs={{0,4},{4,8},{8,12},{12,16},{16,20},{20,24},{24,28},{28,32},{32,36}... | collective-permute-start | bytes 491528 | tf_op jit(solution)/shard_map/ppermute | solution.py:51
  42.6 2.1 %collective-permute-done = bf16[256,320]{0,1:T(8,128)(2,1)S(1)} collective-permute-done((bf16[256,320]{0,1:T(8,128)(2,1)S(1)}, bf16[256,320]{0,1:T(8,128)(2,1)S(1)}, u32[]{:S(2)}, u32[]{:S(2)}) %collective-permute-start) | collective-permute-done | bytes 163872 | tf_op jit(solution)/shard_map/ppermute | solution.py:54
  44.6 5.6 %collective-permute-start.1 = (bf16[256,320]{0,1:T(8,128)(2,1)S(1)}, bf16[256,320]{0,1:T(8,128)(2,1)S(1)}, u32[]{:S(2)}, u32[]{:S(2)}) collective-permute-start(bf16[256,320]{0,1:T(8,128)(2,1)S(1)} %collective-permute-done), channel_id=1, source_target_pairs={{0,44},{4,0},{8,4},{12,8},{16,12},{20,16},{24,20},{28,24},{32,28},... | collective-permute-start | bytes 491528 | tf_op jit(solution)/shard_map/ppermute | solution.py:46
  51.3 2.1 %collective-permute-done.1 = bf16[256,320]{0,1:T(8,128)(2,1)S(1)} collective-permute-done((bf16[256,320]{0,1:T(8,128)(2,1)S(1)}, bf16[256,320]{0,1:T(8,128)(2,1)S(1)}, u32[]{:S(2)}, u32[]{:S(2)}) %collective-permute-start.1) | collective-permute-done | bytes 163872 | tf_op jit(solution)/shard_map/ppermute | solution.py:46
  53.4 1.9 %collective-permute-start.5 = (bf16[256,320]{0,1:T(8,128)(2,1)S(1)}, bf16[256,320]{0,1:T(8,128)(2,1)S(1)}, u32[]{:S(2)}, u32[]{:S(2)}) collective-permute-start(bf16[256,320]{0,1:T(8,128)(2,1)S(1)} %collective-permute-done.2), channel_id=1, source_target_pairs={{0,4},{4,8},{8,12},{12,16},{16,20},{20,24},{24,28},{28,32},{32,36}... | collective-permute-start | bytes 491528 | tf_op jit(solution)/shard_map/ppermute | solution.py:48
  55.3 5.6 %collective-permute-start.3 = (bf16[256,320]{0,1:T(8,128)(2,1)S(1)}, bf16[256,320]{0,1:T(8,128)(2,1)S(1)}, u32[]{:S(2)}, u32[]{:S(2)}) collective-permute-start(bf16[256,320]{0,1:T(8,128)(2,1)S(1)} %collective-permute-done.1), channel_id=1, source_target_pairs={{0,44},{4,0},{8,4},{12,8},{16,12},{20,16},{24,20},{28,24},{32,28},... | collective-permute-start | bytes 491528 | tf_op jit(solution)/shard_map/ppermute | solution.py:54
  62.3 1.9 %collective-permute-start.6 = (bf16[256,320]{0,1:T(8,128)(2,1)S(1)}, bf16[256,320]{0,1:T(8,128)(2,1)S(1)}, u32[]{:S(2)}, u32[]{:S(2)}) collective-permute-start(bf16[256,320]{0,1:T(8,128)(2,1)S(1)} %collective-permute-done.5), channel_id=1, source_target_pairs={{0,4},{4,8},{8,12},{12,16},{16,20},{20,24},{24,28},{28,32},{32,36}... | collective-permute-start | bytes 491528 | tf_op jit(solution)/shard_map/ppermute | solution.py:51
  64.2 5.1 %collective-permute-start.4 = (bf16[256,320]{0,1:T(8,128)(2,1)S(1)}, bf16[256,320]{0,1:T(8,128)(2,1)S(1)}, u32[]{:S(2)}, u32[]{:S(2)}) collective-permute-start(bf16[256,320]{0,1:T(8,128)(2,1)S(1)} %collective-permute-done.3), channel_id=1, source_target_pairs={{0,44},{4,0},{8,4},{12,8},{16,12},{20,16},{24,20},{28,24},{32,28},... | collective-permute-start | bytes 491528 | tf_op jit(solution)/shard_map/ppermute | solution.py:46
  70.7 1.5 %collective-permute-done.4 = bf16[256,320]{0,1:T(8,128)(2,1)S(1)} collective-permute-done((bf16[256,320]{0,1:T(8,128)(2,1)S(1)}, bf16[256,320]{0,1:T(8,128)(2,1)S(1)}, u32[]{:S(2)}, u32[]{:S(2)}) %collective-permute-start.4) | collective-permute-done | bytes 163872 | tf_op jit(solution)/shard_map/ppermute | solution.py:46
  72.1 1.9 %collective-permute-start.8 = (bf16[256,320]{0,1:T(8,128)(2,1)S(1)}, bf16[256,320]{0,1:T(8,128)(2,1)S(1)}, u32[]{:S(2)}, u32[]{:S(2)}) collective-permute-start(bf16[256,320]{0,1:T(8,128)(2,1)S(1)} %collective-permute-done.6), channel_id=1, source_target_pairs={{0,4},{4,8},{8,12},{12,16},{16,20},{20,24},{24,28},{28,32},{32,36}... | collective-permute-start | bytes 491528 | tf_op jit(solution)/shard_map/ppermute | solution.py:48
  74.7 5.6 %collective-permute-start.7 = (bf16[256,320]{0,1:T(8,128)(2,1)S(1)}, bf16[256,320]{0,1:T(8,128)(2,1)S(1)}, u32[]{:S(2)}, u32[]{:S(2)}) collective-permute-start(bf16[256,320]{0,1:T(8,128)(2,1)S(1)} %collective-permute-done.4), channel_id=1, source_target_pairs={{0,44},{4,0},{8,4},{12,8},{16,12},{20,16},{24,20},{28,24},{32,28},... | collective-permute-start | bytes 491528 | tf_op jit(solution)/shard_map/ppermute | solution.py:54
  81.0 1.9 %collective-permute-start.9 = (bf16[256,320]{0,1:T(8,128)(2,1)S(1)}, bf16[256,320]{0,1:T(8,128)(2,1)S(1)}, u32[]{:S(2)}, u32[]{:S(2)}) collective-permute-start(bf16[256,320]{0,1:T(8,128)(2,1)S(1)} %collective-permute-done.8), channel_id=1, source_target_pairs={{0,4},{4,8},{8,12},{12,16},{16,20},{20,24},{24,28},{28,32},{32,36}... | collective-permute-start | bytes 491528 | tf_op jit(solution)/shard_map/ppermute | solution.py:51
  83.6 5.8 %collective-permute-done.9 = bf16[256,320]{0,1:T(8,128)(2,1)S(1)} collective-permute-done((bf16[256,320]{0,1:T(8,128)(2,1)S(1)}, bf16[256,320]{0,1:T(8,128)(2,1)S(1)}, u32[]{:S(2)}, u32[]{:S(2)}) %collective-permute-start.9) | collective-permute-done | bytes 163872 | tf_op jit(solution)/shard_map/ppermute | solution.py:51
  89.4 1.9 %collective-permute-start.10 = (bf16[256,320]{0,1:T(8,128)(2,1)S(1)}, bf16[256,320]{0,1:T(8,128)(2,1)S(1)}, u32[]{:S(2)}, u32[]{:S(2)}) collective-permute-start(bf16[256,320]{0,1:T(8,128)(2,1)S(1)} %collective-permute-done.9), channel_id=1, source_target_pairs={{0,4},{4,8},{8,12},{12,16},{16,20},{20,24},{24,28},{28,32},{32,36}... | collective-permute-start | bytes 491528 | tf_op jit(solution)/shard_map/ppermute | solution.py:51
  92.0 5.8 %collective-permute-done.10 = bf16[256,320]{0,1:T(8,128)(2,1)S(1)} collective-permute-done((bf16[256,320]{0,1:T(8,128)(2,1)S(1)}, bf16[256,320]{0,1:T(8,128)(2,1)S(1)}, u32[]{:S(2)}, u32[]{:S(2)}) %collective-permute-start.10) | collective-permute-done | bytes 163872 | tf_op jit(solution)/shard_map/ppermute | solution.py:51
  101.9 2.5 %fusion.1 = f32[256,256,1]{1,0,2:T(8,128)S(1)} fusion(bf16[12,256,320]{1,2,0:T(8,128)(2,1)} %bitcast_dynamic-update-slice_fusion, s32[]{:T(128)S(6)} %select_n.29, bf16[12,320,256]{2,1,0:T(8,128)(2,1)S(1)} %bitcast.47), kind=kOutput, calls=%fused_computation.3 | convolution fusion | flops 504299520 | bytes 4194308 | tf_op jit(solution)/shard_map/vmc,vcn->mn/dot_general | solution.py:59
  104.5 9.1 %all_to_all.22 = f32[4,64,256]{2,1,0:T(8,128)S(1)} all-to-all(f32[4,64,256]{2,1,0:T(8,128)S(1)} %bitcast.53), channel_id=1, replica_groups=mesh['oy'=8,'oc'=2,'virt'=12,'rep'=4] {'rep'}, dimensions={0} | all-to-all | bytes 524288 | tf_op jit(solution)/shard_map/all_to_all | solution.py:61
  (39 shorter events, 16.0 us)
Async XLA Ops:
  5.9 17.8 %all-to-all-start = ((bf16[4,2,20480]{2,1,0:T(2,128)(2,1)}), bf16[4,2,20480]{2,1,0:T(2,128)(2,1)S(1)}, u32[]{:S(2)}, u32[]{:S(2)}) async-start(bf16[4,2,20480]{2,1,0:T(2,128)(2,1)} %reshape.45), calls=%async_computation | async-start | bytes 655360 | tf_op jit(solution)/shard_map/all_to_all | solution.py:28
  26.2 75.7 %all-to-all-start.1 = ((bf16[16,3,80,256]{3,2,1,0:T(8,128)(2,1)}), bf16[16,3,80,256]{3,2,1,0:T(8,128)(2,1)S(1)}, u32[]{:S(2)}, u32[]{:S(2)}) async-start(bf16[16,3,80,256]{3,2,1,0:T(8,128)(2,1)} %broadcast_in_dim.26), calls=%async_computation.1 | async-start | bytes 3932160 | tf_op jit(solution)/shard_map/all_to_all | solution.py:36
  30.3 14.3 %collective-permute-start = (bf16[256,320]{0,1:T(8,128)(2,1)S(1)}, bf16[256,320]{0,1:T(8,128)(2,1)S(1)}, u32[]{:S(2)}, u32[]{:S(2)}) collective-permute-start(bf16[256,320]{0,1:T(8,128)(2,1)S(1)} %copy.16), channel_id=1, source_target_pairs={{0,44},{4,0},{8,4},{12,8},{16,12},{20,16},{24,20},{28,24},{32,28},... | collective-permute-start | bytes 491528 | tf_op jit(solution)/shard_map/ppermute | solution.py:54
  40.6 10.7 %collective-permute-start.2 = (bf16[256,320]{0,1:T(8,128)(2,1)S(1)}, bf16[256,320]{0,1:T(8,128)(2,1)S(1)}, u32[]{:S(2)}, u32[]{:S(2)}) collective-permute-start(bf16[256,320]{0,1:T(8,128)(2,1)S(1)} %copy.16), channel_id=1, source_target_pairs={{0,4},{4,8},{8,12},{12,16},{16,20},{20,24},{24,28},{28,32},{32,36}... | collective-permute-start | bytes 491528 | tf_op jit(solution)/shard_map/ppermute | solution.py:51
  44.6 8.7 %collective-permute-start.1 = (bf16[256,320]{0,1:T(8,128)(2,1)S(1)}, bf16[256,320]{0,1:T(8,128)(2,1)S(1)}, u32[]{:S(2)}, u32[]{:S(2)}) collective-permute-start(bf16[256,320]{0,1:T(8,128)(2,1)S(1)} %collective-permute-done), channel_id=1, source_target_pairs={{0,44},{4,0},{8,4},{12,8},{16,12},{20,16},{24,20},{28,24},{32,28},... | collective-permute-start | bytes 491528 | tf_op jit(solution)/shard_map/ppermute | solution.py:46
  53.4 8.9 %collective-permute-start.5 = (bf16[256,320]{0,1:T(8,128)(2,1)S(1)}, bf16[256,320]{0,1:T(8,128)(2,1)S(1)}, u32[]{:S(2)}, u32[]{:S(2)}) collective-permute-start(bf16[256,320]{0,1:T(8,128)(2,1)S(1)} %collective-permute-done.2), channel_id=1, source_target_pairs={{0,4},{4,8},{8,12},{12,16},{16,20},{20,24},{24,28},{28,32},{32,36}... | collective-permute-start | bytes 491528 | tf_op jit(solution)/shard_map/ppermute | solution.py:48
  55.3 8.9 %collective-permute-start.3 = (bf16[256,320]{0,1:T(8,128)(2,1)S(1)}, bf16[256,320]{0,1:T(8,128)(2,1)S(1)}, u32[]{:S(2)}, u32[]{:S(2)}) collective-permute-start(bf16[256,320]{0,1:T(8,128)(2,1)S(1)} %collective-permute-done.1), channel_id=1, source_target_pairs={{0,44},{4,0},{8,4},{12,8},{16,12},{20,16},{24,20},{28,24},{32,28},... | collective-permute-start | bytes 491528 | tf_op jit(solution)/shard_map/ppermute | solution.py:54
  62.3 8.4 %collective-permute-start.6 = (bf16[256,320]{0,1:T(8,128)(2,1)S(1)}, bf16[256,320]{0,1:T(8,128)(2,1)S(1)}, u32[]{:S(2)}, u32[]{:S(2)}) collective-permute-start(bf16[256,320]{0,1:T(8,128)(2,1)S(1)} %collective-permute-done.5), channel_id=1, source_target_pairs={{0,4},{4,8},{8,12},{12,16},{16,20},{20,24},{24,28},{28,32},{32,36}... | collective-permute-start | bytes 491528 | tf_op jit(solution)/shard_map/ppermute | solution.py:51
  64.2 8.0 %collective-permute-start.4 = (bf16[256,320]{0,1:T(8,128)(2,1)S(1)}, bf16[256,320]{0,1:T(8,128)(2,1)S(1)}, u32[]{:S(2)}, u32[]{:S(2)}) collective-permute-start(bf16[256,320]{0,1:T(8,128)(2,1)S(1)} %collective-permute-done.3), channel_id=1, source_target_pairs={{0,44},{4,0},{8,4},{12,8},{16,12},{20,16},{24,20},{28,24},{32,28},... | collective-permute-start | bytes 491528 | tf_op jit(solution)/shard_map/ppermute | solution.py:46
  72.1 8.9 %collective-permute-start.8 = (bf16[256,320]{0,1:T(8,128)(2,1)S(1)}, bf16[256,320]{0,1:T(8,128)(2,1)S(1)}, u32[]{:S(2)}, u32[]{:S(2)}) collective-permute-start(bf16[256,320]{0,1:T(8,128)(2,1)S(1)} %collective-permute-done.6), channel_id=1, source_target_pairs={{0,4},{4,8},{8,12},{12,16},{16,20},{20,24},{24,28},{28,32},{32,36}... | collective-permute-start | bytes 491528 | tf_op jit(solution)/shard_map/ppermute | solution.py:48
  74.7 16.6 %collective-permute-start.7 = (bf16[256,320]{0,1:T(8,128)(2,1)S(1)}, bf16[256,320]{0,1:T(8,128)(2,1)S(1)}, u32[]{:S(2)}, u32[]{:S(2)}) collective-permute-start(bf16[256,320]{0,1:T(8,128)(2,1)S(1)} %collective-permute-done.4), channel_id=1, source_target_pairs={{0,44},{4,0},{8,4},{12,8},{16,12},{20,16},{24,20},{28,24},{32,28},... | collective-permute-start | bytes 491528 | tf_op jit(solution)/shard_map/ppermute | solution.py:54
  81.0 8.4 %collective-permute-start.9 = (bf16[256,320]{0,1:T(8,128)(2,1)S(1)}, bf16[256,320]{0,1:T(8,128)(2,1)S(1)}, u32[]{:S(2)}, u32[]{:S(2)}) collective-permute-start(bf16[256,320]{0,1:T(8,128)(2,1)S(1)} %collective-permute-done.8), channel_id=1, source_target_pairs={{0,4},{4,8},{8,12},{12,16},{16,20},{20,24},{24,28},{28,32},{32,36}... | collective-permute-start | bytes 491528 | tf_op jit(solution)/shard_map/ppermute | solution.py:51
  89.4 8.4 %collective-permute-start.10 = (bf16[256,320]{0,1:T(8,128)(2,1)S(1)}, bf16[256,320]{0,1:T(8,128)(2,1)S(1)}, u32[]{:S(2)}, u32[]{:S(2)}) collective-permute-start(bf16[256,320]{0,1:T(8,128)(2,1)S(1)} %collective-permute-done.9), channel_id=1, source_target_pairs={{0,4},{4,8},{8,12},{12,16},{16,20},{20,24},{24,28},{28,32},{32,36}... | collective-permute-start | bytes 491528 | tf_op jit(solution)/shard_map/ppermute | solution.py:51
